TPU v7x, 256 devices: a whole 4x4x8 slice. The times are simulated.
256 devices in a mesh: seq: 32 (over z, x), tp: 8 (over y, core).
Axes of the slice: x: 4, y: 4, z: 8, core: 2. Of those that a mesh axis runs over, the one named last changes fastest.
Arguments:
- inputs: bfloat16 [4096, 8192], P('seq', 'tp'), may hold values from -6 to 6
- input_proj: bfloat16 [4096, 2048], P('seq', 'tp'), may hold values from -0.59765625 to 0.59765625
- readout: bfloat16 [4096, 2048], P('seq', 'tp'), may hold values from -0.59765625 to 0.59765625
- step_size: float32 [4096, 128], P('seq', 'tp'), may hold values from 0.001 to 0.1
- decay_rate: float32 [128], P('tp'), may hold values from 0.002 to 4
- out_grad: bfloat16 [4096, 8192], P('seq', 'tp'), may hold values from -6 to 6
Outputs:
- grad_inputs: bfloat16 [4096, 8192], P('seq', 'tp')
- grad_proj: bfloat16 [4096, 2048], P('seq', 'tp')
- grad_read: bfloat16 [4096, 2048], P('seq', 'tp')
- grad_step: float32 [4096, 128], P(('seq', 'tp'))
All inputs are finite; a program needn't handle non-finite values.
Results may differ from a plain program's by a relative error of at most 0.001.
Values sent between devices are 32-bit elements; how exact they have to be, the bound alone decides.
No kernel may reach another device: no remote copies, remote signals or barrier semaphores. Data moves between devices by JAX's collectives and lax.ppermute only.
A program may use at most 192 MiB of HBM per device.

v0:
```python
import jax
import jax.numpy as jnp
from jax import lax
from jax.sharding import PartitionSpec as P

HEAD_DIM = 64
D_STATE = 256
SPAN = 128


precise = lax.Precision.HIGHEST


def prefix(part, axis, combine, identity, reverse):
    count = lax.axis_size(axis)
    place = lax.axis_index(axis)
    ahead = count - 1 - place if reverse else place
    gathered = jax.tree.map(lambda a: lax.all_gather(a, axis), part)
    state = jax.tree.map(lambda a, e: jnp.zeros_like(a) + jnp.asarray(e, a.dtype), part, identity)

    def one(turn, state):
        source = count - 1 - turn if reverse else turn
        return combine(
            state, jax.tree.map(lambda a: lax.dynamic_index_in_dim(a, source, 0, False), gathered)
        )

    return lax.fori_loop(0, ahead, one, state)


def summarize(inputs, out_grad, input_proj, readout, step_size, decay_rate):
    cumulative = jnp.cumsum(-decay_rate[None] * step_size, axis=0)
    totals = cumulative[-1]
    to_end = jnp.exp(totals[None] - cumulative) * step_size
    forward = jnp.einsum(
        "qghp,qgn->ghnp",
        inputs.astype(jnp.float32) * to_end[..., None],
        input_proj.astype(jnp.float32),
        precision=precise,
    )
    from_start = jnp.exp(cumulative)
    backward = jnp.einsum(
        "qghp,qgn->ghnp",
        out_grad.astype(jnp.float32) * from_start[..., None],
        readout.astype(jnp.float32),
        precision=precise,
    )
    return (totals, forward, backward)


def span_backward(
    inputs_raw, out_raw, proj_raw, read_raw, step_size, decay_rate, state_in, grad_in
):
    inputs = inputs_raw.astype(jnp.float32)
    out_grad = out_raw.astype(jnp.float32)
    input_proj = proj_raw.astype(jnp.float32)
    readout = read_raw.astype(jnp.float32)
    length = inputs.shape[0]
    position = jnp.arange(length)
    causal = (position[:, None] >= position[None, :]).astype(jnp.float32)
    strictly = (position[:, None] < position[None, :]).astype(jnp.float32)
    cumulative = jnp.cumsum(-decay_rate[None] * step_size, axis=0)
    totals = cumulative[-1]
    spread = cumulative[:, None] - cumulative[None, :]
    decays = jnp.exp(jnp.minimum(spread, 0.0)) * causal[:, :, None, None]
    to_end = jnp.exp(totals[None] - cumulative)
    from_start = jnp.exp(cumulative)
    state_match = jnp.einsum("ugn,sgn->usg", read_raw, proj_raw, preferred_element_type=jnp.float32)
    grad_match = jnp.einsum(
        "ughp,sghp->usgh", out_raw, inputs_raw, preferred_element_type=jnp.float32
    )
    mix_input = decays * state_match[..., None]
    back_b = jnp.einsum("ghnp,sgn->sghp", grad_in, input_proj, precision=precise)
    vector = (
        jnp.einsum("usgh,ughp->sghp", mix_input, out_grad, precision=precise)
        + to_end[..., None] * back_b
    )
    grad_inputs = step_size[..., None] * vector
    direct = jnp.sum(inputs * vector, axis=-1)
    mix_state = decays * grad_match * step_size[None]
    back_x = jnp.einsum("ghnp,sghp->sghn", grad_in, inputs, precision=precise)
    grad_proj = jnp.einsum("usgh,ugn->sgn", mix_state, readout, precision=precise) + jnp.einsum(
        "sgh,sghn->sgn", step_size * to_end, back_x, precision=precise
    )
    state_out = jnp.einsum("ghnp,ughp->ughn", state_in, out_grad, precision=precise)
    grad_read = jnp.einsum("usgh,sgn->ugn", mix_state, input_proj, precision=precise) + jnp.einsum(
        "ugh,ughn->ugn", from_start, state_out, precision=precise
    )
    weights = mix_state * state_match[..., None]
    exclusive = jnp.cumsum(weights, axis=1) - weights
    paired = jnp.sum(exclusive * causal[:, :, None, None], axis=0)
    from_init = from_start * jnp.einsum("ugn,ughn->ugh", readout, state_out, precision=precise)
    suffixes = jnp.einsum("ut,ugh->tgh", causal, from_init, precision=precise)
    from_tail = to_end * step_size * jnp.sum(inputs * back_b, axis=-1)
    prefixes = jnp.einsum("st,sgh->tgh", strictly, from_tail, precision=precise)
    constant = jnp.exp(totals) * jnp.sum(grad_in * state_in, axis=(2, 3))
    grad_log = paired + suffixes + prefixes + constant[None]
    grad_step = direct - decay_rate[None] * grad_log
    return (grad_inputs, grad_proj, grad_read, grad_step)


def combine(earlier, later):
    return (earlier[0] + later[0], jnp.exp(later[0])[..., None, None] * earlier[1] + later[1])


def span_prefix(log_sums, states, reverse):
    initial = (jnp.zeros_like(log_sums[0]), jnp.zeros_like(states[0]))

    def advance(carried, element):
        return (combine(carried, element), carried)

    return lax.scan(advance, initial, (log_sums, states), reverse=reverse)


def to_spans(
    inputs, out_grad, input_proj, readout, step_size, group_count, state_dim, head_dim, span_len
):
    span_count = inputs.shape[0] // span_len
    head_count = step_size.shape[1] // group_count
    return (
        inputs.reshape(span_count, span_len, group_count, head_count, head_dim),
        out_grad.reshape(span_count, span_len, group_count, head_count, head_dim),
        input_proj.reshape(span_count, span_len, group_count, state_dim),
        readout.reshape(span_count, span_len, group_count, state_dim),
        step_size.reshape(span_count, span_len, group_count, head_count),
    )


def summaries(blocks, rate_rows):

    def summarize_one(element):
        return summarize(element[0], element[1], element[2], element[3], element[4], rate_rows)

    return lax.map(summarize_one, blocks)


def apply_backward(blocks, rate_rows, state_ins, grad_ins):

    def backward_one(element):
        return span_backward(
            element[0],
            element[1],
            element[2],
            element[3],
            element[4],
            rate_rows,
            element[5],
            element[6],
        )

    gradients = lax.map(backward_one, blocks + (state_ins, grad_ins))
    tokens = gradients[0].shape[0] * gradients[0].shape[1]
    return tuple((item_grad.reshape(tokens, -1) for item_grad in gradients))


def body(inputs, input_proj, readout, step_size, decay_rate, out_grad):
    group_count = input_proj.shape[1] // D_STATE
    blocks = to_spans(
        inputs, out_grad, input_proj, readout, step_size, group_count, D_STATE, HEAD_DIM, SPAN
    )
    rate_rows = decay_rate.reshape(group_count, -1)
    totals, forward, backward = summaries(blocks, rate_rows)
    (device_log, device_fwd), (log_before, fwd_before) = span_prefix(totals, forward, False)
    (ignored_log, device_bwd), (log_after, bwd_after) = span_prefix(totals, backward, True)
    identity = (jnp.zeros_like(device_log), jnp.zeros_like(device_fwd))
    ignored_in, device_in = prefix((device_log, device_fwd), "seq", combine, identity, False)
    ignored_out, device_out = prefix((device_log, device_bwd), "seq", combine, identity, True)
    state_ins = fwd_before + jnp.exp(log_before)[..., None, None] * device_in[None]
    grad_ins = bwd_after + jnp.exp(log_after)[..., None, None] * device_out[None]
    grad_inputs, grad_proj, grad_read, grad_step = apply_backward(
        blocks, rate_rows, state_ins, grad_ins
    )
    regrouped = lax.all_to_all(grad_step, "tp", split_axis=0, concat_axis=1, tiled=True)
    return (
        grad_inputs.astype(jnp.bfloat16),
        grad_proj.astype(jnp.bfloat16),
        grad_read.astype(jnp.bfloat16),
        regrouped,
    )


def solution(mesh):
    in_specs = (
        P("seq", "tp"),
        P("seq", "tp"),
        P("seq", "tp"),
        P("seq", "tp"),
        P("tp"),
        P("seq", "tp"),
    )
    out_specs = (P("seq", "tp"), P("seq", "tp"), P("seq", "tp"), P(("seq", "tp"), None))
    return jax.shard_map(body, mesh=mesh, in_specs=in_specs, out_specs=out_specs, check_vma=False)
```

profile of v0, /device:TPU:1, one launch (start us, length us, event | category | flops | bytes accessed | tf_op | source)
XLA Modules:
  0.0 695.1 jit_solution(4769641890477793412)
XLA Ops:
  19.4 23.3 %fusion.50 = f32[128,128,1,16]{0,3,1,2:T(8,128)S(1)} fusion(f32[128,128,1,16]{0,3,1,2:T(8,128)S(1)} %copy.98), kind=kOutput, calls=%fused_computation.81 | output fusion | flops 33292288 | bytes 2097152 | tf_op jit(solution)/shard_map/while/body/eval_jaxpr/jit(cumsum)/reduce_window_sum | solution.py:89
  43.1 40.7 %all_gather.18 = f32[32,1,16]{2,1,0:T(1,128)} all-gather(f32[1,1,16]{2,1,0:T(1,128)} %get-tuple-element.328), channel_id=1, replica_groups=mesh['seq'=32,'tp'=8] {'seq'}, dimensions={0}, use_global_device_ids=true | all-gather | bytes 2112 | tf_op jit(solution)/shard_map/all_gather | solution.py:18
  85.3 165.7 %all-gather.7.cloned.1.call-done = f32[32,16,256,64]{2,3,1,0:T(8,128)} async-done(((f32[1,16,256,64]{2,3,1,0:T(8,128)}), f32[32,16,256,64]{2,3,1,0:T(8,128)}) %all-gather.7.cloned.1.call-update) | async-done | bytes 33554448 | tf_op jit(solution)/shard_map/all_gather | solution.py:18
  252.6 4.8 fusion.2
  257.3 226.3 %all-gather.5.cloned.1.call-done = f32[32,16,256,64]{2,3,1,0:T(8,128)} async-done(((f32[1,16,256,64]{2,3,1,0:T(8,128)}), f32[32,16,256,64]{2,3,1,0:T(8,128)}) %all-gather.5.cloned.1.call-update) | async-done | bytes 33554448 | tf_op jit(solution)/shard_map/all_gather | solution.py:18
  485.2 181.7 %while.16 = (s32[]{:T(128)}, f32[1,16,256,64]{3,2,1,0:T(8,128)}, s32[]{:T(128)}, f32[32,1,16]{2,1,0:T(1,128)}, f32[32,1,16,256,64]{3,4,2,0,1:T(8,128)}, /*index=5*/s32[]{:T(128)}, s32[]{:T(128)}, s32[]{:T(128)}, s32[]{:T(128)}) while((s32[]{:T(128)}, f32[1,16,256,64]{3,2,1,0:T(8,128)}, s32[]{:T(128)}, f32[32,1,16]{2,1,0:T(1,128)}, ...), condition=%wide.region_2.3_spmd, body=%wide.region_1.2_spmd.sunk | while | flops 524294 | bytes 7340371 | solution.py:27
  487.9 3.3 bitcast_add_fusion.4
  493.7 3.3 bitcast_add_fusion.4
  499.6 3.3 bitcast_add_fusion.4
  511.3 3.3 bitcast_add_fusion.4
  517.2 3.3 bitcast_add_fusion.4
  523.1 3.3 bitcast_add_fusion.4
  534.8 3.3 bitcast_add_fusion.4
  546.6 3.3 bitcast_add_fusion.4
  552.4 3.3 bitcast_add_fusion.4
  558.3 3.3 bitcast_add_fusion.4
  564.2 3.3 bitcast_add_fusion.4
  570.0 3.3 bitcast_add_fusion.4
  581.7 3.3 bitcast_add_fusion.4
  587.6 3.3 bitcast_add_fusion.4
  599.3 3.3 bitcast_add_fusion.4
  605.1 3.3 bitcast_add_fusion.4
  611.0 3.3 bitcast_add_fusion.4
  676.0 5.7 all-to-all-start
  (198 shorter events, 157.9 us)
Async XLA Ops:
  7.2 6.2 copy-start
  7.2 243.9 %all-gather.7.cloned.1.call-start = ((), (), s32[]{:S(2)}) async-start(), calls=%async_computation.2 | async-start | bytes 34603008 | tf_op jit(solution)/shard_map/all_gather | solution.py:18
  8.9 0.7 copy-start.11
  8.9 8.7 %copy-start.12 = (f32[128,1,16]{0,2,1:T(8,128)}, f32[128,1,16]{0,2,1:T(8,128)S(1)}, u32[]{:S(2)}) copy-start(f32[128,1,16]{0,2,1:T(8,128)S(1)} %copy.86) | copy-start | bytes 24580
  11.8 5.8 copy-start.3
  13.2 1.7 copy-start.5
  14.9 2.8 copy-start.17
  14.9 468.7 %all-gather.5.cloned.1.call-start = ((), (), s32[]{:S(2)}) async-start(), calls=%async_computation.1 | async-start | bytes 34603008 | tf_op jit(solution)/shard_map/all_gather | solution.py:18
  17.6 1.3 copy-start.14
  17.6 1.2 copy-start.9
  667.0 2.9 copy-start.1
  669.8 3.8 copy-start.2
  669.8 3.8 copy-start.6
  671.7 2.2 copy-start.13
  671.7 2.2 copy-start.16
  671.7 2.3 copy-start.4
  671.7 2.3 copy-start.10
  671.7 2.3 copy-start.15
  671.7 2.3 copy-start.18
  671.7 2.3 copy-start.19
  673.7 1.4 copy-start.20
  673.8 7.9 %copy-start.7 = (f32[128,256]{0,1:T(8,128)S(1)}, f32[128,256]{0,1:T(8,128)}, u32[]{:S(2)}) copy-start(f32[128,256]{0,1:T(8,128)} %get-tuple-element.331) | copy-start | bytes 393220
  673.9 8.0 %copy-start.8 = (f32[128,128]{1,0:T(8,128)S(1)}, f32[128,128]{1,0:T(8,128)}, u32[]{:S(2)}) copy-start(f32[128,128]{1,0:T(8,128)} %get-tuple-element.324) | copy-start | bytes 196612
  676.0 10.3 %all-to-all-start = ((f32[8,1,256]{2,1,0:T(1,128)}), f32[8,1,256]{2,1,0:T(1,128)S(1)}, u32[]{:S(2)}, u32[]{:S(2)}) async-start(f32[8,1,256]{2,1,0:T(1,128)} %reshape.355), calls=%async_computation | async-start | bytes 16384 | tf_op jit(solution)/shard_map/all_to_all | solution.py:172
Sparse Core Ops, SparseCore 0:
  15.0 235.9 all-gather.6
  253.6 229.9 all-gather.4
where the time goes:
time: 698 us; the launch traced here: 695 us
  waiting for transfers between devices  394 us (56%)
  other arithmetic  134 us (19%)
  local copies, waits for them, and re-layouts  90.8 us (13%)
  blocking collectives  40.7 us (6%)
  matrix products  15.1 us (2%)
  between operations  14.4 us (2%)
    all_gather x2, waiting for transfers between devices, prefix(): gathered = jax.tree.map(lambda a: lax.all_gather(a, axis), part)  392 us
    add x31, other arithmetic, combine(): jnp.exp(later[0])[..., None, None] * earlier[1] + later[1]  102 us
    dynamic_slice x62, local copies, waits for them, and re-layouts, one(): lax.dynamic_index_in_dim(a, source, 0, False)  59.4 us
    all_gather x1, blocking collectives, prefix(): gathered = jax.tree.map(lambda a: lax.all_gather(a, axis), part)  40.7 us
    another operation x1, other arithmetic, span_backward(): exclusive = jnp.cumsum(weights, axis=1) - weights  23.3 us
    exp x31, local copies, waits for them, and re-layouts, combine(): jnp.exp(later[0])[..., None, None] * earlier[1] + later[1]  20 us
  transfers between devices with their start and end apart: 3, of which 3 were waited for; matrix products, arithmetic and copies ran while one was open for 6% of the time, Pallas kernels for 0%

commit v1 on v0

--- a/solution.py
+++ b/solution.py
@@ -25,6 +25,39 @@
         )
 
     return lax.fori_loop(0, ahead, one, state)
+
+
+def seq_scan(device_log, device_fwd, device_bwd, axis):
+    count = lax.axis_size(axis)
+    place = lax.axis_index(axis)
+    logs = lax.all_gather(device_log, axis).reshape(count, -1)
+    heads = logs.shape[1]
+    stacked = jnp.stack([device_fwd, device_bwd])
+    shape = stacked.shape
+    combos = 2 * heads
+    flat = stacked.reshape(count, -1)
+    pieces = lax.all_to_all(flat, axis, 0, 0, tiled=True)
+    if combos % count == 0:
+        per = combos // count
+        held = place * per + jnp.arange(per)
+    else:
+        per = 1
+        held = (place // (count // combos))[None]
+    pieces = pieces.reshape(count, per, -1)
+    chosen = jnp.take(logs, held % heads, axis=1)
+    position = jnp.arange(count)
+    low = jnp.minimum(position[:, None], position[None, :])
+    high = jnp.maximum(position[:, None], position[None, :])
+    between = ((position[None, None, :] > low[..., None]) & (position[None, None, :] < high[..., None]))
+    exponent = jnp.einsum("ijm,mc->cij", between.astype(jnp.float32), chosen, precision=precise)
+    before = (position[None, :] < position[:, None])
+    after = (position[None, :] > position[:, None])
+    mask = jnp.where((held < heads)[:, None, None], before[None], after[None])
+    weights = jnp.where(mask, jnp.exp(exponent), 0.0)
+    scanned = jnp.einsum("cij,jcx->icx", weights, pieces, precision=precise)
+    back = lax.all_to_all(scanned.reshape(count, -1), axis, 0, 0, tiled=True)
+    back = back.reshape(shape)
+    return back[0], back[1]
 
 
 def summarize(inputs, out_grad, input_proj, readout, step_size, decay_rate):
@@ -161,9 +194,7 @@
     totals, forward, backward = summaries(blocks, rate_rows)
     (device_log, device_fwd), (log_before, fwd_before) = span_prefix(totals, forward, False)
     (ignored_log, device_bwd), (log_after, bwd_after) = span_prefix(totals, backward, True)
-    identity = (jnp.zeros_like(device_log), jnp.zeros_like(device_fwd))
-    ignored_in, device_in = prefix((device_log, device_fwd), "seq", combine, identity, False)
-    ignored_out, device_out = prefix((device_log, device_bwd), "seq", combine, identity, True)
+    device_in, device_out = seq_scan(device_log, device_fwd, device_bwd, "seq")
     state_ins = fwd_before + jnp.exp(log_before)[..., None, None] * device_in[None]
     grad_ins = bwd_after + jnp.exp(log_after)[..., None, None] * device_out[None]
     grad_inputs, grad_proj, grad_read, grad_step = apply_backward(

time: 698 us -> 203 us (0.29)
  waiting for transfers between devices: 394 us -> 28.5 us
  other arithmetic: 134 us -> 18.8 us
  local copies, waits for them, and re-layouts: 90.8 us -> 29.7 us
  blocking collectives: 40.7 us -> 72 us
  starting transfers between devices: 5.76 us -> 32.6 us
  between operations: 14.4 us -> 1 us
    all_gather x2 -> x0, waiting for transfers between devices: 392 us -> none  [prefix(): gathered = jax.tree.map(lambda a: lax.all_gather(a, axis), part)]
    add x31 -> x0, other arithmetic: 102 us -> none  [combine(): jnp.exp(later[0])[..., None, None] * earlier[1] + later[1]]
    dynamic_slice x62 -> x0, local copies, waits for them, and re-layouts: 59.4 us -> none  [one(): lax.dynamic_index_in_dim(a, source, 0, False)]
    all_gather x1, blocking collectives: 40.7 us -> 72 us  [seq_scan(): logs = lax.all_gather(device_log, axis).reshape(count, -1)]
    all_to_all x0 -> x2, waiting for transfers between devices: none -> 26.5 us  [the longest x1 26.5 us: seq_scan(): back = lax.all_to_all(scanned.reshape(count, -1), axis, 0, 0, tiled=True)]
    another operation x1, other arithmetic: 23.3 us -> 2.34 us  [span_backward(): exclusive = jnp.cumsum(weights, axis=1) - weights]
    exp x31 -> x0, local copies, waits for them, and re-layouts: 20 us -> none  [combine(): jnp.exp(later[0])[..., None, None] * earlier[1] + later[1]]
    all_to_all x0 -> x2, starting transfers between devices: none -> 16.3 us  [the longest x1 12 us: seq_scan(): pieces = lax.all_to_all(flat, axis, 0, 0, tiled=True)]
  transfers between devices with their start and end apart: 3 -> 3, of which waited for: 3 -> 2; matrix products, arithmetic and copies ran while one was open for 6% -> 8% of each run, Pallas kernels for 0% -> 0%
where the time goes in v1:
time: 203 us; the launch traced here: 202 us
  blocking collectives  72 us (35%)
  starting transfers between devices  32.6 us (16%)
  local copies, waits for them, and re-layouts  29.7 us (15%)
  waiting for transfers between devices  28.5 us (14%)
  matrix products  19.6 us (10%)
  other arithmetic  18.8 us (9%)
    all_gather x1, blocking collectives, seq_scan(): logs = lax.all_gather(device_log, axis).reshape(count, -1)  72 us
    all_to_all x1, waiting for transfers between devices, seq_scan(): back = lax.all_to_all(scanned.reshape(count, -1), axis, 0, 0, tiled=True)  26.5 us
    all_to_all x1, starting transfers between devices, body(): lax.all_to_all(grad_step, 'tp', split_axis=0, concat_axis=1, tiled=True)  16.3 us
    all_to_all x1, starting transfers between devices, seq_scan(): pieces = lax.all_to_all(flat, axis, 0, 0, tiled=True)  12 us
    reduce_sum x1, other arithmetic, span_backward(): constant = jnp.exp(totals) * jnp.sum(grad_in * state_in, axis=(2, 3))  9.25 us
    unnamed x43, local copies, waits for them, and re-layouts  6.02 us
    all_to_all x1, local copies, waits for them, and re-layouts, seq_scan(): pieces = lax.all_to_all(flat, axis, 0, 0, tiled=True)  5.46 us
    all_to_all x1, starting transfers between devices, seq_scan(): back = lax.all_to_all(scanned.reshape(count, -1), axis, 0, 0, tiled=True)  4.27 us
  transfers between devices with their start and end apart: 3, of which 2 were waited for; matrix products, arithmetic and copies ran while one was open for 8% of the time, Pallas kernels for 0%

profile of v1, /device:TPU:1, one launch (start us, length us, event | category | flops | bytes accessed | tf_op | source)
XLA Modules:
  0.0 202.3 jit_solution(7571295561463057084)
XLA Ops:
  5.3 1.4 fusion.53
  8.1 2.7 %copy.89 = f32[2,1,16,256,64]{4,3,2,0,1:T(8,128)} copy(f32[2,1,16,256,64]{3,4,2,1,0:T(8,128)S(1)} %pad_maximum_fusion) | data formatting | bytes 4194304 | tf_op jit(solution)/shard_map/stack | solution.py:35
  10.8 5.5 %all_to_all.31 = f32[32,1,16384]{2,1,0:T(1,128)} reshape(f32[2,1,16,256,64]{4,3,2,0,1:T(8,128)} %copy.89) | data formatting | bytes 4194304 | tf_op jit(solution)/shard_map/all_to_all | solution.py:39
  16.3 12.0 %all-to-all-start = ((f32[32,1,16384]{2,1,0:T(1,128)}), f32[32,1,16384]{2,1,0:T(1,128)S(1)}, u32[]{:S(2)}, u32[]{:S(2)}) async-start(f32[32,1,16384]{2,1,0:T(1,128)} %all_to_all.31), calls=%async_computation | async-start | bytes 4194304 | tf_op jit(solution)/shard_map/all_to_all | solution.py:39
  28.3 72.0 %all_gather.4 = f32[32,1,16]{2,1,0:T(1,128)S(1)} all-gather(f32[1,1,16]{2,1,0:T(1,128)S(1)} %copy-done.16), channel_id=1, replica_groups=mesh['seq'=32,'tp'=8] {'seq'}, dimensions={0}, use_global_device_ids=true | all-gather | bytes 2112 | tf_op jit(solution)/shard_map/all_gather | solution.py:33
  102.0 3.2 %convolution_bitcast_fusion = f32[32,1,16384]{2,0,1:T(8,128)S(1)} fusion(f32[32,1,16384]{2,1,0:T(1,128)S(1)} %all-to-all-done, f32[32,32]{1,0:T(8,128)S(1)} %bitcast.207, pred[]{:T(512)} %bitcast.26), kind=kOutput, calls=%fused_computation | convolution fusion | flops 201330688 | bytes 4198401 | tf_op jit(solution)/shard_map/cij,jcx->icx/dot_general | solution.py:57
  105.2 3.5 %copy.91 = f32[32,1,16384]{2,1,0:T(1,128)} copy(f32[32,1,16384]{2,0,1:T(8,128)S(1)} %convolution_bitcast_fusion) | data formatting | bytes 4194304 | tf_op jit(solution)/shard_map/cij,jcx->icx/transpose | solution.py:57
  108.7 4.3 %all-to-all-start.1 = ((f32[32,1,16384]{2,1,0:T(1,128)}), f32[32,1,16384]{2,1,0:T(1,128)S(1)}, u32[]{:S(2)}, u32[]{:S(2)}) async-start(f32[32,1,16384]{2,1,0:T(1,128)} %copy.91), calls=%async_computation.1 | async-start | bytes 4194304 | tf_op jit(solution)/shard_map/all_to_all | solution.py:58
  115.3 2.2 %broadcast_multiply_fusion = (f32[128,128,1,16]{1,0,3,2:T(8,128)S(1)}, f32[128,128]{1,0:T(8,128)}) fusion(f32[128,128]{1,0:T(8,128)} %copy.85, f32[128,16]{0,1:T(8,128)} %param.9, bf16[128,16,64]{0,2,1:T(8,128)(2,1)S(1)} %bitcast.194, bf16[128,16,64]{0,2,1:T(8,128)(2,1)} %bitcast.197, f32[128,128]{1,0:T(8,128)S(1)} %fusion.39, f32[128,16]{0,1:T(8,128)} %bitcast.205), kind=kOutput, calls=%fused_computation.50 | convolution fusion | flops 35373056 | bytes 1785856 | tf_op jit(solution)/shard_map/while/body/eval_jaxpr/ughp,sghp->usgh/dot_general | solution.py:101
  117.5 1.4 copy.97
  118.9 2.3 %fusion.56 = f32[128,128,1,16]{0,3,1,2:T(8,128)} fusion(f32[128,128,1,16]{0,3,1,2:T(8,128)} %copy.97), kind=kOutput, calls=%fused_computation.95 | output fusion | flops 33292288 | bytes 2097152 | tf_op jit(solution)/shard_map/while/body/eval_jaxpr/jit(cumsum)/reduce_window_sum | solution.py:122
  121.2 2.6 %copy.98 = f32[128,128,1,16]{1,0,3,2:T(8,128)} copy(f32[128,128,1,16]{0,3,1,2:T(8,128)} %fusion.56) | data formatting | bytes 2097152 | tf_op jit(solution)/shard_map/while/body/eval_jaxpr/jit(cumsum)/reduce_window_sum | solution.py:122
  123.8 1.9 multiply_reduce_fusion.1
  125.7 26.5 %all-to-all-done.1 = f32[32,1,16384]{2,1,0:T(1,128)S(1)} async-done(((f32[32,1,16384]{2,1,0:T(1,128)}), f32[32,1,16384]{2,1,0:T(1,128)S(1)}, u32[]{:S(2)}, u32[]{:S(2)}) %all-to-all-start.1) | async-done | bytes 2097184 | tf_op jit(solution)/shard_map/all_to_all | solution.py:58
  152.2 9.3 %multiply_reduce_fusion = (f32[16]{0:T(128)}, f32[16,16384]{1,0:T(8,128)S(1)}, f32[16,16384]{1,0:T(8,128)}) fusion(f32[32,1,16384]{2,1,0:T(1,128)S(1)} %all-to-all-done.1), kind=kLoop, calls=%fused_computation.36 | loop fusion | flops 524272 | bytes 4194368 | tf_op jit(solution)/shard_map/while/body/eval_jaxpr/reduce_sum | solution.py:128
  161.5 2.1 %mul.297 = f32[16,256,64]{2,1,0:T(8,128)S(1)} reshape(f32[16,16384]{1,0:T(8,128)} %get-tuple-element.131) | data formatting | bytes 2097152 | tf_op jit(solution)/shard_map/mul | solution.py:199
  163.6 3.2 %multiply_reduce_fusion.2 = (f32[128,16]{0,1:T(8,128)}, f32[128,16,64]{0,2,1:T(8,128)}) fusion(bf16[128,1024]{0,1:T(8,128)(2,1)S(1)} %copy.87, f32[16,256,64]{2,1,0:T(8,128)S(1)} %mul.297, bf16[128,256]{1,0:T(8,128)(2,1)S(1)} %copy-done), kind=kOutput, calls=%fused_computation.49 | convolution fusion | flops 403044352 | bytes 1908736 | tf_op jit(solution)/shard_map/while/body/eval_jaxpr/ghnp,sgn->sghp/dot_general | solution.py:105
  166.7 1.9 fusion.2
  168.6 1.6 copy.109
  170.2 2.2 %slice.21 = f32[16,256,64]{2,1,0:T(8,128)} reshape(f32[16,16384]{1,0:T(8,128)S(1)} %get-tuple-element.130) | data formatting | bytes 2097152 | tf_op jit(solution)/shard_map/slice | solution.py:60
  172.4 2.8 %fusion.4 = (f32[128,256]{0,1:T(8,128)S(1)}, f32[16,256,128]{2,1,0:T(8,128)S(1)}) fusion(f32[128,16]{0,1:T(8,128)S(1)} %get-tuple-element.153, f32[16,256,64]{2,1,0:T(8,128)} %slice.21, bf16[128,16,64]{0,2,1:T(8,128)(2,1)} %bitcast.198), kind=kOutput, calls=%fused_computation.9 | convolution fusion | flops 403668992 | bytes 3547136 | tf_op jit(solution)/shard_map/while/body/eval_jaxpr/ghnp,ughp->ughn/dot_general | solution.py:117
  176.6 1.8 multiply_reduce_fusion.3
  179.4 16.3 %all-to-all-start.2 = ((f32[8,1,256]{2,1,0:T(1,128)}), f32[8,1,256]{2,1,0:T(1,128)S(1)}, u32[]{:S(2)}, u32[]{:S(2)}) async-start(f32[8,1,256]{2,1,0:T(1,128)} %reshape.448), calls=%async_computation.2 | async-start | bytes 16384 | tf_op jit(solution)/shard_map/all_to_all | solution.py:203
  198.3 2.0 %all-to-all-done.2 = f32[8,1,256]{2,1,0:T(1,128)S(1)} async-done(((f32[8,1,256]{2,1,0:T(1,128)}), f32[8,1,256]{2,1,0:T(1,128)S(1)}, u32[]{:S(2)}, u32[]{:S(2)}) %all-to-all-start.2) | async-done | bytes 8224 | tf_op jit(solution)/shard_map/all_to_all | solution.py:203
  (72 shorter events, 16.6 us)
Async XLA Ops:
  0.6 6.7 %copy-start = (bf16[128,256]{1,0:T(8,128)(2,1)S(1)}, bf16[128,256]{1,0:T(8,128)(2,1)}, u32[]{:S(2)}) copy-start(bf16[128,256]{1,0:T(8,128)(2,1)} %param.7) | copy-start | bytes 196612
  0.6 6.1 %copy-start.3 = (bf16[128,256]{1,0:T(8,128)(2,1)S(1)}, bf16[128,256]{1,0:T(8,128)(2,1)}, u32[]{:S(2)}) copy-start(bf16[128,256]{1,0:T(8,128)(2,1)} %param.8) | copy-start | bytes 196612
  2.4 0.6 copy-start.10
  2.4 4.2 %copy-start.11 = (f32[128,1,16]{0,2,1:T(8,128)}, f32[128,1,16]{0,2,1:T(8,128)S(1)}, u32[]{:S(2)}) copy-start(f32[128,1,16]{0,2,1:T(8,128)S(1)} %copy.84) | copy-start | bytes 24580
  5.2 2.1 %copy-start.1 = (bf16[128,1024]{0,1:T(8,128)(2,1)}, bf16[128,1024]{0,1:T(8,128)(2,1)S(1)}, u32[]{:S(2)}) copy-start(bf16[128,1024]{0,1:T(8,128)(2,1)S(1)} %copy.86) | copy-start | bytes 786436
  16.3 12.0 %copy-start.16 = (f32[1,1,16]{2,1,0:T(1,128)S(1)}, f32[1,1,16]{2,1,0:T(1,128)}, u32[]{:S(2)}) copy-start(f32[1,1,16]{2,1,0:T(1,128)} %get-tuple-element.151) | copy-start | bytes 196
  16.3 85.7 %all-to-all-start = ((f32[32,1,16384]{2,1,0:T(1,128)}), f32[32,1,16384]{2,1,0:T(1,128)S(1)}, u32[]{:S(2)}, u32[]{:S(2)}) async-start(f32[32,1,16384]{2,1,0:T(1,128)} %all_to_all.31), calls=%async_computation | async-start | bytes 4194304 | tf_op jit(solution)/shard_map/all_to_all | solution.py:39
  108.7 43.5 %all-to-all-start.1 = ((f32[32,1,16384]{2,1,0:T(1,128)}), f32[32,1,16384]{2,1,0:T(1,128)S(1)}, u32[]{:S(2)}, u32[]{:S(2)}) async-start(f32[32,1,16384]{2,1,0:T(1,128)} %copy.91), calls=%async_computation.1 | async-start | bytes 4194304 | tf_op jit(solution)/shard_map/all_to_all | solution.py:58
  114.7 0.6 copy-start.8
  172.4 3.0 %copy-start.15 = (f32[16]{0:T(128)S(1)}, f32[16]{0:T(128)}, u32[]{:S(2)}) copy-start(f32[16]{0:T(128)} %get-tuple-element.129) | copy-start | bytes 196
  172.4 3.7 %copy-start.4 = (f32[128,256]{0,1:T(8,128)S(1)}, f32[128,256]{0,1:T(8,128)}, u32[]{:S(2)}) copy-start(f32[128,256]{0,1:T(8,128)} %copy.127) | copy-start | bytes 393220
  175.3 1.1 copy-start.12
  175.3 1.1 copy-start.13
  175.3 1.2 copy-start.2
  175.3 1.2 copy-start.9
  175.4 1.1 copy-start.6
  176.2 2.2 %copy-start.14 = (f32[128,16]{0,1:T(8,128)S(1)}, f32[128,16]{0,1:T(8,128)}, u32[]{:S(2)}) copy-start(f32[128,16]{0,1:T(8,128)} %get-tuple-element.157) | copy-start | bytes 24580
  176.2 2.2 %copy-start.17 = (f32[16]{0:T(128)S(1)}, f32[16]{0:T(128)}, u32[]{:S(2)}) copy-start(f32[16]{0:T(128)} %param.10) | copy-start | bytes 196
  176.2 19.5 %copy-start.5 = (f32[128,256]{1,0:T(8,128)S(1)}, f32[128,256]{1,0:T(8,128)}, u32[]{:S(2)}) copy-start(f32[128,256]{1,0:T(8,128)} %copy.109) | copy-start | bytes 393220
  176.2 19.5 %copy-start.7 = (f32[128,128]{1,0:T(8,128)S(1)}, f32[128,128]{1,0:T(8,128)}, u32[]{:S(2)}) copy-start(f32[128,128]{1,0:T(8,128)} %get-tuple-element.148) | copy-start | bytes 196612
  179.4 21.0 %all-to-all-start.2 = ((f32[8,1,256]{2,1,0:T(1,128)}), f32[8,1,256]{2,1,0:T(1,128)S(1)}, u32[]{:S(2)}, u32[]{:S(2)}) async-start(f32[8,1,256]{2,1,0:T(1,128)} %reshape.448), calls=%async_computation.2 | async-start | bytes 16384 | tf_op jit(solution)/shard_map/all_to_all | solution.py:203

commit v2 on v1

--- a/solution.py
+++ b/solution.py
@@ -1,4 +1,5 @@
 import jax
+import numpy as np
 import jax.numpy as jnp
 from jax import lax
 from jax.sharding import PartitionSpec as P
@@ -30,21 +31,25 @@
 def seq_scan(device_log, device_fwd, device_bwd, axis):
     count = lax.axis_size(axis)
     place = lax.axis_index(axis)
-    logs = lax.all_gather(device_log, axis).reshape(count, -1)
-    heads = logs.shape[1]
+    logs = device_log.reshape(-1)
+    heads = logs.shape[0]
     stacked = jnp.stack([device_fwd, device_bwd])
     shape = stacked.shape
     combos = 2 * heads
-    flat = stacked.reshape(count, -1)
-    pieces = lax.all_to_all(flat, axis, 0, 0, tiled=True)
     if combos % count == 0:
         per = combos // count
+        targets = np.arange(count)[:, None] * per + np.arange(per)[None, :]
         held = place * per + jnp.arange(per)
     else:
         per = 1
+        targets = (np.arange(count) // (count // combos))[:, None]
         held = (place // (count // combos))[None]
-    pieces = pieces.reshape(count, per, -1)
-    chosen = jnp.take(logs, held % heads, axis=1)
+    flat = stacked.reshape(count, per, -1)
+    tags = jnp.broadcast_to(logs[targets % heads][..., None], (count, per, 128))
+    payload = jnp.concatenate([flat, tags], axis=2)
+    pieces = lax.all_to_all(payload, axis, 0, 0, tiled=True)
+    chosen = pieces[:, :, flat.shape[2]]
+    pieces = pieces[:, :, : flat.shape[2]]
     position = jnp.arange(count)
     low = jnp.minimum(position[:, None], position[None, :])
     high = jnp.maximum(position[:, None], position[None, :])
@@ -55,10 +60,9 @@
     mask = jnp.where((held < heads)[:, None, None], before[None], after[None])
     weights = jnp.where(mask, jnp.exp(exponent), 0.0)
     scanned = jnp.einsum("cij,jcx->icx", weights, pieces, precision=precise)
-    back = lax.all_to_all(scanned.reshape(count, -1), axis, 0, 0, tiled=True)
+    back = lax.all_to_all(scanned, axis, 0, 0, tiled=True)
     back = back.reshape(shape)
     return back[0], back[1]
-
 
 def summarize(inputs, out_grad, input_proj, readout, step_size, decay_rate):
     cumulative = jnp.cumsum(-decay_rate[None] * step_size, axis=0)

time: 203 us -> 179 us (0.88)
  blocking collectives: 72 us -> 0 us
  waiting for transfers between devices: 28.5 us -> 85.3 us
  starting transfers between devices: 32.6 us -> 26.5 us
    all_gather x1 -> x0, blocking collectives: 72 us -> none  [seq_scan(): logs = lax.all_gather(device_log, axis).reshape(count, -1)]
    all_to_all x2, waiting for transfers between devices: 26.5 us -> 83.4 us  [the longest x1 48.6 us: seq_scan(): pieces = lax.all_to_all(payload, axis, 0, 0, tiled=True)]
    all_to_all x1, starting transfers between devices: 16.3 us -> 7.58 us  [body(): lax.all_to_all(grad_step, 'tp', split_axis=0, concat_axis=1, tiled=True)]
    all_to_all x1 -> x0, local copies, waits for them, and re-layouts: 5.46 us -> none  [seq_scan(): pieces = lax.all_to_all(flat, axis, 0, 0, tiled=True)]
    concatenate x0 -> x1, local copies, waits for them, and re-layouts: none -> 3.53 us  [seq_scan(): payload = jnp.concatenate([flat, tags], axis=2)]
    reshape x0 -> x1, local copies, waits for them, and re-layouts: none -> 2.93 us  [seq_scan(): flat = stacked.reshape(count, per, -1)]
    all_to_all x2, starting transfers between devices: 16.3 us -> 18.9 us  [the longest x1 12 us: seq_scan(): pieces = lax.all_to_all(payload, axis, 0, 0, tiled=True)]
    unnamed x43 -> x49, local copies, waits for them, and re-layouts: 6.02 us -> 6.09 us
  transfers between devices with their start and end apart: 3 -> 3, of which waited for: 2 -> 3; matrix products, arithmetic and copies ran while one was open for 8% -> 8% of each run, Pallas kernels for 0% -> 0%
where the time goes in v2:
time: 179 us; the launch traced here: 178 us
  waiting for transfers between devices  85.3 us (48%)
  local copies, waits for them, and re-layouts  28.8 us (16%)
  starting transfers between devices  26.5 us (15%)
  other arithmetic  18.5 us (10%)
  matrix products  18.1 us (10%)
    all_to_all x1, waiting for transfers between devices, seq_scan(): pieces = lax.all_to_all(payload, axis, 0, 0, tiled=True)  48.6 us
    all_to_all x1, waiting for transfers between devices, seq_scan(): back = lax.all_to_all(scanned, axis, 0, 0, tiled=True)  34.8 us
    all_to_all x1, starting transfers between devices, seq_scan(): pieces = lax.all_to_all(payload, axis, 0, 0, tiled=True)  12 us
    reduce_sum x1, other arithmetic, span_backward(): constant = jnp.exp(totals) * jnp.sum(grad_in * state_in, axis=(2, 3))  9.25 us
    all_to_all x1, starting transfers between devices, body(): lax.all_to_all(grad_step, 'tp', split_axis=0, concat_axis=1, tiled=True)  7.58 us
    all_to_all x1, starting transfers between devices, seq_scan(): back = lax.all_to_all(scanned, axis, 0, 0, tiled=True)  6.9 us
    unnamed x49, local copies, waits for them, and re-layouts  6.09 us
  transfers between devices with their start and end apart: 3, of which 3 were waited for; matrix products, arithmetic and copies ran while one was open for 8% of the time, Pallas kernels for 0%

profile of v2, /device:TPU:1, one launch (start us, length us, event | category | flops | bytes accessed | tf_op | source)
XLA Modules:
  0.0 178.2 jit_solution(1155358781079610206)
XLA Ops:
  2.4 1.1 copy.112
  4.7 1.4 fusion.52
  7.7 2.7 %copy.114 = f32[2,1,16,256,64]{4,3,2,0,1:T(8,128)} copy(f32[2,1,16,256,64]{3,4,2,1,0:T(8,128)S(1)} %pad_maximum_fusion.1) | data formatting | bytes 4194304 | tf_op jit(solution)/shard_map/stack | solution.py:36
  10.3 2.9 %reshape.373 = f32[32,1,16384]{2,0,1:T(8,128)S(1)} reshape(f32[2,1,16,256,64]{4,3,2,0,1:T(8,128)} %copy.114) | data formatting | bytes 4194304 | tf_op jit(solution)/shard_map/reshape | solution.py:47
  14.2 3.5 %copy.115 = f32[32,1,16512]{2,1,0:T(1,128)} copy(f32[32,1,16512]{2,0,1:T(8,128)S(1)} %pad_maximum_fusion) | data formatting | bytes 4227072 | tf_op jit(solution)/shard_map/concatenate | solution.py:49
  17.8 12.0 %all-to-all-start = ((f32[32,1,16512]{2,1,0:T(1,128)}), f32[32,1,16512]{2,1,0:T(1,128)S(1)}, u32[]{:S(2)}, u32[]{:S(2)}) async-start(f32[32,1,16512]{2,1,0:T(1,128)} %copy.115), calls=%async_computation | async-start | bytes 4227072 | tf_op jit(solution)/shard_map/all_to_all | solution.py:50
  29.8 48.6 %all-to-all-done = f32[32,1,16512]{2,1,0:T(1,128)S(1)} async-done(((f32[32,1,16512]{2,1,0:T(1,128)}), f32[32,1,16512]{2,1,0:T(1,128)S(1)}, u32[]{:S(2)}, u32[]{:S(2)}) %all-to-all-start) | async-done | bytes 2113568 | tf_op jit(solution)/shard_map/all_to_all | solution.py:50
  78.8 1.2 fusion.32
  80.3 3.2 %convolution_bitcast_fusion = f32[32,1,16384]{2,0,1:T(8,128)S(1)} fusion(f32[32,1,16384]{2,1,0:T(1,128)S(1)} %slice.31, f32[32,32]{1,0:T(8,128)S(1)} %bitcast.204, pred[]{:T(512)S(6)} %lt.54), kind=kOutput, calls=%fused_computation.1 | convolution fusion | flops 201330688 | bytes 4198401 | tf_op jit(solution)/shard_map/cij,jcx->icx/dot_general | solution.py:62
  83.5 3.5 %copy.116 = f32[32,1,16384]{2,1,0:T(1,128)} copy(f32[32,1,16384]{2,0,1:T(8,128)S(1)} %convolution_bitcast_fusion) | data formatting | bytes 4194304 | tf_op jit(solution)/shard_map/cij,jcx->icx/transpose | solution.py:62
  87.1 6.9 %all-to-all-start.1 = ((f32[32,1,16384]{2,1,0:T(1,128)}), f32[32,1,16384]{2,1,0:T(1,128)S(1)}, u32[]{:S(2)}, u32[]{:S(2)}) async-start(f32[32,1,16384]{2,1,0:T(1,128)} %copy.116), calls=%async_computation.1 | async-start | bytes 4194304 | tf_op jit(solution)/shard_map/all_to_all | solution.py:63
  96.3 2.2 %broadcast_multiply_fusion = (f32[128,128,1,16]{1,0,3,2:T(8,128)S(1)}, f32[128,128]{1,0:T(8,128)}) fusion(f32[128,128]{1,0:T(8,128)} %copy.110, f32[128,16]{0,1:T(8,128)} %param.11, bf16[128,16,64]{0,2,1:T(8,128)(2,1)S(1)} %bitcast.191, bf16[128,16,64]{0,2,1:T(8,128)(2,1)} %bitcast.194, f32[128,128]{1,0:T(8,128)S(1)} %fusion.39, f32[128,16]{0,1:T(8,128)} %bitcast.202), kind=kOutput, calls=%fused_computation.52 | convolution fusion | flops 35373056 | bytes 1785856 | tf_op jit(solution)/shard_map/while/body/eval_jaxpr/ughp,sghp->usgh/dot_general | solution.py:105
  98.4 1.4 copy.122
  99.8 2.3 %fusion.54 = f32[128,128,1,16]{0,3,1,2:T(8,128)} fusion(f32[128,128,1,16]{0,3,1,2:T(8,128)} %copy.122), kind=kOutput, calls=%fused_computation.96 | output fusion | flops 33292288 | bytes 2097152 | tf_op jit(solution)/shard_map/while/body/eval_jaxpr/jit(cumsum)/reduce_window_sum | solution.py:126
  102.2 2.6 %copy.123 = f32[128,128,1,16]{1,0,3,2:T(8,128)} copy(f32[128,128,1,16]{0,3,1,2:T(8,128)} %fusion.54) | data formatting | bytes 2097152 | tf_op jit(solution)/shard_map/while/body/eval_jaxpr/jit(cumsum)/reduce_window_sum | solution.py:126
  104.7 1.9 %multiply_reduce_fusion.1 = f32[128,16]{0,1:T(8,128)} fusion(f32[128,128,1,16]{1,0,3,2:T(8,128)} %copy.123, f32[128,128,1,16]{1,0,3,2:T(8,128)S(1)} %get-tuple-element.127, f32[128,128]{1,0:T(8,128)} %copy-done.8), kind=kLoop, calls=%fused_computation.39 | loop fusion | flops 784384 | bytes 2170880 | tf_op jit(solution)/shard_map/while/body/eval_jaxpr/reduce_sum | solution.py:127
  106.7 34.8 %all-to-all-done.1 = f32[32,1,16384]{2,1,0:T(1,128)S(1)} async-done(((f32[32,1,16384]{2,1,0:T(1,128)}), f32[32,1,16384]{2,1,0:T(1,128)S(1)}, u32[]{:S(2)}, u32[]{:S(2)}) %all-to-all-start.1) | async-done | bytes 2097184 | tf_op jit(solution)/shard_map/all_to_all | solution.py:63
  141.5 9.3 %multiply_reduce_fusion = (f32[16]{0:T(128)}, f32[16,16384]{1,0:T(8,128)S(1)}, f32[16,16384]{1,0:T(8,128)}) fusion(f32[32,1,16384]{2,1,0:T(1,128)S(1)} %all-to-all-done.1), kind=kLoop, calls=%fused_computation.38 | loop fusion | flops 524272 | bytes 4194368 | tf_op jit(solution)/shard_map/while/body/eval_jaxpr/reduce_sum | solution.py:132
  150.8 2.1 %mul.296 = f32[16,256,64]{2,1,0:T(8,128)S(1)} reshape(f32[16,16384]{1,0:T(8,128)} %get-tuple-element.124) | data formatting | bytes 2097152 | tf_op jit(solution)/shard_map/mul | solution.py:203
  152.8 3.2 %multiply_reduce_fusion.2 = (f32[128,16]{0,1:T(8,128)}, f32[128,16,64]{0,2,1:T(8,128)}) fusion(bf16[128,1024]{0,1:T(8,128)(2,1)S(1)} %copy.112, f32[16,256,64]{2,1,0:T(8,128)S(1)} %mul.296, bf16[128,256]{1,0:T(8,128)(2,1)S(1)} %copy-done), kind=kOutput, calls=%fused_computation.51 | convolution fusion | flops 403044352 | bytes 1908736 | tf_op jit(solution)/shard_map/while/body/eval_jaxpr/ghnp,sgn->sghp/dot_general | solution.py:109
  156.0 1.9 %fusion.2 = f32[128,256]{0,1:T(8,128)} fusion(f32[16,256,64]{2,1,0:T(8,128)S(1)} %mul.296, bf16[128,16,64]{0,2,1:T(8,128)(2,1)S(1)} %bitcast.192, f32[128,16]{0,1:T(8,128)S(1)} %get-tuple-element.125), kind=kOutput, calls=%fused_computation.7 | convolution fusion | flops 403668992 | bytes 1449984 | tf_op jit(solution)/shard_map/while/body/eval_jaxpr/ghnp,sghp->sghn/dot_general | solution.py:117
  158.7 2.2 %fusion.4 = (f32[128,256]{0,1:T(8,128)S(1)}, f32[16,256,128]{2,1,0:T(8,128)S(1)}) fusion(f32[128,16]{0,1:T(8,128)S(1)} %get-tuple-element.131, f32[16,256,64]{2,1,0:T(8,128)S(1)} %slice.27, bf16[128,16,64]{0,2,1:T(8,128)(2,1)} %bitcast.195), kind=kOutput, calls=%fused_computation.11 | convolution fusion | flops 403668992 | bytes 3547136 | tf_op jit(solution)/shard_map/while/body/eval_jaxpr/ghnp,ughp->ughn/dot_general | solution.py:121
  164.1 7.6 %all-to-all-start.2 = ((f32[8,1,256]{2,1,0:T(1,128)}), f32[8,1,256]{2,1,0:T(1,128)S(1)}, u32[]{:S(2)}, u32[]{:S(2)}) async-start(f32[8,1,256]{2,1,0:T(1,128)} %reshape.402), calls=%async_computation.2 | async-start | bytes 16384 | tf_op jit(solution)/shard_map/all_to_all | solution.py:207
  174.4 1.8 %all-to-all-done.2 = f32[8,1,256]{2,1,0:T(1,128)S(1)} async-done(((f32[8,1,256]{2,1,0:T(1,128)}), f32[8,1,256]{2,1,0:T(1,128)S(1)}, u32[]{:S(2)}, u32[]{:S(2)}) %all-to-all-start.2) | async-done | bytes 8224 | tf_op jit(solution)/shard_map/all_to_all | solution.py:207
  (83 shorter events, 16.7 us)
Async XLA Ops:
  0.6 5.6 %copy-start = (bf16[128,256]{1,0:T(8,128)(2,1)S(1)}, bf16[128,256]{1,0:T(8,128)(2,1)}, u32[]{:S(2)}) copy-start(bf16[128,256]{1,0:T(8,128)(2,1)} %param.9) | copy-start | bytes 196612
  2.3 3.8 %copy-start.10 = (f32[128,1,16]{2,1,0:T(1,128)}, f32[128,1,16]{2,1,0:T(1,128)S(1)}, u32[]{:S(2)}) copy-start(f32[128,1,16]{2,1,0:T(1,128)S(1)} %fusion.53) | copy-start | bytes 24580
  2.4 4.4 %copy-start.11 = (f32[128,1,16]{0,2,1:T(8,128)}, f32[128,1,16]{0,2,1:T(8,128)S(1)}, u32[]{:S(2)}) copy-start(f32[128,1,16]{0,2,1:T(8,128)S(1)} %copy.109) | copy-start | bytes 24580
  2.4 4.4 %copy-start.3 = (bf16[128,256]{1,0:T(8,128)(2,1)S(1)}, bf16[128,256]{1,0:T(8,128)(2,1)}, u32[]{:S(2)}) copy-start(bf16[128,256]{1,0:T(8,128)(2,1)} %param.10) | copy-start | bytes 196612
  4.7 2.7 %copy-start.1 = (bf16[128,1024]{0,1:T(8,128)(2,1)}, bf16[128,1024]{0,1:T(8,128)(2,1)S(1)}, u32[]{:S(2)}) copy-start(bf16[128,1024]{0,1:T(8,128)(2,1)S(1)} %copy.111) | copy-start | bytes 786436
  10.3 2.9 %copy-start.19 = (s32[32]{0:T(128)S(1)}, s32[32]{0:T(128)}, u32[]{:S(2)}) copy-start(s32[32]{0:T(128)} %constant.94) | copy-start | bytes 388
  17.8 60.7 %all-to-all-start = ((f32[32,1,16512]{2,1,0:T(1,128)}), f32[32,1,16512]{2,1,0:T(1,128)S(1)}, u32[]{:S(2)}, u32[]{:S(2)}) async-start(f32[32,1,16512]{2,1,0:T(1,128)} %copy.115), calls=%async_computation | async-start | bytes 4227072 | tf_op jit(solution)/shard_map/all_to_all | solution.py:50
  87.1 54.4 %all-to-all-start.1 = ((f32[32,1,16384]{2,1,0:T(1,128)}), f32[32,1,16384]{2,1,0:T(1,128)S(1)}, u32[]{:S(2)}, u32[]{:S(2)}) async-start(f32[32,1,16384]{2,1,0:T(1,128)} %copy.116), calls=%async_computation.1 | async-start | bytes 4194304 | tf_op jit(solution)/shard_map/all_to_all | solution.py:63
  95.6 0.6 copy-start.8
  158.7 2.4 %copy-start.18 = (f32[16]{0:T(128)S(1)}, f32[16]{0:T(128)}, u32[]{:S(2)}) copy-start(f32[16]{0:T(128)} %get-tuple-element.122) | copy-start | bytes 196
  158.7 3.0 %copy-start.5 = (f32[128,256]{0,1:T(8,128)S(1)}, f32[128,256]{0,1:T(8,128)}, u32[]{:S(2)}) copy-start(f32[128,256]{0,1:T(8,128)} %copy.152) | copy-start | bytes 393220
  160.9 0.9 copy-start.12
  161.0 0.9 copy-start.14
  161.0 1.1 copy-start.2
  161.0 1.1 copy-start.6
  161.0 1.1 copy-start.9
  161.0 1.1 copy-start.13
  161.0 1.1 copy-start.15
  161.0 1.1 copy-start.17
  161.7 1.4 copy-start.16
  161.7 1.4 copy-start.20
  161.9 9.9 %copy-start.4 = (f32[128,256]{0,1:T(8,128)S(1)}, f32[128,256]{0,1:T(8,128)}, u32[]{:S(2)}) copy-start(f32[128,256]{0,1:T(8,128)} %fusion.2) | copy-start | bytes 393220
  161.9 10.0 %copy-start.7 = (f32[128,128]{1,0:T(8,128)S(1)}, f32[128,128]{1,0:T(8,128)}, u32[]{:S(2)}) copy-start(f32[128,128]{1,0:T(8,128)} %get-tuple-element.128) | copy-start | bytes 196612
  164.1 12.2 %all-to-all-start.2 = ((f32[8,1,256]{2,1,0:T(1,128)}), f32[8,1,256]{2,1,0:T(1,128)S(1)}, u32[]{:S(2)}, u32[]{:S(2)}) async-start(f32[8,1,256]{2,1,0:T(1,128)} %reshape.402), calls=%async_computation.2 | async-start | bytes 16384 | tf_op jit(solution)/shard_map/all_to_all | solution.py:207

commit v3 on v2

--- a/solution.py
+++ b/solution.py
@@ -33,7 +33,7 @@
     place = lax.axis_index(axis)
     logs = device_log.reshape(-1)
     heads = logs.shape[0]
-    stacked = jnp.stack([device_fwd, device_bwd])
+    stacked = jnp.stack([device_fwd, device_bwd]).transpose(0, 1, 3, 2, 4)
     shape = stacked.shape
     combos = 2 * heads
     if combos % count == 0:
@@ -61,7 +61,7 @@
     weights = jnp.where(mask, jnp.exp(exponent), 0.0)
     scanned = jnp.einsum("cij,jcx->icx", weights, pieces, precision=precise)
     back = lax.all_to_all(scanned, axis, 0, 0, tiled=True)
-    back = back.reshape(shape)
+    back = back.reshape(shape).transpose(0, 1, 3, 2, 4)
     return back[0], back[1]
 
 def summarize(inputs, out_grad, input_proj, readout, step_size, decay_rate):
@@ -69,14 +69,14 @@
     totals = cumulative[-1]
     to_end = jnp.exp(totals[None] - cumulative) * step_size
     forward = jnp.einsum(
-        "qghp,qgn->ghnp",
+        "qghp,qgn->gnhp",
         inputs.astype(jnp.float32) * to_end[..., None],
         input_proj.astype(jnp.float32),
         precision=precise,
     )
     from_start = jnp.exp(cumulative)
     backward = jnp.einsum(
-        "qghp,qgn->ghnp",
+        "qghp,qgn->gnhp",
         out_grad.astype(jnp.float32) * from_start[..., None],
         readout.astype(jnp.float32),
         precision=precise,
@@ -84,9 +84,40 @@
     return (totals, forward, backward)
 
 
-def span_backward(
-    inputs_raw, out_raw, proj_raw, read_raw, step_size, decay_rate, state_in, grad_in
+def span_local(inputs_raw, out_raw, proj_raw, read_raw, step_size, decay_rate):
+    inputs = inputs_raw.astype(jnp.float32)
+    out_grad = out_raw.astype(jnp.float32)
+    input_proj = proj_raw.astype(jnp.float32)
+    readout = read_raw.astype(jnp.float32)
+    length = inputs.shape[0]
+    position = jnp.arange(length)
+    causal = (position[:, None] >= position[None, :]).astype(jnp.float32)
+    cumulative = jnp.cumsum(-decay_rate[None] * step_size, axis=0)
+    totals = cumulative[-1]
+    spread = cumulative[:, None] - cumulative[None, :]
+    decays = jnp.exp(jnp.minimum(spread, 0.0)) * causal[:, :, None, None]
+    to_end = jnp.exp(totals[None] - cumulative)
+    from_start = jnp.exp(cumulative)
+    state_match = jnp.einsum("ugn,sgn->usg", read_raw, proj_raw, preferred_element_type=jnp.float32)
+    grad_match = jnp.einsum(
+        "ughp,sghp->usgh", out_raw, inputs_raw, preferred_element_type=jnp.float32
+    )
+    mix_input = decays * state_match[..., None]
+    vector = jnp.einsum("usgh,ughp->sghp", mix_input, out_grad, precision=precise)
+    direct = jnp.sum(inputs * vector, axis=-1)
+    mix_state = decays * grad_match * step_size[None]
+    grad_proj = jnp.einsum("usgh,ugn->sgn", mix_state, readout, precision=precise)
+    grad_read = jnp.einsum("usgh,sgn->ugn", mix_state, input_proj, precision=precise)
+    weights = mix_state * state_match[..., None]
+    exclusive = jnp.cumsum(weights, axis=1) - weights
+    paired = jnp.sum(exclusive * causal[:, :, None, None], axis=0)
+    return (vector, direct, grad_proj, grad_read, paired)
+
+
+def span_state(
+    inputs_raw, out_raw, proj_raw, read_raw, step_size, decay_rate, state_in, grad_in, local
 ):
+    vector, direct, grad_proj, grad_read, paired = local
     inputs = inputs_raw.astype(jnp.float32)
     out_grad = out_raw.astype(jnp.float32)
     input_proj = proj_raw.astype(jnp.float32)
@@ -97,46 +128,30 @@
     strictly = (position[:, None] < position[None, :]).astype(jnp.float32)
     cumulative = jnp.cumsum(-decay_rate[None] * step_size, axis=0)
     totals = cumulative[-1]
-    spread = cumulative[:, None] - cumulative[None, :]
-    decays = jnp.exp(jnp.minimum(spread, 0.0)) * causal[:, :, None, None]
     to_end = jnp.exp(totals[None] - cumulative)
     from_start = jnp.exp(cumulative)
-    state_match = jnp.einsum("ugn,sgn->usg", read_raw, proj_raw, preferred_element_type=jnp.float32)
-    grad_match = jnp.einsum(
-        "ughp,sghp->usgh", out_raw, inputs_raw, preferred_element_type=jnp.float32
-    )
-    mix_input = decays * state_match[..., None]
-    back_b = jnp.einsum("ghnp,sgn->sghp", grad_in, input_proj, precision=precise)
-    vector = (
-        jnp.einsum("usgh,ughp->sghp", mix_input, out_grad, precision=precise)
-        + to_end[..., None] * back_b
-    )
+    back_b = jnp.einsum("gnhp,sgn->sghp", grad_in, input_proj, precision=precise)
+    vector = vector + to_end[..., None] * back_b
     grad_inputs = step_size[..., None] * vector
-    direct = jnp.sum(inputs * vector, axis=-1)
-    mix_state = decays * grad_match * step_size[None]
-    back_x = jnp.einsum("ghnp,sghp->sghn", grad_in, inputs, precision=precise)
-    grad_proj = jnp.einsum("usgh,ugn->sgn", mix_state, readout, precision=precise) + jnp.einsum(
-        "sgh,sghn->sgn", step_size * to_end, back_x, precision=precise
-    )
-    state_out = jnp.einsum("ghnp,ughp->ughn", state_in, out_grad, precision=precise)
-    grad_read = jnp.einsum("usgh,sgn->ugn", mix_state, input_proj, precision=precise) + jnp.einsum(
-        "ugh,ughn->ugn", from_start, state_out, precision=precise
-    )
-    weights = mix_state * state_match[..., None]
-    exclusive = jnp.cumsum(weights, axis=1) - weights
-    paired = jnp.sum(exclusive * causal[:, :, None, None], axis=0)
-    from_init = from_start * jnp.einsum("ugn,ughn->ugh", readout, state_out, precision=precise)
+    tail_dot = jnp.sum(inputs * back_b, axis=-1)
+    direct = direct + to_end * tail_dot
+    scaled_x = (step_size * to_end)[..., None] * inputs
+    grad_proj = grad_proj + jnp.einsum("sghp,gnhp->sgn", scaled_x, grad_in, precision=precise)
+    scaled_y = from_start[..., None] * out_grad
+    grad_read = grad_read + jnp.einsum("ughp,gnhp->ugn", scaled_y, state_in, precision=precise)
+    read_state = jnp.einsum("ugn,gnhp->ughp", readout, state_in, precision=precise)
+    from_init = from_start * jnp.sum(read_state * out_grad, axis=-1)
     suffixes = jnp.einsum("ut,ugh->tgh", causal, from_init, precision=precise)
-    from_tail = to_end * step_size * jnp.sum(inputs * back_b, axis=-1)
+    from_tail = to_end * step_size * tail_dot
     prefixes = jnp.einsum("st,sgh->tgh", strictly, from_tail, precision=precise)
-    constant = jnp.exp(totals) * jnp.sum(grad_in * state_in, axis=(2, 3))
+    constant = jnp.exp(totals) * jnp.einsum("gnhp,gnhp->gh", grad_in, state_in, precision=precise)
     grad_log = paired + suffixes + prefixes + constant[None]
     grad_step = direct - decay_rate[None] * grad_log
     return (grad_inputs, grad_proj, grad_read, grad_step)
 
 
 def combine(earlier, later):
-    return (earlier[0] + later[0], jnp.exp(later[0])[..., None, None] * earlier[1] + later[1])
+    return (earlier[0] + later[0], jnp.exp(later[0])[:, None, :, None] * earlier[1] + later[1])
 
 
 def span_prefix(log_sums, states, reverse):
@@ -162,31 +177,10 @@
     )
 
 
-def summaries(blocks, rate_rows):
-
-    def summarize_one(element):
-        return summarize(element[0], element[1], element[2], element[3], element[4], rate_rows)
-
-    return lax.map(summarize_one, blocks)
-
-
-def apply_backward(blocks, rate_rows, state_ins, grad_ins):
-
-    def backward_one(element):
-        return span_backward(
-            element[0],
-            element[1],
-            element[2],
-            element[3],
-            element[4],
-            rate_rows,
-            element[5],
-            element[6],
-        )
-
-    gradients = lax.map(backward_one, blocks + (state_ins, grad_ins))
-    tokens = gradients[0].shape[0] * gradients[0].shape[1]
-    return tuple((item_grad.reshape(tokens, -1) for item_grad in gradients))
+def over_spans(function, items):
+    if jax.tree.leaves(items)[0].shape[0] == 1:
+        return jax.tree.map(lambda a: a[None], function(jax.tree.map(lambda a: a[0], items)))
+    return lax.map(function, items)
 
 
 def body(inputs, input_proj, readout, step_size, decay_rate, out_grad):
@@ -195,15 +189,24 @@
         inputs, out_grad, input_proj, readout, step_size, group_count, D_STATE, HEAD_DIM, SPAN
     )
     rate_rows = decay_rate.reshape(group_count, -1)
-    totals, forward, backward = summaries(blocks, rate_rows)
-    (device_log, device_fwd), (log_before, fwd_before) = span_prefix(totals, forward, False)
-    (ignored_log, device_bwd), (log_after, bwd_after) = span_prefix(totals, backward, True)
+    totals, forward, backward = over_spans(lambda e: summarize(*e, rate_rows), blocks)
+    if totals.shape[0] == 1:
+        device_log, device_fwd, device_bwd = totals[0], forward[0], backward[0]
+        log_before = log_after = jnp.zeros_like(totals)
+        fwd_before = bwd_after = jnp.zeros_like(forward)
+    else:
+        (device_log, device_fwd), (log_before, fwd_before) = span_prefix(totals, forward, False)
+        (ignored_log, device_bwd), (log_after, bwd_after) = span_prefix(totals, backward, True)
+    local = over_spans(lambda e: span_local(*e, rate_rows), blocks)
     device_in, device_out = seq_scan(device_log, device_fwd, device_bwd, "seq")
-    state_ins = fwd_before + jnp.exp(log_before)[..., None, None] * device_in[None]
-    grad_ins = bwd_after + jnp.exp(log_after)[..., None, None] * device_out[None]
-    grad_inputs, grad_proj, grad_read, grad_step = apply_backward(
-        blocks, rate_rows, state_ins, grad_ins
-    )
+    state_ins = fwd_before + jnp.exp(log_before)[:, :, None, :, None] * device_in[None]
+    grad_ins = bwd_after + jnp.exp(log_after)[:, :, None, :, None] * device_out[None]
+    gradients = over_spans(
+        lambda e: span_state(*e[0], rate_rows, e[1], e[2], e[3]),
+        (blocks, state_ins, grad_ins, local),
+    )
+    tokens = gradients[0].shape[0] * gradients[0].shape[1]
+    grad_inputs, grad_proj, grad_read, grad_step = (g.reshape(tokens, -1) for g in gradients)
     regrouped = lax.all_to_all(grad_step, "tp", split_axis=0, concat_axis=1, tiled=True)
     return (
         grad_inputs.astype(jnp.bfloat16),

time: 179 us -> 178 us (level)
  waiting for transfers between devices: 85.3 us -> 90.8 us
  other arithmetic: 18.5 us -> 15 us
  matrix products: 18.1 us -> 15.4 us
    reduce_sum x2 -> x1, other arithmetic: 11.2 us -> 1.57 us  [span_local(): paired = jnp.sum(exclusive * causal[:, :, None, None], axis=0)]
    all_to_all x0 -> x1, other arithmetic: none -> 6.75 us  [seq_scan(): back = lax.all_to_all(scanned, axis, 0, 0, tiled=True)]
    reshape x0 -> x2, local copies, waits for them, and re-layouts: none -> 6.09 us  [seq_scan(): back = back.reshape(shape).transpose(0, 1, 3, 2, 4)]
    all_to_all x1, waiting for transfers between devices: 34.8 us -> 40.8 us  [seq_scan(): back = lax.all_to_all(scanned, axis, 0, 0, tiled=True)]
    another operation x3 -> x2, local copies, waits for them, and re-layouts: 5.31 us -> 1.63 us  [the longest x1 1.58 us: span_local(): exclusive = jnp.cumsum(weights, axis=1) - weights]
    mul x4 -> x3, local copies, waits for them, and re-layouts: 4.32 us -> 0.75 us  [the longest x1 0.51 us: span_local(): weights = mix_state * state_match[..., None]]
    dot_general x12 -> x13, matrix products: 13.6 us -> 10.2 us  [the longest x1 1.66 us: span_state(): jnp.einsum('ughp,gnhp->ugn', scaled_y, state_in, precision=precise)]
    transpose x0 -> x1, local copies, waits for them, and re-layouts: none -> 2.7 us  [seq_scan(): stacked = jnp.stack([device_fwd, device_bwd]).transpose(0, 1, 3, 2, 4)]
  transfers between devices with their start and end apart: 3 -> 3, of which waited for: 3 -> 3; matrix products, arithmetic and copies ran while one was open for 8% -> 5% of each run, Pallas kernels for 0% -> 0%
where the time goes in v3:
time: 178 us; the launch traced here: 177 us
  waiting for transfers between devices  90.8 us (51%)
  local copies, waits for them, and re-layouts  27.9 us (16%)
  starting transfers between devices  27.2 us (15%)
  matrix products  15.4 us (9%)
  other arithmetic  15 us (8%)
    all_to_all x1, waiting for transfers between devices, seq_scan(): pieces = lax.all_to_all(payload, axis, 0, 0, tiled=True)  48 us
    all_to_all x1, waiting for transfers between devices, seq_scan(): back = lax.all_to_all(scanned, axis, 0, 0, tiled=True)  40.8 us
    all_to_all x1, starting transfers between devices, seq_scan(): pieces = lax.all_to_all(payload, axis, 0, 0, tiled=True)  12 us
    all_to_all x1, starting transfers between devices, body(): lax.all_to_all(grad_step, 'tp', split_axis=0, concat_axis=1, tiled=True)  8.07 us
    all_to_all x1, starting transfers between devices, seq_scan(): back = lax.all_to_all(scanned, axis, 0, 0, tiled=True)  7.15 us
    all_to_all x1, other arithmetic, seq_scan(): back = lax.all_to_all(scanned, axis, 0, 0, tiled=True)  6.75 us
    reshape x2, local copies, waits for them, and re-layouts, seq_scan(): back = back.reshape(shape).transpose(0, 1, 3, 2, 4)  6.09 us
    unnamed x50, local copies, waits for them, and re-layouts  4.78 us
  transfers between devices with their start and end apart: 3, of which 3 were waited for; matrix products, arithmetic and copies ran while one was open for 5% of the time, Pallas kernels for 0%

profile of v3, /device:TPU:1, one launch (start us, length us, event | category | flops | bytes accessed | tf_op | source)
XLA Modules:
  0.0 177.5 jit_solution(5216300941156466898)
XLA Ops:
  2.4 1.1 copy.70
  3.6 1.2 copy.69
  4.8 1.4 fusion.57
  7.7 2.7 %copy.72 = f32[2,1,16,256,64]{4,3,2,0,1:T(8,128)} copy(f32[2,1,16,256,64]{3,4,2,1,0:T(8,128)S(1)} %maximum_bitcast_fusion) | data formatting | bytes 4194304 | tf_op jit(solution)/shard_map/transpose | solution.py:36
  10.4 2.9 %reshape.324 = f32[32,1,16384]{2,0,1:T(8,128)S(1)} reshape(f32[2,1,16,256,64]{4,3,2,0,1:T(8,128)} %copy.72) | data formatting | bytes 4194304 | tf_op jit(solution)/shard_map/reshape | solution.py:47
  14.3 3.5 %copy.73 = f32[32,1,16512]{2,1,0:T(1,128)} copy(f32[32,1,16512]{2,0,1:T(8,128)S(1)} %pad_maximum_fusion) | data formatting | bytes 4227072 | tf_op jit(solution)/shard_map/concatenate | solution.py:49
  17.8 12.0 %all-to-all-start = ((f32[32,1,16512]{2,1,0:T(1,128)}), f32[32,1,16512]{2,1,0:T(1,128)S(1)}, u32[]{:S(2)}, u32[]{:S(2)}) async-start(f32[32,1,16512]{2,1,0:T(1,128)} %copy.73), calls=%async_computation | async-start | bytes 4227072 | tf_op jit(solution)/shard_map/all_to_all | solution.py:50
  30.5 48.0 %all-to-all-done = f32[32,1,16512]{2,1,0:T(1,128)S(1)} async-done(((f32[32,1,16512]{2,1,0:T(1,128)}), f32[32,1,16512]{2,1,0:T(1,128)S(1)}, u32[]{:S(2)}, u32[]{:S(2)}) %all-to-all-start) | async-done | bytes 2113568 | tf_op jit(solution)/shard_map/all_to_all | solution.py:50
  78.8 1.9 %fusion.37 = f32[1,32,32]{2,0,1:T(1,128)S(1)} fusion(s32[32,32]{1,0:T(8,128)} %get-tuple-element.32, s32[32,32]{1,0:T(8,128)} %get-tuple-element.33, f32[32]{0:T(128)S(1)} %slice_reduce_fusion), kind=kOutput, calls=%fused_computation.64 | convolution fusion | flops 491520 | bytes 12416 | tf_op jit(solution)/shard_map/ijm,mc->cij/dot_general | solution.py:57
  81.1 3.2 %convolution_bitcast_fusion = f32[32,1,16384]{2,0,1:T(8,128)S(1)} fusion(f32[32,1,16384]{2,1,0:T(1,128)S(1)} %slice.24, f32[32,32]{1,0:T(8,128)S(1)} %bitcast.197, pred[]{:T(512)S(6)} %lt.49), kind=kOutput, calls=%fused_computation.1 | convolution fusion | flops 201330688 | bytes 4198401 | tf_op jit(solution)/shard_map/cij,jcx->icx/dot_general | solution.py:62
  84.3 3.5 %copy.74 = f32[32,1,16384]{2,1,0:T(1,128)} copy(f32[32,1,16384]{2,0,1:T(8,128)S(1)} %convolution_bitcast_fusion) | data formatting | bytes 4194304 | tf_op jit(solution)/shard_map/cij,jcx->icx/transpose | solution.py:62
  87.8 7.1 %all-to-all-start.1 = ((f32[32,1,16384]{2,1,0:T(1,128)}), f32[32,1,16384]{2,1,0:T(1,128)}, u32[]{:S(2)}, u32[]{:S(2)}) async-start(f32[32,1,16384]{2,1,0:T(1,128)} %copy.74), calls=%async_computation.1 | async-start | bytes 4194304 | tf_op jit(solution)/shard_map/all_to_all | solution.py:63
  95.3 1.2 broadcast_multiply_fusion
  97.0 1.1 fusion.59
  98.1 1.6 copy.81
  99.7 1.6 multiply_reduce_fusion
  101.3 40.8 %all-to-all-done.1 = f32[32,1,16384]{2,1,0:T(1,128)} async-done(((f32[32,1,16384]{2,1,0:T(1,128)}), f32[32,1,16384]{2,1,0:T(1,128)}, u32[]{:S(2)}, u32[]{:S(2)}) %all-to-all-start.1) | async-done | bytes 2097184 | tf_op jit(solution)/shard_map/all_to_all | solution.py:63
  142.0 6.7 %reduce.8 = f32[32,16384]{1,0:T(8,128)S(1)} reduce(f32[32,1,16384]{2,1,0:T(1,128)} %all-to-all-done.1, f32[]{:T(128)} %constant.30), dimensions={1}, to_apply=%all_to_all.21.reduce_sub_computation | reduce | bytes 4194308 | tf_op jit(solution)/shard_map/all_to_all | solution.py:63
  148.8 3.0 %reshape.327 = f32[2,1,16,256,64]{4,3,2,0,1:T(8,128)} reshape(f32[32,16384]{1,0:T(8,128)S(1)} %reduce.8) | data formatting | bytes 4194304 | tf_op jit(solution)/shard_map/reshape | solution.py:64
  151.8 3.1 %copy.75 = f32[2,1,16,256,64]{3,4,2,1,0:T(8,128)S(1)} copy(f32[2,1,16,256,64]{4,3,2,0,1:T(8,128)} %reshape.327) | data formatting | bytes 4194304 | tf_op jit(solution)/shard_map/reshape | solution.py:64
  154.9 1.6 multiply_reduce_fusion.1
  156.7 1.7 convolution_bitcast_fusion.9
  162.8 8.1 %all-to-all-start.2 = ((f32[8,1,256]{2,1,0:T(1,128)}), f32[8,1,256]{2,1,0:T(1,128)S(1)}, u32[]{:S(2)}, u32[]{:S(2)}) async-start(f32[8,1,256]{2,1,0:T(1,128)} %reshape.354), calls=%async_computation.2 | async-start | bytes 16384 | tf_op jit(solution)/shard_map/all_to_all | solution.py:210
  173.5 2.0 %all-to-all-done.2 = f32[8,1,256]{2,1,0:T(1,128)S(1)} async-done(((f32[8,1,256]{2,1,0:T(1,128)}), f32[8,1,256]{2,1,0:T(1,128)S(1)}, u32[]{:S(2)}, u32[]{:S(2)}) %all-to-all-start.2) | async-done | bytes 8224 | tf_op jit(solution)/shard_map/all_to_all | solution.py:210
  (82 shorter events, 15.3 us)
Async XLA Ops:
  0.6 6.3 %copy-start = (bf16[128,256]{1,0:T(8,128)(2,1)S(1)}, bf16[128,256]{1,0:T(8,128)(2,1)}, u32[]{:S(2)}) copy-start(bf16[128,256]{1,0:T(8,128)(2,1)} %param.9) | copy-start | bytes 196612
  0.6 5.7 %copy-start.4 = (bf16[128,256]{1,0:T(8,128)(2,1)S(1)}, bf16[128,256]{1,0:T(8,128)(2,1)}, u32[]{:S(2)}) copy-start(bf16[128,256]{1,0:T(8,128)(2,1)} %param.10) | copy-start | bytes 196612
  2.4 3.8 %copy-start.9 = (f32[128,1,16]{2,1,0:T(1,128)}, f32[128,1,16]{2,1,0:T(1,128)S(1)}, u32[]{:S(2)}) copy-start(f32[128,1,16]{2,1,0:T(1,128)S(1)} %fusion.58) | copy-start | bytes 24580
  2.4 3.8 %copy-start.10 = (f32[128,1,16]{0,2,1:T(8,128)}, f32[128,1,16]{0,2,1:T(8,128)S(1)}, u32[]{:S(2)}) copy-start(f32[128,1,16]{0,2,1:T(8,128)S(1)} %copy.67) | copy-start | bytes 24580
  3.6 3.3 %copy-start.1 = (bf16[128,1024]{0,1:T(8,128)(2,1)}, bf16[128,1024]{0,1:T(8,128)(2,1)S(1)}, u32[]{:S(2)}) copy-start(bf16[128,1024]{0,1:T(8,128)(2,1)S(1)} %copy.70) | copy-start | bytes 786436
  10.4 2.9 %copy-start.20 = (s32[32]{0:T(128)S(1)}, s32[32]{0:T(128)}, u32[]{:S(2)}) copy-start(s32[32]{0:T(128)} %constant.28) | copy-start | bytes 388
  17.8 60.7 %all-to-all-start = ((f32[32,1,16512]{2,1,0:T(1,128)}), f32[32,1,16512]{2,1,0:T(1,128)S(1)}, u32[]{:S(2)}, u32[]{:S(2)}) async-start(f32[32,1,16512]{2,1,0:T(1,128)} %copy.73), calls=%async_computation | async-start | bytes 4227072 | tf_op jit(solution)/shard_map/all_to_all | solution.py:50
  87.8 7.5 %copy-start.2 = (bf16[128,1024]{0,1:T(8,128)(2,1)S(1)}, bf16[128,1024]{0,1:T(8,128)(2,1)}, u32[]{:S(2)}) copy-start(bf16[128,1024]{0,1:T(8,128)(2,1)} %copy-done.1) | copy-start | bytes 786436
  87.8 7.5 %copy-start.11 = (f32[128,1,16]{0,2,1:T(8,128)S(1)}, f32[128,1,16]{0,2,1:T(8,128)}, u32[]{:S(2)}) copy-start(f32[128,1,16]{0,2,1:T(8,128)} %copy-done.10) | copy-start | bytes 24580
  87.8 7.5 %copy-start.17 = (f32[128,16]{0,1:T(8,128)S(1)}, f32[128,16]{0,1:T(8,128)}, u32[]{:S(2)}) copy-start(f32[128,16]{0,1:T(8,128)} %param.11) | copy-start | bytes 24580
  87.8 54.2 %all-to-all-start.1 = ((f32[32,1,16384]{2,1,0:T(1,128)}), f32[32,1,16384]{2,1,0:T(1,128)}, u32[]{:S(2)}, u32[]{:S(2)}) async-start(f32[32,1,16384]{2,1,0:T(1,128)} %copy.74), calls=%async_computation.1 | async-start | bytes 4194304 | tf_op jit(solution)/shard_map/all_to_all | solution.py:63
  95.2 1.2 copy-start.12
  95.3 1.2 copy-start.7
  156.7 4.0 %copy-start.16 = (f32[128,16]{0,1:T(8,128)S(1)}, f32[128,16]{0,1:T(8,128)}, u32[]{:S(2)}) copy-start(f32[128,16]{0,1:T(8,128)} %multiply_reduce_fusion) | copy-start | bytes 24580
  156.7 4.2 %copy-start.3 = (bf16[128,1024]{0,1:T(8,128)(2,1)S(1)}, bf16[128,1024]{0,1:T(8,128)(2,1)}, u32[]{:S(2)}) copy-start(bf16[128,1024]{0,1:T(8,128)(2,1)} %copy-done.1) | copy-start | bytes 786436
  156.7 4.2 %copy-start.8 = (f32[128,128]{1,0:T(8,128)S(1)}, f32[128,128]{1,0:T(8,128)}, u32[]{:S(2)}) copy-start(f32[128,128]{1,0:T(8,128)} %copy-done.7) | copy-start | bytes 196612
  156.7 4.2 %copy-start.13 = (f32[128,128]{1,0:T(8,128)S(1)}, f32[128,128]{1,0:T(8,128)}, u32[]{:S(2)}) copy-start(f32[128,128]{1,0:T(8,128)} %copy-done.12) | copy-start | bytes 196612
  156.7 4.2 %copy-start.18 = (f32[128,16]{0,1:T(8,128)S(1)}, f32[128,16]{0,1:T(8,128)}, u32[]{:S(2)}) copy-start(f32[128,16]{0,1:T(8,128)} %param.11) | copy-start | bytes 24580
  156.7 4.2 %copy-start.19 = (f32[128,16]{0,1:T(8,128)S(1)}, f32[128,16]{0,1:T(8,128)}, u32[]{:S(2)}) copy-start(f32[128,16]{0,1:T(8,128)} %get-tuple-element.21) | copy-start | bytes 24580
  159.4 2.4 %copy-start.15 = (f32[128,16]{0,1:T(8,128)S(1)}, f32[128,16]{0,1:T(8,128)}, u32[]{:S(2)}) copy-start(f32[128,16]{0,1:T(8,128)} %copy-done.14) | copy-start | bytes 24580
  159.4 2.4 %copy-start.21 = (f32[16]{0:T(128)S(1)}, f32[16]{0:T(128)}, u32[]{:S(2)}) copy-start(f32[16]{0:T(128)} %param.12) | copy-start | bytes 196
  159.4 11.5 %copy-start.5 = (f32[256,128]{0,1:T(8,128)S(1)}, f32[256,128]{0,1:T(8,128)}, u32[]{:S(2)}) copy-start(f32[256,128]{0,1:T(8,128)} %convolution_bitcast_fusion.9) | copy-start | bytes 393220
  159.4 11.5 %copy-start.6 = (f32[128,128]{1,0:T(8,128)S(1)}, f32[128,128]{1,0:T(8,128)}, u32[]{:S(2)}) copy-start(f32[128,128]{1,0:T(8,128)} %get-tuple-element.23) | copy-start | bytes 196612
  162.8 12.7 %all-to-all-start.2 = ((f32[8,1,256]{2,1,0:T(1,128)}), f32[8,1,256]{2,1,0:T(1,128)S(1)}, u32[]{:S(2)}, u32[]{:S(2)}) async-start(f32[8,1,256]{2,1,0:T(1,128)} %reshape.354), calls=%async_computation.2 | async-start | bytes 16384 | tf_op jit(solution)/shard_map/all_to_all | solution.py:210
  (1 other events, 0.7 us)

commit v4 on v3

--- a/solution.py
+++ b/solution.py
@@ -44,12 +44,14 @@
         per = 1
         targets = (np.arange(count) // (count // combos))[:, None]
         held = (place // (count // combos))[None]
-    flat = stacked.reshape(count, per, -1)
-    tags = jnp.broadcast_to(logs[targets % heads][..., None], (count, per, 128))
+    flat = stacked.reshape(count, per * 8, -1)
+    width = flat.shape[2]
+    tags = jnp.repeat(logs[targets % heads], 8, axis=1)
+    tags = jnp.broadcast_to(tags[..., None], (count, per * 8, 128))
     payload = jnp.concatenate([flat, tags], axis=2)
     pieces = lax.all_to_all(payload, axis, 0, 0, tiled=True)
-    chosen = pieces[:, :, flat.shape[2]]
-    pieces = pieces[:, :, : flat.shape[2]]
+    chosen = pieces[:, ::8, width]
+    pieces = pieces[:, :, :width].reshape(count, per, -1)
     position = jnp.arange(count)
     low = jnp.minimum(position[:, None], position[None, :])
     high = jnp.maximum(position[:, None], position[None, :])
@@ -60,7 +62,7 @@
     mask = jnp.where((held < heads)[:, None, None], before[None], after[None])
     weights = jnp.where(mask, jnp.exp(exponent), 0.0)
     scanned = jnp.einsum("cij,jcx->icx", weights, pieces, precision=precise)
-    back = lax.all_to_all(scanned, axis, 0, 0, tiled=True)
+    back = lax.all_to_all(scanned.reshape(count, per * 8, -1), axis, 0, 0, tiled=True)
     back = back.reshape(shape).transpose(0, 1, 3, 2, 4)
     return back[0], back[1]
 

time: 178 us -> 171 us (0.961)
  waiting for transfers between devices: 90.8 us -> 84.8 us
  other arithmetic: 15 us -> 11.1 us
  local copies, waits for them, and re-layouts: 27.9 us -> 30.2 us
    all_to_all x1, waiting for transfers between devices: 40.8 us -> 31.7 us  [seq_scan(): lax.all_to_all(scanned.reshape(count, per * 8, -1), axis, 0, 0, tiled=True)]
    all_to_all x1 -> x0, other arithmetic: 6.75 us -> none  [seq_scan(): back = lax.all_to_all(scanned, axis, 0, 0, tiled=True)]
    unnamed x50 -> x42, local copies, waits for them, and re-layouts: 4.78 us -> 9.17 us
    concatenate x1 -> x0, local copies, waits for them, and re-layouts: 3.52 us -> none  [seq_scan(): payload = jnp.concatenate([flat, tags], axis=2)]
    transpose x1 -> x0, local copies, waits for them, and re-layouts: 3.46 us -> none  [seq_scan(): scanned = jnp.einsum('cij,jcx->icx', weights, pieces, precision=precise)]
    all_to_all x1, waiting for transfers between devices: 48 us -> 51.1 us  [seq_scan(): pieces = lax.all_to_all(payload, axis, 0, 0, tiled=True)]
    mul x1, local copies, waits for them, and re-layouts: 0.51 us -> 2.61 us  [span_local(): weights = mix_state * state_match[..., None]]
    dot_general x1, matrix products: 1.18 us -> 3.14 us  [span_local(): jnp.einsum('ughp,sghp->usgh', out_raw, inputs_raw, preferred_element_type...]
  transfers between devices with their start and end apart: 3 -> 3, of which waited for: 3 -> 3; matrix products, arithmetic and copies ran while one was open for 5% -> 11% of each run, Pallas kernels for 0% -> 0%
where the time goes in v4:
time: 171 us; the launch traced here: 170 us
  waiting for transfers between devices  84.8 us (50%)
  local copies, waits for them, and re-layouts  30.2 us (18%)
  starting transfers between devices  26.9 us (16%)
  matrix products  16 us (9%)
  other arithmetic  11.1 us (6%)
    all_to_all x1, waiting for transfers between devices, seq_scan(): pieces = lax.all_to_all(payload, axis, 0, 0, tiled=True)  51.1 us
    all_to_all x1, waiting for transfers between devices, seq_scan(): lax.all_to_all(scanned.reshape(count, per * 8, -1), axis, 0, 0, tiled=True)  31.7 us
    all_to_all x1, starting transfers between devices, seq_scan(): pieces = lax.all_to_all(payload, axis, 0, 0, tiled=True)  11.9 us
    unnamed x42, local copies, waits for them, and re-layouts  9.17 us
    all_to_all x1, starting transfers between devices, body(): lax.all_to_all(grad_step, 'tp', split_axis=0, concat_axis=1, tiled=True)  7.79 us
    all_to_all x1, starting transfers between devices, seq_scan(): lax.all_to_all(scanned.reshape(count, per * 8, -1), axis, 0, 0, tiled=True)  7.2 us
    reshape x2, local copies, waits for them, and re-layouts, seq_scan(): back = back.reshape(shape).transpose(0, 1, 3, 2, 4)  5.8 us
    reshape x1, local copies, waits for them, and re-layouts, seq_scan(): flat = stacked.reshape(count, per * 8, -1)  3.61 us
  transfers between devices with their start and end apart: 3, of which 3 were waited for; matrix products, arithmetic and copies ran while one was open for 11% of the time, Pallas kernels for 0%

profile of v4, /device:TPU:1, one launch (start us, length us, event | category | flops | bytes accessed | tf_op | source)
XLA Modules:
  0.0 169.9 jit_solution(2991703952451001509)
XLA Ops:
  3.6 1.2 copy.68
  4.8 1.4 fusion.56
  7.7 2.7 %copy.71 = f32[2,1,16,256,64]{4,3,2,0,1:T(8,128)} copy(f32[2,1,16,256,64]{3,4,2,1,0:T(8,128)S(1)} %maximum_bitcast_fusion) | data formatting | bytes 4194304 | tf_op jit(solution)/shard_map/transpose | solution.py:36
  10.4 3.6 %reshape.327 = f32[32,8,2048]{2,1,0:T(8,128)S(1)} reshape(f32[2,1,16,256,64]{4,3,2,0,1:T(8,128)} %copy.71) | data formatting | bytes 4194304 | tf_op jit(solution)/shard_map/reshape | solution.py:47
  14.9 1.6 pad_maximum_fusion
  16.4 11.9 %all-to-all-start = ((f32[32,8,2176]{2,1,0:T(8,128)}), f32[32,8,2176]{2,1,0:T(8,128)S(1)}, u32[]{:S(2)}, u32[]{:S(2)}) async-start(f32[32,8,2176]{2,1,0:T(8,128)} %pad_maximum_fusion), calls=%async_computation | async-start | bytes 4456448 | tf_op jit(solution)/shard_map/all_to_all | solution.py:52
  28.3 51.1 %all-to-all-done = f32[32,8,2176]{2,1,0:T(8,128)S(1)} async-done(((f32[32,8,2176]{2,1,0:T(8,128)}), f32[32,8,2176]{2,1,0:T(8,128)S(1)}, u32[]{:S(2)}, u32[]{:S(2)}) %all-to-all-start) | async-done | bytes 2228256 | tf_op jit(solution)/shard_map/all_to_all | solution.py:52
  79.7 1.2 copy.93
  82.4 1.9 %fusion.44 = f32[16384,32]{0,1:T(8,128)S(1)} fusion(f32[32,16384]{1,0:T(8,128)S(1)} %bitcast.187, f32[32,32]{1,0:T(8,128)S(1)} %bitcast.204, pred[]{:T(512)S(6)} %lt.49), kind=kOutput, calls=%fused_computation.72 | convolution fusion | flops 201330688 | bytes 4198401 | tf_op jit(solution)/shard_map/cij,jcx->icx/dot_general | solution.py:64
  84.3 2.6 %copy.94 = f32[4,8,8,2048]{3,2,1,0:T(8,128)} copy(f32[4,8,8,2048]{3,1,2,0:T(8,128)S(1)} %bitcast.188) | data formatting | bytes 4194304
  86.9 7.2 %all-to-all-start.1 = ((f32[32,8,2048]{2,1,0:T(8,128)}), f32[32,8,2048]{2,1,0:T(8,128)S(1)}, u32[]{:S(2)}, u32[]{:S(2)}) async-start(f32[32,8,2048]{2,1,0:T(8,128)} %bitcast.186), calls=%async_computation.1 | async-start | bytes 4194304 | tf_op jit(solution)/shard_map/all_to_all | solution.py:65
  94.9 1.6 copy.67
  97.1 3.1 %broadcast_multiply_fusion = (f32[128,128,1,16]{1,0,3,2:T(8,128)}, f32[128,128]{1,0:T(8,128)}) fusion(f32[128,128]{1,0:T(8,128)} %copy.67, f32[128,16]{0,1:T(8,128)} %param.11, bf16[128,16,64]{0,2,1:T(8,128)(2,1)} %bitcast.197, bf16[128,16,64]{0,2,1:T(8,128)(2,1)S(1)} %bitcast.194, f32[128,128]{1,0:T(8,128)S(1)} %fusion.43, f32[128,16]{0,1:T(8,128)S(1)} %bitcast.202), kind=kOutput, calls=%fused_computation.52 | convolution fusion | flops 35373056 | bytes 1785856 | tf_op jit(solution)/shard_map/ughp,sghp->usgh/dot_general | solution.py:104
  100.3 2.6 %copy.77 = f32[128,128,1,16]{0,3,1,2:T(8,128)} copy(f32[128,128,1,16]{1,0,3,2:T(8,128)} %get-tuple-element.22) | data formatting | bytes 2097152 | tf_op jit(solution)/shard_map/mul | solution.py:113
  102.9 2.3 %fusion.58 = f32[128,128,1,16]{0,3,1,2:T(8,128)} fusion(f32[128,128,1,16]{0,3,1,2:T(8,128)} %copy.77), kind=kOutput, calls=%fused_computation.96 | output fusion | flops 33292288 | bytes 2097152 | tf_op jit(solution)/shard_map/jit(cumsum)/reduce_window_sum | solution.py:114
  105.2 2.6 %copy.78 = f32[128,128,1,16]{1,0,3,2:T(8,128)} copy(f32[128,128,1,16]{0,3,1,2:T(8,128)} %fusion.58) | data formatting | bytes 2097152 | tf_op jit(solution)/shard_map/jit(cumsum)/reduce_window_sum | solution.py:114
  107.8 2.3 %multiply_reduce_fusion = f32[128,16]{0,1:T(8,128)} fusion(f32[128,128,1,16]{1,0,3,2:T(8,128)} %copy.78, f32[128,128,1,16]{1,0,3,2:T(8,128)} %get-tuple-element.22, f32[128,128]{1,0:T(8,128)} %copy-done.8), kind=kLoop, calls=%fused_computation.35 | loop fusion | flops 784384 | bytes 2170880 | tf_op jit(solution)/shard_map/reduce_sum | solution.py:115
  110.1 31.7 %all-to-all-done.1 = f32[32,8,2048]{2,1,0:T(8,128)S(1)} async-done(((f32[32,8,2048]{2,1,0:T(8,128)}), f32[32,8,2048]{2,1,0:T(8,128)S(1)}, u32[]{:S(2)}, u32[]{:S(2)}) %all-to-all-start.1) | async-done | bytes 2097184 | tf_op jit(solution)/shard_map/all_to_all | solution.py:65
  141.7 3.0 %reshape.331 = f32[2,1,16,256,64]{4,3,2,0,1:T(8,128)} reshape(f32[32,8,2048]{2,1,0:T(8,128)S(1)} %all-to-all-done.1) | data formatting | bytes 4194304 | tf_op jit(solution)/shard_map/reshape | solution.py:66
  144.7 2.8 %copy.72 = f32[2,1,16,256,64]{3,4,2,1,0:T(8,128)S(1)} copy(f32[2,1,16,256,64]{4,3,2,0,1:T(8,128)} %reshape.331) | data formatting | bytes 4194304 | tf_op jit(solution)/shard_map/reshape | solution.py:66
  147.5 1.6 multiply_reduce_fusion.1
  149.4 1.7 convolution_bitcast_fusion.8
  155.5 7.8 %all-to-all-start.2 = ((f32[8,1,256]{2,1,0:T(1,128)}), f32[8,1,256]{2,1,0:T(1,128)S(1)}, u32[]{:S(2)}, u32[]{:S(2)}) async-start(f32[8,1,256]{2,1,0:T(1,128)} %reshape.357), calls=%async_computation.2 | async-start | bytes 16384 | tf_op jit(solution)/shard_map/all_to_all | solution.py:212
  165.9 2.0 %all-to-all-done.2 = f32[8,1,256]{2,1,0:T(1,128)S(1)} async-done(((f32[8,1,256]{2,1,0:T(1,128)}), f32[8,1,256]{2,1,0:T(1,128)S(1)}, u32[]{:S(2)}, u32[]{:S(2)}) %all-to-all-start.2) | async-done | bytes 8224 | tf_op jit(solution)/shard_map/all_to_all | solution.py:212
  (71 shorter events, 17.5 us)
Async XLA Ops:
  0.6 6.3 %copy-start = (bf16[128,256]{1,0:T(8,128)(2,1)S(1)}, bf16[128,256]{1,0:T(8,128)(2,1)}, u32[]{:S(2)}) copy-start(bf16[128,256]{1,0:T(8,128)(2,1)} %param.9) | copy-start | bytes 196612
  0.6 5.7 %copy-start.5 = (bf16[128,256]{1,0:T(8,128)(2,1)S(1)}, bf16[128,256]{1,0:T(8,128)(2,1)}, u32[]{:S(2)}) copy-start(bf16[128,256]{1,0:T(8,128)(2,1)} %param.10) | copy-start | bytes 196612
  2.4 3.9 %copy-start.10 = (f32[128,1,16]{2,1,0:T(1,128)}, f32[128,1,16]{2,1,0:T(1,128)S(1)}, u32[]{:S(2)}) copy-start(f32[128,1,16]{2,1,0:T(1,128)S(1)} %fusion.57) | copy-start | bytes 24580
  3.6 3.3 %copy-start.3 = (bf16[128,1024]{0,1:T(8,128)(2,1)}, bf16[128,1024]{0,1:T(8,128)(2,1)S(1)}, u32[]{:S(2)}) copy-start(bf16[128,1024]{0,1:T(8,128)(2,1)S(1)} %copy.69) | copy-start | bytes 786436
  4.8 2.1 %copy-start.1 = (bf16[128,1024]{0,1:T(8,128)(2,1)}, bf16[128,1024]{0,1:T(8,128)(2,1)S(1)}, u32[]{:S(2)}) copy-start(bf16[128,1024]{0,1:T(8,128)(2,1)S(1)} %copy.68) | copy-start | bytes 786436
  10.4 3.6 %copy-start.15 = (s32[32]{0:T(128)S(1)}, s32[32]{0:T(128)}, u32[]{:S(2)}) copy-start(s32[32]{0:T(128)} %constant.28) | copy-start | bytes 388
  16.4 63.0 %all-to-all-start = ((f32[32,8,2176]{2,1,0:T(8,128)}), f32[32,8,2176]{2,1,0:T(8,128)S(1)}, u32[]{:S(2)}, u32[]{:S(2)}) async-start(f32[32,8,2176]{2,1,0:T(8,128)} %pad_maximum_fusion), calls=%async_computation | async-start | bytes 4456448 | tf_op jit(solution)/shard_map/all_to_all | solution.py:52
  86.9 10.2 %copy-start.2 = (bf16[128,1024]{0,1:T(8,128)(2,1)S(1)}, bf16[128,1024]{0,1:T(8,128)(2,1)}, u32[]{:S(2)}) copy-start(bf16[128,1024]{0,1:T(8,128)(2,1)} %copy-done.1) | copy-start | bytes 786436
  86.9 54.8 %all-to-all-start.1 = ((f32[32,8,2048]{2,1,0:T(8,128)}), f32[32,8,2048]{2,1,0:T(8,128)S(1)}, u32[]{:S(2)}, u32[]{:S(2)}) async-start(f32[32,8,2048]{2,1,0:T(8,128)} %bitcast.186), calls=%async_computation.1 | async-start | bytes 4194304 | tf_op jit(solution)/shard_map/all_to_all | solution.py:65
  96.5 0.6 copy-start.8
  149.3 4.1 %copy-start.12 = (f32[128,16]{0,1:T(8,128)S(1)}, f32[128,16]{0,1:T(8,128)}, u32[]{:S(2)}) copy-start(f32[128,16]{0,1:T(8,128)} %multiply_reduce_fusion) | copy-start | bytes 24580
  149.3 4.2 %copy-start.4 = (bf16[128,1024]{0,1:T(8,128)(2,1)S(1)}, bf16[128,1024]{0,1:T(8,128)(2,1)}, u32[]{:S(2)}) copy-start(bf16[128,1024]{0,1:T(8,128)(2,1)} %copy-done.3) | copy-start | bytes 786436
  149.3 4.2 %copy-start.9 = (f32[128,128]{1,0:T(8,128)S(1)}, f32[128,128]{1,0:T(8,128)}, u32[]{:S(2)}) copy-start(f32[128,128]{1,0:T(8,128)} %copy-done.8) | copy-start | bytes 196612
  149.3 4.2 %copy-start.11 = (f32[128,128]{1,0:T(8,128)S(1)}, f32[128,128]{1,0:T(8,128)}, u32[]{:S(2)}) copy-start(f32[128,128]{1,0:T(8,128)} %copy.67) | copy-start | bytes 196612
  149.3 4.2 %copy-start.13 = (f32[128,16]{0,1:T(8,128)S(1)}, f32[128,16]{0,1:T(8,128)}, u32[]{:S(2)}) copy-start(f32[128,16]{0,1:T(8,128)} %param.11) | copy-start | bytes 24580
  149.4 4.2 %copy-start.14 = (f32[128,16]{0,1:T(8,128)S(1)}, f32[128,16]{0,1:T(8,128)}, u32[]{:S(2)}) copy-start(f32[128,16]{0,1:T(8,128)} %get-tuple-element.21) | copy-start | bytes 24580
  152.1 2.5 %copy-start.16 = (f32[16]{0:T(128)S(1)}, f32[16]{0:T(128)}, u32[]{:S(2)}) copy-start(f32[16]{0:T(128)} %param.12) | copy-start | bytes 196
  152.1 11.2 %copy-start.6 = (f32[256,128]{0,1:T(8,128)S(1)}, f32[256,128]{0,1:T(8,128)}, u32[]{:S(2)}) copy-start(f32[256,128]{0,1:T(8,128)} %convolution_bitcast_fusion.8) | copy-start | bytes 393220
  152.1 11.2 %copy-start.7 = (f32[128,128]{1,0:T(8,128)S(1)}, f32[128,128]{1,0:T(8,128)}, u32[]{:S(2)}) copy-start(f32[128,128]{1,0:T(8,128)} %get-tuple-element.23) | copy-start | bytes 196612
  155.5 12.4 %all-to-all-start.2 = ((f32[8,1,256]{2,1,0:T(1,128)}), f32[8,1,256]{2,1,0:T(1,128)S(1)}, u32[]{:S(2)}, u32[]{:S(2)}) async-start(f32[8,1,256]{2,1,0:T(1,128)} %reshape.357), calls=%async_computation.2 | async-start | bytes 16384 | tf_op jit(solution)/shard_map/all_to_all | solution.py:212

commit v5 on v3

--- a/solution.py
+++ b/solution.py
@@ -2,7 +2,7 @@
 import numpy as np
 import jax.numpy as jnp
 from jax import lax
-from jax.sharding import PartitionSpec as P
+from jax.sharding import Mesh, PartitionSpec as P
 
 HEAD_DIM = 64
 D_STATE = 256
@@ -28,40 +28,61 @@
     return lax.fori_loop(0, ahead, one, state)
 
 
-def seq_scan(device_log, device_fwd, device_bwd, axis):
-    count = lax.axis_size(axis)
-    place = lax.axis_index(axis)
+def spread(values, tags, axis):
+    count, per, size = values.shape
+    rows = values.reshape(count, per * 8, size // 8)
+    tag = jnp.broadcast_to(jnp.repeat(tags, 8, axis=1)[..., None], (count, per * 8, 128))
+    got = lax.all_to_all(jnp.concatenate([rows, tag], axis=2), axis, 0, 0, tiled=True)
+    return got[:, :, : size // 8].reshape(count, per, size), got[:, ::8, size // 8]
+
+
+def gather_back(values, axis):
+    count, per, size = values.shape
+    got = lax.all_to_all(values.reshape(count, per * 8, size // 8), axis, 0, 0, tiled=True)
+    return got.reshape(count, per, size)
+
+
+def scan_weights(logs, forward):
+    count = logs.shape[0]
+    position = np.arange(count)
+    low = np.minimum(position[:, None], position[None, :])
+    high = np.maximum(position[:, None], position[None, :])
+    between = (position[None, None, :] > low[..., None]) & (position[None, None, :] < high[..., None])
+    below = (position[None, :] < position[:, None]).astype(np.float32)
+    above = (position[None, :] > position[:, None]).astype(np.float32)
+    inner = jnp.einsum("ijm,mc->cij", between.astype(np.float32), logs, precision=precise)
+    mask = jnp.where(forward[:, None, None], below[None] > 0, above[None] > 0)
+    weights = jnp.where(mask, jnp.exp(inner), 0.0)
+    before = jnp.einsum("im,mc->ci", below, logs, precision=precise)
+    after = jnp.einsum("im,mc->ci", above, logs, precision=precise)
+    total = jnp.exp(jnp.where(forward[:, None], after, before))
+    entry = jnp.exp(jnp.where(forward[:, None], before, after))
+    return weights, total, entry
+
+
+def seq_scan(device_log, device_fwd, device_bwd, outer, inner):
     logs = device_log.reshape(-1)
     heads = logs.shape[0]
     stacked = jnp.stack([device_fwd, device_bwd]).transpose(0, 1, 3, 2, 4)
     shape = stacked.shape
-    combos = 2 * heads
-    if combos % count == 0:
-        per = combos // count
-        targets = np.arange(count)[:, None] * per + np.arange(per)[None, :]
-        held = place * per + jnp.arange(per)
-    else:
-        per = 1
-        targets = (np.arange(count) // (count // combos))[:, None]
-        held = (place // (count // combos))[None]
-    flat = stacked.reshape(count, per, -1)
-    tags = jnp.broadcast_to(logs[targets % heads][..., None], (count, per, 128))
-    payload = jnp.concatenate([flat, tags], axis=2)
-    pieces = lax.all_to_all(payload, axis, 0, 0, tiled=True)
-    chosen = pieces[:, :, flat.shape[2]]
-    pieces = pieces[:, :, : flat.shape[2]]
-    position = jnp.arange(count)
-    low = jnp.minimum(position[:, None], position[None, :])
-    high = jnp.maximum(position[:, None], position[None, :])
-    between = ((position[None, None, :] > low[..., None]) & (position[None, None, :] < high[..., None]))
-    exponent = jnp.einsum("ijm,mc->cij", between.astype(jnp.float32), chosen, precision=precise)
-    before = (position[None, :] < position[:, None])
-    after = (position[None, :] > position[:, None])
-    mask = jnp.where((held < heads)[:, None, None], before[None], after[None])
-    weights = jnp.where(mask, jnp.exp(exponent), 0.0)
-    scanned = jnp.einsum("cij,jcx->icx", weights, pieces, precision=precise)
-    back = lax.all_to_all(scanned, axis, 0, 0, tiled=True)
-    back = back.reshape(shape).transpose(0, 1, 3, 2, 4)
+    members = lax.axis_size(inner)
+    groups = lax.axis_size(outer)
+    per = 2 * heads // members
+    targets = np.arange(members)[:, None] * per + np.arange(per)[None, :]
+    held = lax.axis_index(inner) * per + jnp.arange(per)
+    pieces, member_logs = spread(stacked.reshape(members, per, -1), logs[targets % heads], inner)
+    weights, total, entry = scan_weights(member_logs, held < heads)
+    local = jnp.einsum("cij,jcx->icx", weights, pieces, precision=precise)
+    summary = jnp.einsum("cj,jcx->cx", total, pieces, precision=precise)
+    group_log = jnp.sum(member_logs, axis=0)
+    split = per // groups
+    chunks, group_logs = spread(summary.reshape(groups, split, -1), group_log.reshape(groups, split), outer)
+    mine = held.reshape(groups, split)[lax.axis_index(outer)]
+    group_weights, ignored_total, ignored_entry = scan_weights(group_logs, mine < heads)
+    scanned = jnp.einsum("cij,jcx->icx", group_weights, chunks, precision=precise)
+    incoming = gather_back(scanned, outer).reshape(per, -1)
+    result = local + entry.T[..., None] * incoming[None]
+    back = gather_back(result, inner).reshape(shape).transpose(0, 1, 3, 2, 4)
     return back[0], back[1]
 
 def summarize(inputs, out_grad, input_proj, readout, step_size, decay_rate):
@@ -198,7 +219,7 @@
         (device_log, device_fwd), (log_before, fwd_before) = span_prefix(totals, forward, False)
         (ignored_log, device_bwd), (log_after, bwd_after) = span_prefix(totals, backward, True)
     local = over_spans(lambda e: span_local(*e, rate_rows), blocks)
-    device_in, device_out = seq_scan(device_log, device_fwd, device_bwd, "seq")
+    device_in, device_out = seq_scan(device_log, device_fwd, device_bwd, "z", "x")
     state_ins = fwd_before + jnp.exp(log_before)[:, :, None, :, None] * device_in[None]
     grad_ins = bwd_after + jnp.exp(log_after)[:, :, None, :, None] * device_out[None]
     gradients = over_spans(
@@ -217,13 +238,10 @@
 
 
 def solution(mesh):
-    in_specs = (
-        P("seq", "tp"),
-        P("seq", "tp"),
-        P("seq", "tp"),
-        P("seq", "tp"),
-        P("tp"),
-        P("seq", "tp"),
-    )
-    out_specs = (P("seq", "tp"), P("seq", "tp"), P("seq", "tp"), P(("seq", "tp"), None))
-    return jax.shard_map(body, mesh=mesh, in_specs=in_specs, out_specs=out_specs, check_vma=False)
+    rows = mesh.devices.shape[0]
+    inner = len({device.coords[0] for device in mesh.devices[:, 0]})
+    grid = Mesh(mesh.devices.reshape(rows // inner, inner, -1), ("z", "x", "tp"))
+    seq = ("z", "x")
+    in_specs = (P(seq, "tp"), P(seq, "tp"), P(seq, "tp"), P(seq, "tp"), P("tp"), P(seq, "tp"))
+    out_specs = (P(seq, "tp"), P(seq, "tp"), P(seq, "tp"), P(("z", "x", "tp"), None))
+    return jax.shard_map(body, mesh=grid, in_specs=in_specs, out_specs=out_specs, check_vma=False)

time: 178 us -> 173 us (0.972)
  waiting for transfers between devices: 90.8 us -> 68.2 us
  local copies, waits for them, and re-layouts: 27.9 us -> 37.1 us
  matrix products: 15.4 us -> 22.1 us
  other arithmetic: 15 us -> 12 us
  starting transfers between devices: 27.2 us -> 30.2 us
    all_to_all x2 -> x4, waiting for transfers between devices: 88.8 us -> 66.2 us  [the longest x2 41.2 us: spread(): lax.all_to_all(jnp.concatenate([rows, tag], axis=2), axis, 0, 0, tiled=True)]
    another operation x0 -> x3, local copies, waits for them, and re-layouts: none -> 9.43 us  [the longest x2 5.82 us: seq_scan(): back = gather_back(result, inner).reshape(shape).transpose(0, 1, 3, 2, 4)]
    all_to_all x1 -> x0, other arithmetic: 6.75 us -> none  [seq_scan(): back = lax.all_to_all(scanned, axis, 0, 0, tiled=True)]
    dot_general x2 -> x7, matrix products: 5.17 us -> 10.5 us  [the longest x1 4.73 us: seq_scan(): local = jnp.einsum('cij,jcx->icx', weights, pieces, precision=precise)]
    reshape x3, local copies, waits for them, and re-layouts: 9.01 us -> 4.4 us  [the longest x2 2.66 us: gather_back(): values.reshape(count, per * 8, size // 8)]
    unnamed x50 -> x62, local copies, waits for them, and re-layouts: 4.78 us -> 8.39 us
    concatenate x1 -> x0, local copies, waits for them, and re-layouts: 3.52 us -> none  [seq_scan(): payload = jnp.concatenate([flat, tags], axis=2)]
    transpose x1 -> x0, local copies, waits for them, and re-layouts: 3.46 us -> none  [seq_scan(): scanned = jnp.einsum('cij,jcx->icx', weights, pieces, precision=precise)]
  transfers between devices with their start and end apart: 3 -> 5, of which waited for: 3 -> 5; matrix products, arithmetic and copies ran while one was open for 5% -> 10% of each run, Pallas kernels for 0% -> 0%
where the time goes in v5:
time: 173 us; the launch traced here: 172 us
  waiting for transfers between devices  68.2 us (39%)
  local copies, waits for them, and re-layouts  37.1 us (21%)
  starting transfers between devices  30.2 us (17%)
  matrix products  22.1 us (13%)
  other arithmetic  12 us (7%)
  between operations  1.78 us (1%)
    all_to_all x2, waiting for transfers between devices, spread(): lax.all_to_all(jnp.concatenate([rows, tag], axis=2), axis, 0, 0, tiled=True)  41.2 us
    all_to_all x2, waiting for transfers between devices, gather_back(): lax.all_to_all(values.reshape(count, per * 8, size // 8), axis, 0, 0, til...  25 us
    all_to_all x2, starting transfers between devices, spread(): lax.all_to_all(jnp.concatenate([rows, tag], axis=2), axis, 0, 0, tiled=True)  14.1 us
    unnamed x62, local copies, waits for them, and re-layouts  8.39 us
    all_to_all x2, starting transfers between devices, gather_back(): lax.all_to_all(values.reshape(count, per * 8, size // 8), axis, 0, 0, til...  8.06 us
    all_to_all x1, starting transfers between devices, body(): lax.all_to_all(grad_step, 'tp', split_axis=0, concat_axis=1, tiled=True)  8 us
    another operation x2, local copies, waits for them, and re-layouts, seq_scan(): back = gather_back(result, inner).reshape(shape).transpose(0, 1, 3, 2, 4)  5.82 us
    dot_general x1, matrix products, seq_scan(): local = jnp.einsum('cij,jcx->icx', weights, pieces, precision=precise)  4.73 us
  transfers between devices with their start and end apart: 5, of which 5 were waited for; matrix products, arithmetic and copies ran while one was open for 10% of the time, Pallas kernels for 0%

profile of v5, /device:TPU:1, one launch (start us, length us, event | category | flops | bytes accessed | tf_op | source)
XLA Modules:
  0.0 171.5 jit_solution(1765436773486337185)
XLA Ops:
  8.3 2.7 %copy.109 = f32[2,1,16,256,64]{4,3,2,0,1:T(8,128)} copy(f32[2,1,16,256,64]{3,4,2,1,0:T(8,128)S(1)} %maximum_bitcast_fusion) | data formatting | bytes 4194304 | tf_op jit(solution)/shard_map/transpose | solution.py:66
  11.0 3.6 %reshape_reshape.9 = f32[4,64,2048]{2,1,0:T(8,128)S(1)} reshape(f32[2,1,16,256,64]{4,3,2,0,1:T(8,128)} %copy.109) | data formatting | bytes 4194304 | tf_op jit(solution)/shard_map/reshape;reshape | solution.py:33
  15.7 1.6 pad_maximum_fusion
  17.3 5.0 %all-to-all-start = ((f32[4,64,2176]{2,1,0:T(8,128)}), f32[4,64,2176]{2,1,0:T(8,128)S(1)}, u32[]{:S(2)}, u32[]{:S(2)}) async-start(f32[4,64,2176]{2,1,0:T(8,128)} %pad_maximum_fusion), calls=%async_computation | async-start | bytes 4456448 | tf_op jit(solution)/shard_map/all_to_all | solution.py:35
  22.2 25.9 %all-to-all-done = f32[4,64,2176]{2,1,0:T(8,128)S(1)} async-done(((f32[4,64,2176]{2,1,0:T(8,128)}), f32[4,64,2176]{2,1,0:T(8,128)S(1)}, u32[]{:S(2)}, u32[]{:S(2)}) %all-to-all-start) | async-done | bytes 2228256 | tf_op jit(solution)/shard_map/all_to_all | solution.py:35
  48.6 1.6 slice.33
  50.3 1.7 %reshape.315 = f32[4,8,16384]{2,1,0:T(8,128)S(1)} reshape(f32[4,64,2048]{2,1,0:T(8,128)} %slice.33) | data formatting | bytes 4194304 | tf_op jit(solution)/shard_map/reshape | solution.py:36
  52.0 4.3 %fusion.1 = f32[8,1,16384]{2,1,0:T(1,128)S(1)} fusion(f32[8,4,1]{1,2,0:T(1,128)S(1)} %copy.125, f32[4,8,16384]{2,1,0:T(8,128)S(1)} %reshape.315), kind=kOutput, calls=%fused_computation.5 | convolution fusion | flops 6291456 | bytes 2621568 | tf_op jit(solution)/shard_map/cj,jcx->cx/dot_general | solution.py:76
  57.9 9.2 %all-to-all-start.1 = ((f32[8,8,2176]{2,1,0:T(8,128)}), f32[8,8,2176]{2,1,0:T(8,128)}, u32[]{:S(2)}, u32[]{:S(2)}) async-start(f32[8,8,2176]{2,1,0:T(8,128)} %pad_maximum_fusion.1), calls=%async_computation.1 | async-start | bytes 1114112 | tf_op jit(solution)/shard_map/all_to_all | solution.py:35
  68.3 15.3 %all-to-all-done.1 = f32[8,8,2176]{2,1,0:T(8,128)} async-done(((f32[8,8,2176]{2,1,0:T(8,128)}), f32[8,8,2176]{2,1,0:T(8,128)}, u32[]{:S(2)}, u32[]{:S(2)}) %all-to-all-start.1) | async-done | bytes 557088 | tf_op jit(solution)/shard_map/all_to_all | solution.py:35
  88.2 4.3 %all-to-all-start.2 = ((f32[8,8,2048]{2,1,0:T(8,128)}), f32[8,8,2048]{2,1,0:T(8,128)}, u32[]{:S(2)}, u32[]{:S(2)}) async-start(f32[8,8,2048]{2,1,0:T(8,128)} %copy.113), calls=%async_computation.2 | async-start | bytes 1048576 | tf_op jit(solution)/shard_map/all_to_all | solution.py:41
  92.9 14.5 %all-to-all-done.2 = f32[8,8,2048]{2,1,0:T(8,128)} async-done(((f32[8,8,2048]{2,1,0:T(8,128)}), f32[8,8,2048]{2,1,0:T(8,128)}, u32[]{:S(2)}, u32[]{:S(2)}) %all-to-all-start.2) | async-done | bytes 524320 | tf_op jit(solution)/shard_map/all_to_all | solution.py:41
  108.8 4.7 %fusion = f32[4,8,16384]{2,0,1:T(4,128)S(1)} fusion(f32[8,4,4]{2,1,0:T(4,128)S(1)} %copy.111, f32[4,8,16384]{2,1,0:T(8,128)S(1)} %reshape.315, f32[8,16384]{1,0:T(8,128)S(1)} %bitcast.233, f32[4,8]{0,1:T(8,128)S(1)} %copy.112), kind=kOutput, calls=%fused_computation.2 | convolution fusion | flops 26214400 | bytes 4719232 | tf_op jit(solution)/shard_map/cij,jcx->icx/dot_general | solution.py:75
  116.3 3.7 %all-to-all-start.3 = ((f32[4,64,2048]{2,1,0:T(8,128)}), f32[4,64,2048]{2,1,0:T(8,128)S(1)}, u32[]{:S(2)}, u32[]{:S(2)}) async-start(f32[4,64,2048]{2,1,0:T(8,128)} %reshape.320), calls=%async_computation.3 | async-start | bytes 4194304 | tf_op jit(solution)/shard_map/all_to_all | solution.py:41
  120.4 3.2 %broadcast_multiply_fusion = (f32[128,128,1,16]{1,0,3,2:T(8,128)}, f32[128,128]{1,0:T(8,128)}) fusion(f32[128,128]{1,0:T(8,128)S(1)} %copy.105, f32[128,16]{0,1:T(8,128)S(1)} %copy-done.14, bf16[128,16,64]{0,2,1:T(8,128)(2,1)} %bitcast.227, bf16[128,16,64]{0,2,1:T(8,128)(2,1)} %bitcast.224, f32[128,128]{1,0:T(8,128)S(1)} %fusion.43, f32[128,16]{0,1:T(8,128)S(1)} %bitcast.237), kind=kOutput, calls=%fused_computation.60 | convolution fusion | flops 35373056 | bytes 1785856 | tf_op jit(solution)/shard_map/ughp,sghp->usgh/dot_general | solution.py:123
  123.6 2.6 %copy.120 = f32[128,128,1,16]{0,3,1,2:T(8,128)} copy(f32[128,128,1,16]{1,0,3,2:T(8,128)} %get-tuple-element.28) | data formatting | bytes 2097152 | tf_op jit(solution)/shard_map/mul | solution.py:132
  126.2 2.3 %fusion.60 = f32[128,128,1,16]{0,3,1,2:T(8,128)} fusion(f32[128,128,1,16]{0,3,1,2:T(8,128)} %copy.120), kind=kOutput, calls=%fused_computation.104 | output fusion | flops 33292288 | bytes 2097152 | tf_op jit(solution)/shard_map/jit(cumsum)/reduce_window_sum | solution.py:133
  128.5 2.6 %copy.121 = f32[128,128,1,16]{1,0,3,2:T(8,128)} copy(f32[128,128,1,16]{0,3,1,2:T(8,128)} %fusion.60) | data formatting | bytes 2097152 | tf_op jit(solution)/shard_map/jit(cumsum)/reduce_window_sum | solution.py:133
  131.1 2.3 %multiply_reduce_fusion = f32[128,16]{0,1:T(8,128)} fusion(f32[128,128,1,16]{1,0,3,2:T(8,128)} %copy.121, f32[128,128,1,16]{1,0,3,2:T(8,128)} %get-tuple-element.28, f32[128,128]{1,0:T(8,128)S(1)} %fusion.43), kind=kLoop, calls=%fused_computation.42 | loop fusion | flops 784384 | bytes 2170880 | tf_op jit(solution)/shard_map/reduce_sum | solution.py:134
  133.3 10.4 %all-to-all-done.3 = f32[4,64,2048]{2,1,0:T(8,128)S(1)} async-done(((f32[4,64,2048]{2,1,0:T(8,128)}), f32[4,64,2048]{2,1,0:T(8,128)S(1)}, u32[]{:S(2)}, u32[]{:S(2)}) %all-to-all-start.3) | async-done | bytes 2097184 | tf_op jit(solution)/shard_map/all_to_all | solution.py:41
  143.8 3.0 %reshape_reshape.11 = f32[2,1,16,256,64]{4,3,2,0,1:T(8,128)} reshape(f32[4,64,2048]{2,1,0:T(8,128)S(1)} %all-to-all-done.3) | data formatting | bytes 4194304 | tf_op jit(solution)/shard_map/reshape;reshape | solution.py:85
  146.8 2.8 %copy.115 = f32[2,1,16,256,64]{3,4,2,1,0:T(8,128)S(1)} copy(f32[2,1,16,256,64]{4,3,2,0,1:T(8,128)} %reshape_reshape.11) | data formatting | bytes 4194304 | tf_op jit(solution)/shard_map/reshape;reshape | solution.py:85
  156.9 8.0 %all-to-all-start.4 = ((f32[8,1,256]{2,1,0:T(1,128)}), f32[8,1,256]{2,1,0:T(1,128)S(1)}, u32[]{:S(2)}, u32[]{:S(2)}) async-start(f32[8,1,256]{2,1,0:T(1,128)} %reshape.352), calls=%async_computation.4 | async-start | bytes 16384 | tf_op jit(solution)/shard_map/all_to_all | solution.py:231
  167.5 2.0 %all-to-all-done.4 = f32[8,1,256]{2,1,0:T(1,128)S(1)} async-done(((f32[8,1,256]{2,1,0:T(1,128)}), f32[8,1,256]{2,1,0:T(1,128)S(1)}, u32[]{:S(2)}, u32[]{:S(2)}) %all-to-all-start.4) | async-done | bytes 8224 | tf_op jit(solution)/shard_map/all_to_all | solution.py:231
  (117 shorter events, 32.2 us)
Async XLA Ops:
  0.6 6.8 %copy-start = (bf16[128,256]{1,0:T(8,128)(2,1)S(1)}, bf16[128,256]{1,0:T(8,128)(2,1)}, u32[]{:S(2)}) copy-start(bf16[128,256]{1,0:T(8,128)(2,1)} %param.17) | copy-start | bytes 196612
  0.6 6.2 %copy-start.5 = (bf16[128,256]{1,0:T(8,128)(2,1)S(1)}, bf16[128,256]{1,0:T(8,128)(2,1)}, u32[]{:S(2)}) copy-start(bf16[128,256]{1,0:T(8,128)(2,1)} %param.18) | copy-start | bytes 196612
  11.0 3.6 %copy-start.21 = (s32[32]{0:T(128)S(1)}, s32[32]{0:T(128)}, u32[]{:S(2)}) copy-start(s32[32]{0:T(128)} %constant.63) | copy-start | bytes 388
  17.3 31.0 %copy-start.17 = (f32[4,4]{1,0:T(4,128)S(1)}, f32[4,4]{1,0:T(4,128)}, u32[]{:S(2)}) copy-start(f32[4,4]{1,0:T(4,128)} %constant.55.clone) | copy-start | bytes 196
  17.3 31.1 %copy-start.18 = (f32[4,4]{1,0:T(4,128)S(1)}, f32[4,4]{1,0:T(4,128)}, u32[]{:S(2)}) copy-start(f32[4,4]{1,0:T(4,128)} %constant.56.clone) | copy-start | bytes 196
  17.3 30.8 %all-to-all-start = ((f32[4,64,2176]{2,1,0:T(8,128)}), f32[4,64,2176]{2,1,0:T(8,128)S(1)}, u32[]{:S(2)}, u32[]{:S(2)}) async-start(f32[4,64,2176]{2,1,0:T(8,128)} %pad_maximum_fusion), calls=%async_computation | async-start | bytes 4456448 | tf_op jit(solution)/shard_map/all_to_all | solution.py:35
  57.0 29.0 %copy-start.13 = (f32[8,8,8]{2,1,0:T(8,128)S(1)}, f32[8,8,8]{2,1,0:T(8,128)}, u32[]{:S(2)}) copy-start(f32[8,8,8]{2,1,0:T(8,128)} %constant.57.clone) | copy-start | bytes 6148
  57.0 29.5 %copy-start.19 = (pred[1,8,8]{2,1,0:T(8,128)(4,1)S(1)}, pred[1,8,8]{2,1,0:T(8,128)(4,1)}, u32[]{:S(2)}) copy-start(pred[1,8,8]{2,1,0:T(8,128)(4,1)} %constant.58.clone) | copy-start | bytes 196
  57.0 29.5 %copy-start.20 = (pred[1,8,8]{2,1,0:T(8,128)(4,1)S(1)}, pred[1,8,8]{2,1,0:T(8,128)(4,1)}, u32[]{:S(2)}) copy-start(pred[1,8,8]{2,1,0:T(8,128)(4,1)} %constant.59.clone) | copy-start | bytes 196
  57.9 25.8 %all-to-all-start.1 = ((f32[8,8,2176]{2,1,0:T(8,128)}), f32[8,8,2176]{2,1,0:T(8,128)}, u32[]{:S(2)}, u32[]{:S(2)}) async-start(f32[8,8,2176]{2,1,0:T(8,128)} %pad_maximum_fusion.1), calls=%async_computation.1 | async-start | bytes 1114112 | tf_op jit(solution)/shard_map/all_to_all | solution.py:35
  84.7 7.9 %copy-start.23 = (f32[4,4,4]{2,1,0:T(4,128)S(1)}, f32[4,4,4]{2,1,0:T(4,128)}, u32[]{:S(2)}) copy-start(f32[4,4,4]{2,1,0:T(4,128)} %constant.52.clone) | copy-start | bytes 772
  84.7 7.9 %copy-start.24 = (pred[4,4]{1,0:T(4,128)(4,1)S(1)}, pred[4,4]{1,0:T(4,128)(4,1)}, u32[]{:S(2)}) copy-start(pred[4,4]{1,0:T(4,128)(4,1)} %constant.61) | copy-start | bytes 52
  84.7 7.9 %copy-start.25 = (pred[4,4]{1,0:T(4,128)(4,1)S(1)}, pred[4,4]{1,0:T(4,128)(4,1)}, u32[]{:S(2)}) copy-start(pred[4,4]{1,0:T(4,128)(4,1)} %constant.62) | copy-start | bytes 52
  88.2 19.2 %all-to-all-start.2 = ((f32[8,8,2048]{2,1,0:T(8,128)}), f32[8,8,2048]{2,1,0:T(8,128)}, u32[]{:S(2)}, u32[]{:S(2)}) async-start(f32[8,8,2048]{2,1,0:T(8,128)} %copy.113), calls=%async_computation.2 | async-start | bytes 1048576 | tf_op jit(solution)/shard_map/all_to_all | solution.py:41
  116.3 4.1 %copy-start.14 = (f32[128,16]{0,1:T(8,128)S(1)}, f32[128,16]{0,1:T(8,128)}, u32[]{:S(2)}) copy-start(f32[128,16]{0,1:T(8,128)} %param.19) | copy-start | bytes 24580
  116.3 27.5 %all-to-all-start.3 = ((f32[4,64,2048]{2,1,0:T(8,128)}), f32[4,64,2048]{2,1,0:T(8,128)S(1)}, u32[]{:S(2)}, u32[]{:S(2)}) async-start(f32[4,64,2048]{2,1,0:T(8,128)} %reshape.320), calls=%async_computation.3 | async-start | bytes 4194304 | tf_op jit(solution)/shard_map/all_to_all | solution.py:41
  120.3 5.9 %copy-start.10 = (f32[128,128]{1,0:T(8,128)}, f32[128,128]{1,0:T(8,128)S(1)}, u32[]{:S(2)}) copy-start(f32[128,128]{1,0:T(8,128)S(1)} %copy.105) | copy-start | bytes 196612
  120.3 10.7 %copy-start.7 = (f32[128,128]{1,0:T(8,128)}, f32[128,128]{1,0:T(8,128)S(1)}, u32[]{:S(2)}) copy-start(f32[128,128]{1,0:T(8,128)S(1)} %fusion.43) | copy-start | bytes 196612
  151.4 3.6 %copy-start.8 = (f32[128,128]{1,0:T(8,128)S(1)}, f32[128,128]{1,0:T(8,128)}, u32[]{:S(2)}) copy-start(f32[128,128]{1,0:T(8,128)} %copy-done.7) | copy-start | bytes 196612
  151.4 3.6 %copy-start.11 = (f32[128,128]{1,0:T(8,128)S(1)}, f32[128,128]{1,0:T(8,128)}, u32[]{:S(2)}) copy-start(f32[128,128]{1,0:T(8,128)} %copy-done.10) | copy-start | bytes 196612
  151.4 3.6 %copy-start.15 = (f32[128,16]{0,1:T(8,128)S(1)}, f32[128,16]{0,1:T(8,128)}, u32[]{:S(2)}) copy-start(f32[128,16]{0,1:T(8,128)} %param.19) | copy-start | bytes 24580
  151.4 3.6 %copy-start.16 = (f32[128,16]{0,1:T(8,128)S(1)}, f32[128,16]{0,1:T(8,128)}, u32[]{:S(2)}) copy-start(f32[128,16]{0,1:T(8,128)} %get-tuple-element.27) | copy-start | bytes 24580
  153.5 11.4 %copy-start.6 = (f32[128,128]{1,0:T(8,128)S(1)}, f32[128,128]{1,0:T(8,128)}, u32[]{:S(2)}) copy-start(f32[128,128]{1,0:T(8,128)} %get-tuple-element.29) | copy-start | bytes 196612
  156.9 12.6 %all-to-all-start.4 = ((f32[8,1,256]{2,1,0:T(1,128)}), f32[8,1,256]{2,1,0:T(1,128)S(1)}, u32[]{:S(2)}, u32[]{:S(2)}) async-start(f32[8,1,256]{2,1,0:T(1,128)} %reshape.352), calls=%async_computation.4 | async-start | bytes 16384 | tf_op jit(solution)/shard_map/all_to_all | solution.py:231
  (7 other events, 17.7 us)

commit v6 on v4

--- a/solution.py
+++ b/solution.py
@@ -31,39 +31,34 @@
 def seq_scan(device_log, device_fwd, device_bwd, axis):
     count = lax.axis_size(axis)
     place = lax.axis_index(axis)
-    logs = device_log.reshape(-1)
-    heads = logs.shape[0]
-    stacked = jnp.stack([device_fwd, device_bwd]).transpose(0, 1, 3, 2, 4)
+    group_count, state_dim, heads, head_dim = device_fwd.shape
+    stacked = jnp.stack([device_fwd, device_bwd])
     shape = stacked.shape
-    combos = 2 * heads
-    if combos % count == 0:
-        per = combos // count
-        targets = np.arange(count)[:, None] * per + np.arange(per)[None, :]
-        held = place * per + jnp.arange(per)
-    else:
-        per = 1
-        targets = (np.arange(count) // (count // combos))[:, None]
-        held = (place // (count // combos))[None]
-    flat = stacked.reshape(count, per * 8, -1)
+    rows = 2 * group_count * state_dim // count
+    block = (place * rows) // state_dim
+    forward = block < group_count
+    group = block % group_count
+    flat = stacked.reshape(count, rows, heads * head_dim)
     width = flat.shape[2]
-    tags = jnp.repeat(logs[targets % heads], 8, axis=1)
-    tags = jnp.broadcast_to(tags[..., None], (count, per * 8, 128))
+    owner = (np.arange(count) * rows // state_dim) % group_count
+    tags = jnp.pad(device_log[owner], ((0, 0), (0, 128 - heads)))
+    tags = jnp.broadcast_to(tags[:, None, :], (count, rows, 128))
     payload = jnp.concatenate([flat, tags], axis=2)
     pieces = lax.all_to_all(payload, axis, 0, 0, tiled=True)
-    chosen = pieces[:, ::8, width]
-    pieces = pieces[:, :, :width].reshape(count, per, -1)
+    chosen = pieces[:, 0, width : width + heads]
+    pieces = pieces[:, :, :width].reshape(count, rows, heads, head_dim)
     position = jnp.arange(count)
     low = jnp.minimum(position[:, None], position[None, :])
     high = jnp.maximum(position[:, None], position[None, :])
     between = ((position[None, None, :] > low[..., None]) & (position[None, None, :] < high[..., None]))
-    exponent = jnp.einsum("ijm,mc->cij", between.astype(jnp.float32), chosen, precision=precise)
+    exponent = jnp.einsum("ijm,mh->hij", between.astype(jnp.float32), chosen, precision=precise)
     before = (position[None, :] < position[:, None])
     after = (position[None, :] > position[:, None])
-    mask = jnp.where((held < heads)[:, None, None], before[None], after[None])
-    weights = jnp.where(mask, jnp.exp(exponent), 0.0)
-    scanned = jnp.einsum("cij,jcx->icx", weights, pieces, precision=precise)
-    back = lax.all_to_all(scanned.reshape(count, per * 8, -1), axis, 0, 0, tiled=True)
-    back = back.reshape(shape).transpose(0, 1, 3, 2, 4)
+    mask = jnp.where(forward, before, after)
+    weights = jnp.where(mask[None], jnp.exp(exponent), 0.0)
+    scanned = jnp.einsum("hij,jrhp->irhp", weights, pieces, precision=precise)
+    back = lax.all_to_all(scanned.reshape(count, rows, width), axis, 0, 0, tiled=True)
+    back = back.reshape(shape)
     return back[0], back[1]
 
 def summarize(inputs, out_grad, input_proj, readout, step_size, decay_rate):

time: 171 us -> 199 us (1.16)
  local copies, waits for them, and re-layouts: 30.2 us -> 43.2 us
  waiting for transfers between devices: 84.8 us -> 92.2 us
  matrix products: 16 us -> 22.1 us
  other arithmetic: 11.1 us -> 13.1 us
    another operation x0 -> x5, local copies, waits for them, and re-layouts: none -> 11.8 us
    dot_general x2, matrix products: 3.11 us -> 10 us  [the longest x1 8.47 us: seq_scan(): scanned = jnp.einsum('hij,jrhp->irhp', weights, pieces, precision=precise)]
    all_to_all x1, waiting for transfers between devices: 31.7 us -> 36.3 us  [seq_scan(): lax.all_to_all(scanned.reshape(count, rows, width), axis, 0, 0, tiled=True)]
    unnamed x42, local copies, waits for them, and re-layouts: 9.17 us -> 5.73 us
    reshape x3, local copies, waits for them, and re-layouts: 9.41 us -> 12.9 us  [the longest x1 4.86 us: seq_scan(): scanned.reshape(count, rows, width)]
    all_to_all x1, waiting for transfers between devices: 51.1 us -> 53.9 us  [seq_scan(): pieces = lax.all_to_all(payload, axis, 0, 0, tiled=True)]
    dot_general x1, other arithmetic: 0.22 us -> 2.57 us  [span_state(): jnp.einsum('gnhp,gnhp->gh', grad_in, state_in, precision=precise)]
    slice x2 -> x3, local copies, waits for them, and re-layouts: 0.57 us -> 2.77 us  [the longest x1 1.6 us: seq_scan(): pieces = pieces[:, :, :width].reshape(count, rows, heads, head_dim)]
  transfers between devices with their start and end apart: 3 -> 3, of which waited for: 3 -> 3; matrix products, arithmetic and copies ran while one was open for 11% -> 7% of each run, Pallas kernels for 0% -> 0%
where the time goes in v6:
time: 199 us; the launch traced here: 198 us
  waiting for transfers between devices  92.2 us (46%)
  local copies, waits for them, and re-layouts  43.2 us (22%)
  starting transfers between devices  26.1 us (13%)
  matrix products  22.1 us (11%)
  other arithmetic  13.1 us (7%)
    all_to_all x1, waiting for transfers between devices, seq_scan(): pieces = lax.all_to_all(payload, axis, 0, 0, tiled=True)  53.9 us
    all_to_all x1, waiting for transfers between devices, seq_scan(): lax.all_to_all(scanned.reshape(count, rows, width), axis, 0, 0, tiled=True)  36.3 us
    all_to_all x1, starting transfers between devices, seq_scan(): pieces = lax.all_to_all(payload, axis, 0, 0, tiled=True)  12 us
    dot_general x1, matrix products, seq_scan(): scanned = jnp.einsum('hij,jrhp->irhp', weights, pieces, precision=precise)  8.47 us
    another operation x4, local copies, waits for them, and re-layouts  8.07 us
    all_to_all x1, starting transfers between devices, body(): lax.all_to_all(grad_step, 'tp', split_axis=0, concat_axis=1, tiled=True)  7.11 us
    all_to_all x1, starting transfers between devices, seq_scan(): lax.all_to_all(scanned.reshape(count, rows, width), axis, 0, 0, tiled=True)  6.96 us
    unnamed x42, local copies, waits for them, and re-layouts  5.73 us
  transfers between devices with their start and end apart: 3, of which 3 were waited for; matrix products, arithmetic and copies ran while one was open for 7% of the time, Pallas kernels for 0%

profile of v6, /device:TPU:1, one launch (start us, length us, event | category | flops | bytes accessed | tf_op | source)
XLA Modules:
  0.0 197.7 jit_solution(5795166373495768620)
XLA Ops:
  8.0 3.8 %copy.85 = f32[2,1,256,16,64]{4,3,2,0,1:T(8,128)} copy(f32[2,1,256,16,64]{2,4,3,1,0:T(8,128)S(1)} %pad_maximum_fusion.1) | data formatting | bytes 4194304 | tf_op jit(solution)/shard_map/stack | solution.py:35
  11.8 3.5 %reshape.335 = f32[32,16,1024]{2,1,0:T(8,128)S(1)} reshape(f32[2,1,256,16,64]{4,3,2,0,1:T(8,128)} %copy.85) | data formatting | bytes 4194304 | tf_op jit(solution)/shard_map/reshape | solution.py:41
  15.3 1.7 pad_maximum_fusion
  16.9 12.0 %all-to-all-start = ((f32[32,16,1152]{2,1,0:T(8,128)}), f32[32,16,1152]{2,1,0:T(8,128)S(1)}, u32[]{:S(2)}, u32[]{:S(2)}) async-start(f32[32,16,1152]{2,1,0:T(8,128)} %pad_maximum_fusion), calls=%async_computation | async-start | bytes 4718592 | tf_op jit(solution)/shard_map/all_to_all | solution.py:47
  29.0 53.9 %all-to-all-done = f32[32,16,1152]{2,1,0:T(8,128)S(1)} async-done(((f32[32,16,1152]{2,1,0:T(8,128)}), f32[32,16,1152]{2,1,0:T(8,128)S(1)}, u32[]{:S(2)}, u32[]{:S(2)}) %all-to-all-start) | async-done | bytes 2359328 | tf_op jit(solution)/shard_map/all_to_all | solution.py:47
  84.5 4.5 %reshape.336 = f32[32,16,16,64]{3,2,1,0:T(8,128)} reshape(f32[32,16,1024]{2,1,0:T(8,128)} %slice.24) | data formatting | bytes 4194304 | tf_op jit(solution)/shard_map/reshape | solution.py:49
  90.6 8.5 %fusion.2 = f32[32,16,16,64]{3,0,1,2:T(8,128)S(1)} fusion(f32[32,16,16,64]{3,2,1,0:T(8,128)} %reshape.336, f32[16,32,32,1]{2,0,1,3:T(8,128)S(1)} %fusion.10), kind=kOutput, calls=%fused_computation.3 | convolution fusion | flops 201326592 | bytes 4259840 | tf_op jit(solution)/shard_map/hij,jrhp->irhp/dot_general | solution.py:59
  99.1 4.4 %copy.89 = f32[32,16,16,64]{3,2,1,0:T(8,128)} copy(f32[32,16,16,64]{3,0,1,2:T(8,128)S(1)} %fusion.2) | data formatting | bytes 4194304 | tf_op jit(solution)/shard_map/hij,jrhp->irhp/transpose | solution.py:59
  103.4 4.9 %reshape.337 = f32[32,16,1024]{2,1,0:T(8,128)} reshape(f32[32,16,16,64]{3,2,1,0:T(8,128)} %copy.89) | data formatting | bytes 4194304 | tf_op jit(solution)/shard_map/reshape | solution.py:60
  108.3 7.0 %all-to-all-start.1 = ((f32[32,16,1024]{2,1,0:T(8,128)}), f32[32,16,1024]{2,1,0:T(8,128)S(1)}, u32[]{:S(2)}, u32[]{:S(2)}) async-start(f32[32,16,1024]{2,1,0:T(8,128)} %reshape.337), calls=%async_computation.1 | async-start | bytes 4194304 | tf_op jit(solution)/shard_map/all_to_all | solution.py:60
  116.8 2.2 %broadcast_multiply_fusion = (f32[128,128,1,16]{1,0,3,2:T(8,128)S(1)}, f32[128,128]{1,0:T(8,128)}) fusion(f32[128,128]{1,0:T(8,128)} %copy.81, f32[128,16]{0,1:T(8,128)} %param.11, bf16[128,16,64]{0,2,1:T(8,128)(2,1)} %bitcast.168, bf16[128,16,64]{0,2,1:T(8,128)(2,1)S(1)} %bitcast.165, f32[128,128]{1,0:T(8,128)S(1)} %fusion.41, f32[128,16]{0,1:T(8,128)S(1)} %bitcast.173), kind=kOutput, calls=%fused_computation.48 | convolution fusion | flops 35373056 | bytes 1785856 | tf_op jit(solution)/shard_map/ughp,sghp->usgh/dot_general | solution.py:99
  120.4 2.3 %fusion.49 = f32[128,128,1,16]{0,3,1,2:T(8,128)} fusion(f32[128,128,1,16]{0,3,1,2:T(8,128)} %copy.97), kind=kOutput, calls=%fused_computation.86 | output fusion | flops 33292288 | bytes 2097152 | tf_op jit(solution)/shard_map/jit(cumsum)/reduce_window_sum | solution.py:109
  122.7 2.6 %copy.98 = f32[128,128,1,16]{1,0,3,2:T(8,128)} copy(f32[128,128,1,16]{0,3,1,2:T(8,128)} %fusion.49) | data formatting | bytes 2097152 | tf_op jit(solution)/shard_map/jit(cumsum)/reduce_window_sum | solution.py:109
  125.3 1.9 multiply_reduce_fusion.1
  127.3 36.3 %all-to-all-done.1 = f32[32,16,1024]{2,1,0:T(8,128)S(1)} async-done(((f32[32,16,1024]{2,1,0:T(8,128)}), f32[32,16,1024]{2,1,0:T(8,128)S(1)}, u32[]{:S(2)}, u32[]{:S(2)}) %all-to-all-start.1) | async-done | bytes 2097184 | tf_op jit(solution)/shard_map/all_to_all | solution.py:60
  164.7 1.7 reshape.338
  166.4 1.9 reshape.340
  168.3 2.5 %copy.94 = f32[256,16,64]{0,2,1:T(8,128)S(1)} copy(f32[256,16,64]{2,1,0:T(8,128)} %reshape.340) | data formatting | bytes 2097152 | tf_op jit(solution)/shard_map/reshape.53
  170.8 2.6 %multiply_reduce_fusion = f32[16]{0:T(128)} fusion(f32[256,16,64]{2,1,0:T(8,128)} %reshape.340, f32[256,16,64]{2,1,0:T(8,128)S(1)} %reshape.338), kind=kLoop, calls=%fused_computation.5 | loop fusion | flops 524272 | bytes 2097216 | tf_op jit(solution)/shard_map/gnhp,gnhp->gh/dot_general | solution.py:144
  173.3 2.0 %copy.90 = f32[256,16,64]{0,2,1:T(8,128)} copy(f32[256,16,64]{2,1,0:T(8,128)S(1)} %reshape.338) | data formatting | bytes 2097152 | tf_op jit(solution)/shard_map/reshape.35
  175.3 2.0 %multiply_reduce_fusion.2 = (f32[128,16]{0,1:T(8,128)S(1)}, f32[128,16,64]{0,2,1:T(8,128)S(1)}) fusion(bf16[128,1024]{0,1:T(8,128)(2,1)} %copy-done.5, f32[256,16,64]{0,2,1:T(8,128)} %copy.90, bf16[128,256]{1,0:T(8,128)(2,1)S(1)} %copy-done), kind=kOutput, calls=%fused_computation.49 | convolution fusion | flops 403044352 | bytes 1908736 | tf_op jit(solution)/shard_map/gnhp,sgn->sghp/dot_general | solution.py:130
  177.4 2.1 %convolution_bitcast_fusion.9 = f32[256,128]{0,1:T(8,128)S(1)} fusion(f32[256,16,64]{0,2,1:T(8,128)S(1)} %copy-done.1, f32[128,16,64]{0,2,1:T(8,128)} %bitcast.164), kind=kOutput, calls=%fused_computation.24 | convolution fusion | flops 402653184 | bytes 1703936 | tf_op jit(solution)/shard_map/sghp,gnhp->sgn/dot_general | solution.py:136
  184.0 7.1 %all-to-all-start.2 = ((f32[8,1,256]{2,1,0:T(1,128)}), f32[8,1,256]{2,1,0:T(1,128)S(1)}, u32[]{:S(2)}, u32[]{:S(2)}) async-start(f32[8,1,256]{2,1,0:T(1,128)} %reshape.355), calls=%async_computation.2 | async-start | bytes 16384 | tf_op jit(solution)/shard_map/all_to_all | solution.py:207
  193.7 2.0 %all-to-all-done.2 = f32[8,1,256]{2,1,0:T(1,128)S(1)} async-done(((f32[8,1,256]{2,1,0:T(1,128)}), f32[8,1,256]{2,1,0:T(1,128)S(1)}, u32[]{:S(2)}, u32[]{:S(2)}) %all-to-all-start.2) | async-done | bytes 8224 | tf_op jit(solution)/shard_map/all_to_all | solution.py:207
  (76 shorter events, 23.5 us)
Async XLA Ops:
  0.6 6.6 %copy-start = (bf16[128,256]{1,0:T(8,128)(2,1)S(1)}, bf16[128,256]{1,0:T(8,128)(2,1)}, u32[]{:S(2)}) copy-start(bf16[128,256]{1,0:T(8,128)(2,1)} %param.9) | copy-start | bytes 196612
  0.6 5.6 %copy-start.7 = (bf16[128,256]{1,0:T(8,128)(2,1)S(1)}, bf16[128,256]{1,0:T(8,128)(2,1)}, u32[]{:S(2)}) copy-start(bf16[128,256]{1,0:T(8,128)(2,1)} %param.10) | copy-start | bytes 196612
  2.4 4.5 %copy-start.11 = (f32[128,1,16]{2,1,0:T(1,128)}, f32[128,1,16]{2,1,0:T(1,128)S(1)}, u32[]{:S(2)}) copy-start(f32[128,1,16]{2,1,0:T(1,128)S(1)} %fusion.48) | copy-start | bytes 24580
  5.0 2.9 %copy-start.5 = (bf16[128,1024]{0,1:T(8,128)(2,1)}, bf16[128,1024]{0,1:T(8,128)(2,1)S(1)}, u32[]{:S(2)}) copy-start(bf16[128,1024]{0,1:T(8,128)(2,1)S(1)} %copy.83) | copy-start | bytes 786436
  6.3 0.8 copy-start.2
  6.3 1.0 copy-start.4
  16.9 66.0 %all-to-all-start = ((f32[32,16,1152]{2,1,0:T(8,128)}), f32[32,16,1152]{2,1,0:T(8,128)S(1)}, u32[]{:S(2)}, u32[]{:S(2)}) async-start(f32[32,16,1152]{2,1,0:T(8,128)} %pad_maximum_fusion), calls=%async_computation | async-start | bytes 4718592 | tf_op jit(solution)/shard_map/all_to_all | solution.py:47
  108.3 55.2 %all-to-all-start.1 = ((f32[32,16,1024]{2,1,0:T(8,128)}), f32[32,16,1024]{2,1,0:T(8,128)S(1)}, u32[]{:S(2)}, u32[]{:S(2)}) async-start(f32[32,16,1024]{2,1,0:T(8,128)} %reshape.337), calls=%async_computation.1 | async-start | bytes 4194304 | tf_op jit(solution)/shard_map/all_to_all | solution.py:60
  116.2 0.6 copy-start.9
  175.3 2.0 %copy-start.1 = (f32[256,16,64]{0,2,1:T(8,128)S(1)}, f32[256,16,64]{0,2,1:T(8,128)}, u32[]{:S(2)}) copy-start(f32[256,16,64]{0,2,1:T(8,128)} %copy.90) | copy-start | bytes 3145732
  175.3 4.2 %copy-start.16 = (f32[16]{0:T(128)S(1)}, f32[16]{0:T(128)}, u32[]{:S(2)}) copy-start(f32[16]{0:T(128)} %multiply_reduce_fusion) | copy-start | bytes 196
  175.3 4.9 %copy-start.3 = (f32[128,1024]{0,1:T(8,128)S(1)}, f32[128,1024]{0,1:T(8,128)}, u32[]{:S(2)}) copy-start(f32[128,1024]{0,1:T(8,128)} %copy-done.2) | copy-start | bytes 1572868
  177.3 4.5 %copy-start.13 = (f32[128,16]{0,1:T(8,128)S(1)}, f32[128,16]{0,1:T(8,128)}, u32[]{:S(2)}) copy-start(f32[128,16]{0,1:T(8,128)} %multiply_reduce_fusion.1) | copy-start | bytes 24580
  177.3 4.7 %copy-start.6 = (bf16[128,1024]{0,1:T(8,128)(2,1)S(1)}, bf16[128,1024]{0,1:T(8,128)(2,1)}, u32[]{:S(2)}) copy-start(bf16[128,1024]{0,1:T(8,128)(2,1)} %copy-done.5) | copy-start | bytes 786436
  177.3 4.7 %copy-start.10 = (f32[128,128]{1,0:T(8,128)S(1)}, f32[128,128]{1,0:T(8,128)}, u32[]{:S(2)}) copy-start(f32[128,128]{1,0:T(8,128)} %copy-done.9) | copy-start | bytes 196612
  177.4 4.7 %copy-start.12 = (f32[128,128]{1,0:T(8,128)S(1)}, f32[128,128]{1,0:T(8,128)}, u32[]{:S(2)}) copy-start(f32[128,128]{1,0:T(8,128)} %copy.81) | copy-start | bytes 196612
  177.4 4.7 %copy-start.14 = (f32[128,16]{0,1:T(8,128)S(1)}, f32[128,16]{0,1:T(8,128)}, u32[]{:S(2)}) copy-start(f32[128,16]{0,1:T(8,128)} %param.11) | copy-start | bytes 24580
  177.4 4.7 %copy-start.15 = (f32[128,16]{0,1:T(8,128)S(1)}, f32[128,16]{0,1:T(8,128)}, u32[]{:S(2)}) copy-start(f32[128,16]{0,1:T(8,128)} %get-tuple-element.21) | copy-start | bytes 24580
  181.2 1.8 copy-start.17
  181.2 9.9 %copy-start.8 = (f32[128,128]{1,0:T(8,128)S(1)}, f32[128,128]{1,0:T(8,128)}, u32[]{:S(2)}) copy-start(f32[128,128]{1,0:T(8,128)} %get-tuple-element.25) | copy-start | bytes 196612
  184.0 11.7 %all-to-all-start.2 = ((f32[8,1,256]{2,1,0:T(1,128)}), f32[8,1,256]{2,1,0:T(1,128)S(1)}, u32[]{:S(2)}, u32[]{:S(2)}) async-start(f32[8,1,256]{2,1,0:T(1,128)} %reshape.355), calls=%async_computation.2 | async-start | bytes 16384 | tf_op jit(solution)/shard_map/all_to_all | solution.py:207

commit v7 on v4

--- a/solution.py
+++ b/solution.py
@@ -10,6 +10,7 @@
 
 
 precise = lax.Precision.HIGHEST
+fast = lax.Precision.HIGH
 
 
 def prefix(part, axis, combine, identity, reverse):
@@ -61,7 +62,7 @@
     after = (position[None, :] > position[:, None])
     mask = jnp.where((held < heads)[:, None, None], before[None], after[None])
     weights = jnp.where(mask, jnp.exp(exponent), 0.0)
-    scanned = jnp.einsum("cij,jcx->icx", weights, pieces, precision=precise)
+    scanned = jnp.einsum("cij,jcx->icx", weights, pieces, precision=fast)
     back = lax.all_to_all(scanned.reshape(count, per * 8, -1), axis, 0, 0, tiled=True)
     back = back.reshape(shape).transpose(0, 1, 3, 2, 4)
     return back[0], back[1]
@@ -74,14 +75,14 @@
         "qghp,qgn->gnhp",
         inputs.astype(jnp.float32) * to_end[..., None],
         input_proj.astype(jnp.float32),
-        precision=precise,
+        precision=fast,
     )
     from_start = jnp.exp(cumulative)
     backward = jnp.einsum(
         "qghp,qgn->gnhp",
         out_grad.astype(jnp.float32) * from_start[..., None],
         readout.astype(jnp.float32),
-        precision=precise,
+        precision=fast,
     )
     return (totals, forward, backward)
 
@@ -105,11 +106,11 @@
         "ughp,sghp->usgh", out_raw, inputs_raw, preferred_element_type=jnp.float32
     )
     mix_input = decays * state_match[..., None]
-    vector = jnp.einsum("usgh,ughp->sghp", mix_input, out_grad, precision=precise)
+    vector = jnp.einsum("usgh,ughp->sghp", mix_input, out_grad, precision=fast)
     direct = jnp.sum(inputs * vector, axis=-1)
     mix_state = decays * grad_match * step_size[None]
-    grad_proj = jnp.einsum("usgh,ugn->sgn", mix_state, readout, precision=precise)
-    grad_read = jnp.einsum("usgh,sgn->ugn", mix_state, input_proj, precision=precise)
+    grad_proj = jnp.einsum("usgh,ugn->sgn", mix_state, readout, precision=fast)
+    grad_read = jnp.einsum("usgh,sgn->ugn", mix_state, input_proj, precision=fast)
     weights = mix_state * state_match[..., None]
     exclusive = jnp.cumsum(weights, axis=1) - weights
     paired = jnp.sum(exclusive * causal[:, :, None, None], axis=0)
@@ -132,21 +133,21 @@
     totals = cumulative[-1]
     to_end = jnp.exp(totals[None] - cumulative)
     from_start = jnp.exp(cumulative)
-    back_b = jnp.einsum("gnhp,sgn->sghp", grad_in, input_proj, precision=precise)
+    back_b = jnp.einsum("gnhp,sgn->sghp", grad_in, input_proj, precision=fast)
     vector = vector + to_end[..., None] * back_b
     grad_inputs = step_size[..., None] * vector
     tail_dot = jnp.sum(inputs * back_b, axis=-1)
     direct = direct + to_end * tail_dot
     scaled_x = (step_size * to_end)[..., None] * inputs
-    grad_proj = grad_proj + jnp.einsum("sghp,gnhp->sgn", scaled_x, grad_in, precision=precise)
+    grad_proj = grad_proj + jnp.einsum("sghp,gnhp->sgn", scaled_x, grad_in, precision=fast)
     scaled_y = from_start[..., None] * out_grad
-    grad_read = grad_read + jnp.einsum("ughp,gnhp->ugn", scaled_y, state_in, precision=precise)
-    read_state = jnp.einsum("ugn,gnhp->ughp", readout, state_in, precision=precise)
+    grad_read = grad_read + jnp.einsum("ughp,gnhp->ugn", scaled_y, state_in, precision=fast)
+    read_state = jnp.einsum("ugn,gnhp->ughp", readout, state_in, precision=fast)
     from_init = from_start * jnp.sum(read_state * out_grad, axis=-1)
-    suffixes = jnp.einsum("ut,ugh->tgh", causal, from_init, precision=precise)
+    suffixes = jnp.einsum("ut,ugh->tgh", causal, from_init, precision=fast)
     from_tail = to_end * step_size * tail_dot
-    prefixes = jnp.einsum("st,sgh->tgh", strictly, from_tail, precision=precise)
-    constant = jnp.exp(totals) * jnp.einsum("gnhp,gnhp->gh", grad_in, state_in, precision=precise)
+    prefixes = jnp.einsum("st,sgh->tgh", strictly, from_tail, precision=fast)
+    constant = jnp.exp(totals) * jnp.einsum("gnhp,gnhp->gh", grad_in, state_in, precision=fast)
     grad_log = paired + suffixes + prefixes + constant[None]
     grad_step = direct - decay_rate[None] * grad_log
     return (grad_inputs, grad_proj, grad_read, grad_step)

time: 171 us -> 168 us (0.982)
  matrix products: 16 us -> 13.3 us
    dot_general x10, matrix products: 9.69 us -> 7.31 us  [the longest x1 1.41 us: span_state(): back_b = jnp.einsum('gnhp,sgn->sghp', grad_in, input_proj, precision=fast)]
where the time goes in v7:
time: 168 us; the launch traced here: 167 us
  waiting for transfers between devices  84.8 us (50%)
  local copies, waits for them, and re-layouts  30.2 us (18%)
  starting transfers between devices  26.8 us (16%)
  matrix products  13.3 us (8%)
  other arithmetic  11.1 us (7%)
    all_to_all x1, waiting for transfers between devices, seq_scan(): pieces = lax.all_to_all(payload, axis, 0, 0, tiled=True)  51.1 us
    all_to_all x1, waiting for transfers between devices, seq_scan(): lax.all_to_all(scanned.reshape(count, per * 8, -1), axis, 0, 0, tiled=True)  31.7 us
    all_to_all x1, starting transfers between devices, seq_scan(): pieces = lax.all_to_all(payload, axis, 0, 0, tiled=True)  11.9 us
    unnamed x42, local copies, waits for them, and re-layouts  9.15 us
    all_to_all x1, starting transfers between devices, body(): lax.all_to_all(grad_step, 'tp', split_axis=0, concat_axis=1, tiled=True)  7.78 us
    all_to_all x1, starting transfers between devices, seq_scan(): lax.all_to_all(scanned.reshape(count, per * 8, -1), axis, 0, 0, tiled=True)  7.21 us
    reshape x2, local copies, waits for them, and re-layouts, seq_scan(): back = back.reshape(shape).transpose(0, 1, 3, 2, 4)  5.8 us
    reshape x1, local copies, waits for them, and re-layouts, seq_scan(): flat = stacked.reshape(count, per * 8, -1)  3.61 us
  transfers between devices with their start and end apart: 3, of which 3 were waited for; matrix products, arithmetic and copies ran while one was open for 11% of the time, Pallas kernels for 0%

profile of v7, /device:TPU:1, one launch (start us, length us, event | category | flops | bytes accessed | tf_op | source)
XLA Modules:
  0.0 167.2 jit_solution(15047707702179350676)
XLA Ops:
  3.6 1.2 copy.68
  4.8 1.4 fusion.56
  7.4 2.7 %copy.71 = f32[2,1,16,256,64]{4,3,2,0,1:T(8,128)} copy(f32[2,1,16,256,64]{3,4,2,1,0:T(8,128)S(1)} %maximum_bitcast_fusion) | data formatting | bytes 4194304 | tf_op jit(solution)/shard_map/transpose | solution.py:37
  10.1 3.6 %reshape.327 = f32[32,8,2048]{2,1,0:T(8,128)S(1)} reshape(f32[2,1,16,256,64]{4,3,2,0,1:T(8,128)} %copy.71) | data formatting | bytes 4194304 | tf_op jit(solution)/shard_map/reshape | solution.py:48
  14.6 1.6 pad_maximum_fusion
  16.2 11.9 %all-to-all-start = ((f32[32,8,2176]{2,1,0:T(8,128)}), f32[32,8,2176]{2,1,0:T(8,128)S(1)}, u32[]{:S(2)}, u32[]{:S(2)}) async-start(f32[32,8,2176]{2,1,0:T(8,128)} %pad_maximum_fusion), calls=%async_computation | async-start | bytes 4456448 | tf_op jit(solution)/shard_map/all_to_all | solution.py:53
  28.0 51.1 %all-to-all-done = f32[32,8,2176]{2,1,0:T(8,128)S(1)} async-done(((f32[32,8,2176]{2,1,0:T(8,128)}), f32[32,8,2176]{2,1,0:T(8,128)S(1)}, u32[]{:S(2)}, u32[]{:S(2)}) %all-to-all-start) | async-done | bytes 2228256 | tf_op jit(solution)/shard_map/all_to_all | solution.py:53
  79.4 1.2 copy.93
  80.9 1.2 fusion.35
  83.1 2.6 %copy.94 = f32[4,8,8,2048]{3,2,1,0:T(8,128)} copy(f32[4,8,8,2048]{3,1,2,0:T(8,128)S(1)} %bitcast.188) | data formatting | bytes 4194304
  85.7 7.2 %all-to-all-start.1 = ((f32[32,8,2048]{2,1,0:T(8,128)}), f32[32,8,2048]{2,1,0:T(8,128)S(1)}, u32[]{:S(2)}, u32[]{:S(2)}) async-start(f32[32,8,2048]{2,1,0:T(8,128)} %bitcast.186), calls=%async_computation.1 | async-start | bytes 4194304 | tf_op jit(solution)/shard_map/all_to_all | solution.py:66
  93.7 1.6 copy.67
  95.9 3.1 %broadcast_multiply_fusion = (f32[128,128,1,16]{1,0,3,2:T(8,128)}, f32[128,128]{1,0:T(8,128)}) fusion(f32[128,128]{1,0:T(8,128)} %copy.67, f32[128,16]{0,1:T(8,128)} %param.11, bf16[128,16,64]{0,2,1:T(8,128)(2,1)} %bitcast.197, bf16[128,16,64]{0,2,1:T(8,128)(2,1)S(1)} %bitcast.194, f32[128,128]{1,0:T(8,128)S(1)} %fusion.43, f32[128,16]{0,1:T(8,128)S(1)} %bitcast.202), kind=kOutput, calls=%fused_computation.52 | convolution fusion | flops 35373056 | bytes 1785856 | tf_op jit(solution)/shard_map/ughp,sghp->usgh/dot_general | solution.py:105
  99.1 2.6 %copy.77 = f32[128,128,1,16]{0,3,1,2:T(8,128)} copy(f32[128,128,1,16]{1,0,3,2:T(8,128)} %get-tuple-element.22) | data formatting | bytes 2097152 | tf_op jit(solution)/shard_map/mul | solution.py:114
  101.7 2.3 %fusion.58 = f32[128,128,1,16]{0,3,1,2:T(8,128)} fusion(f32[128,128,1,16]{0,3,1,2:T(8,128)} %copy.77), kind=kOutput, calls=%fused_computation.96 | output fusion | flops 33292288 | bytes 2097152 | tf_op jit(solution)/shard_map/jit(cumsum)/reduce_window_sum | solution.py:115
  104.0 2.6 %copy.78 = f32[128,128,1,16]{1,0,3,2:T(8,128)} copy(f32[128,128,1,16]{0,3,1,2:T(8,128)} %fusion.58) | data formatting | bytes 2097152 | tf_op jit(solution)/shard_map/jit(cumsum)/reduce_window_sum | solution.py:115
  106.6 2.3 %multiply_reduce_fusion = f32[128,16]{0,1:T(8,128)} fusion(f32[128,128,1,16]{1,0,3,2:T(8,128)} %copy.78, f32[128,128,1,16]{1,0,3,2:T(8,128)} %get-tuple-element.22, f32[128,128]{1,0:T(8,128)} %copy-done.8), kind=kLoop, calls=%fused_computation.35 | loop fusion | flops 784384 | bytes 2170880 | tf_op jit(solution)/shard_map/reduce_sum | solution.py:116
  108.8 31.7 %all-to-all-done.1 = f32[32,8,2048]{2,1,0:T(8,128)S(1)} async-done(((f32[32,8,2048]{2,1,0:T(8,128)}), f32[32,8,2048]{2,1,0:T(8,128)S(1)}, u32[]{:S(2)}, u32[]{:S(2)}) %all-to-all-start.1) | async-done | bytes 2097184 | tf_op jit(solution)/shard_map/all_to_all | solution.py:66
  140.5 3.0 %reshape.331 = f32[2,1,16,256,64]{4,3,2,0,1:T(8,128)} reshape(f32[32,8,2048]{2,1,0:T(8,128)S(1)} %all-to-all-done.1) | data formatting | bytes 4194304 | tf_op jit(solution)/shard_map/reshape | solution.py:67
  143.5 2.8 %copy.72 = f32[2,1,16,256,64]{3,4,2,1,0:T(8,128)S(1)} copy(f32[2,1,16,256,64]{4,3,2,0,1:T(8,128)} %reshape.331) | data formatting | bytes 4194304 | tf_op jit(solution)/shard_map/reshape | solution.py:67
  146.3 1.4 multiply_reduce_fusion.1
  148.0 1.2 convolution_bitcast_fusion.8
  152.9 7.8 %all-to-all-start.2 = ((f32[8,1,256]{2,1,0:T(1,128)}), f32[8,1,256]{2,1,0:T(1,128)S(1)}, u32[]{:S(2)}, u32[]{:S(2)}) async-start(f32[8,1,256]{2,1,0:T(1,128)} %reshape.357), calls=%async_computation.2 | async-start | bytes 16384 | tf_op jit(solution)/shard_map/all_to_all | solution.py:213
  163.2 2.1 %all-to-all-done.2 = f32[8,1,256]{2,1,0:T(1,128)S(1)} async-done(((f32[8,1,256]{2,1,0:T(1,128)}), f32[8,1,256]{2,1,0:T(1,128)S(1)}, u32[]{:S(2)}, u32[]{:S(2)}) %all-to-all-start.2) | async-done | bytes 8224 | tf_op jit(solution)/shard_map/all_to_all | solution.py:213
  (71 shorter events, 16.1 us)
Async XLA Ops:
  0.6 6.1 %copy-start = (bf16[128,256]{1,0:T(8,128)(2,1)S(1)}, bf16[128,256]{1,0:T(8,128)(2,1)}, u32[]{:S(2)}) copy-start(bf16[128,256]{1,0:T(8,128)(2,1)} %param.9) | copy-start | bytes 196612
  0.6 5.7 %copy-start.5 = (bf16[128,256]{1,0:T(8,128)(2,1)S(1)}, bf16[128,256]{1,0:T(8,128)(2,1)}, u32[]{:S(2)}) copy-start(bf16[128,256]{1,0:T(8,128)(2,1)} %param.10) | copy-start | bytes 196612
  2.4 3.9 %copy-start.10 = (f32[128,1,16]{2,1,0:T(1,128)}, f32[128,1,16]{2,1,0:T(1,128)S(1)}, u32[]{:S(2)}) copy-start(f32[128,1,16]{2,1,0:T(1,128)S(1)} %fusion.57) | copy-start | bytes 24580
  3.6 3.2 %copy-start.3 = (bf16[128,1024]{0,1:T(8,128)(2,1)}, bf16[128,1024]{0,1:T(8,128)(2,1)S(1)}, u32[]{:S(2)}) copy-start(bf16[128,1024]{0,1:T(8,128)(2,1)S(1)} %copy.69) | copy-start | bytes 786436
  4.8 1.9 %copy-start.1 = (bf16[128,1024]{0,1:T(8,128)(2,1)}, bf16[128,1024]{0,1:T(8,128)(2,1)S(1)}, u32[]{:S(2)}) copy-start(bf16[128,1024]{0,1:T(8,128)(2,1)S(1)} %copy.68) | copy-start | bytes 786436
  10.1 3.6 %copy-start.15 = (s32[32]{0:T(128)S(1)}, s32[32]{0:T(128)}, u32[]{:S(2)}) copy-start(s32[32]{0:T(128)} %constant.28) | copy-start | bytes 388
  16.2 63.0 %all-to-all-start = ((f32[32,8,2176]{2,1,0:T(8,128)}), f32[32,8,2176]{2,1,0:T(8,128)S(1)}, u32[]{:S(2)}, u32[]{:S(2)}) async-start(f32[32,8,2176]{2,1,0:T(8,128)} %pad_maximum_fusion), calls=%async_computation | async-start | bytes 4456448 | tf_op jit(solution)/shard_map/all_to_all | solution.py:53
  85.7 10.2 %copy-start.2 = (bf16[128,1024]{0,1:T(8,128)(2,1)S(1)}, bf16[128,1024]{0,1:T(8,128)(2,1)}, u32[]{:S(2)}) copy-start(bf16[128,1024]{0,1:T(8,128)(2,1)} %copy-done.1) | copy-start | bytes 786436
  85.7 54.8 %all-to-all-start.1 = ((f32[32,8,2048]{2,1,0:T(8,128)}), f32[32,8,2048]{2,1,0:T(8,128)S(1)}, u32[]{:S(2)}, u32[]{:S(2)}) async-start(f32[32,8,2048]{2,1,0:T(8,128)} %bitcast.186), calls=%async_computation.1 | async-start | bytes 4194304 | tf_op jit(solution)/shard_map/all_to_all | solution.py:66
  95.3 0.6 copy-start.8
  147.9 3.1 %copy-start.12 = (f32[128,16]{0,1:T(8,128)S(1)}, f32[128,16]{0,1:T(8,128)}, u32[]{:S(2)}) copy-start(f32[128,16]{0,1:T(8,128)} %multiply_reduce_fusion) | copy-start | bytes 24580
  147.9 3.2 %copy-start.4 = (bf16[128,1024]{0,1:T(8,128)(2,1)S(1)}, bf16[128,1024]{0,1:T(8,128)(2,1)}, u32[]{:S(2)}) copy-start(bf16[128,1024]{0,1:T(8,128)(2,1)} %copy-done.3) | copy-start | bytes 786436
  147.9 3.2 %copy-start.9 = (f32[128,128]{1,0:T(8,128)S(1)}, f32[128,128]{1,0:T(8,128)}, u32[]{:S(2)}) copy-start(f32[128,128]{1,0:T(8,128)} %copy-done.8) | copy-start | bytes 196612
  147.9 3.2 %copy-start.11 = (f32[128,128]{1,0:T(8,128)S(1)}, f32[128,128]{1,0:T(8,128)}, u32[]{:S(2)}) copy-start(f32[128,128]{1,0:T(8,128)} %copy.67) | copy-start | bytes 196612
  148.0 3.2 %copy-start.13 = (f32[128,16]{0,1:T(8,128)S(1)}, f32[128,16]{0,1:T(8,128)}, u32[]{:S(2)}) copy-start(f32[128,16]{0,1:T(8,128)} %param.11) | copy-start | bytes 24580
  148.0 3.2 %copy-start.14 = (f32[128,16]{0,1:T(8,128)S(1)}, f32[128,16]{0,1:T(8,128)}, u32[]{:S(2)}) copy-start(f32[128,16]{0,1:T(8,128)} %get-tuple-element.21) | copy-start | bytes 24580
  149.8 2.1 %copy-start.16 = (f32[16]{0:T(128)S(1)}, f32[16]{0:T(128)}, u32[]{:S(2)}) copy-start(f32[16]{0:T(128)} %param.12) | copy-start | bytes 196
  149.8 10.8 %copy-start.6 = (f32[256,128]{0,1:T(8,128)S(1)}, f32[256,128]{0,1:T(8,128)}, u32[]{:S(2)}) copy-start(f32[256,128]{0,1:T(8,128)} %convolution_bitcast_fusion.8) | copy-start | bytes 393220
  149.8 10.8 %copy-start.7 = (f32[128,128]{1,0:T(8,128)S(1)}, f32[128,128]{1,0:T(8,128)}, u32[]{:S(2)}) copy-start(f32[128,128]{1,0:T(8,128)} %get-tuple-element.23) | copy-start | bytes 196612
  152.9 12.4 %all-to-all-start.2 = ((f32[8,1,256]{2,1,0:T(1,128)}), f32[8,1,256]{2,1,0:T(1,128)S(1)}, u32[]{:S(2)}, u32[]{:S(2)}) async-start(f32[8,1,256]{2,1,0:T(1,128)} %reshape.357), calls=%async_computation.2 | async-start | bytes 16384 | tf_op jit(solution)/shard_map/all_to_all | solution.py:213

commit v8 on v7

--- a/solution.py
+++ b/solution.py
@@ -32,27 +32,25 @@
 def seq_scan(device_log, device_fwd, device_bwd, axis):
     count = lax.axis_size(axis)
     place = lax.axis_index(axis)
-    logs = device_log.reshape(-1)
-    heads = logs.shape[0]
-    stacked = jnp.stack([device_fwd, device_bwd]).transpose(0, 1, 3, 2, 4)
+    group_count, state_dim, heads, head_dim = device_fwd.shape
+    tiles = heads * head_dim // 128
+    per_tile = 128 // head_dim
+    halves = count // (2 * group_count * tiles)
+    rows = state_dim // halves
+    stacked = jnp.stack([device_fwd, device_bwd])
     shape = stacked.shape
-    combos = 2 * heads
-    if combos % count == 0:
-        per = combos // count
-        targets = np.arange(count)[:, None] * per + np.arange(per)[None, :]
-        held = place * per + jnp.arange(per)
-    else:
-        per = 1
-        targets = (np.arange(count) // (count // combos))[:, None]
-        held = (place // (count // combos))[None]
-    flat = stacked.reshape(count, per * 8, -1)
-    width = flat.shape[2]
-    tags = jnp.repeat(logs[targets % heads], 8, axis=1)
-    tags = jnp.broadcast_to(tags[..., None], (count, per * 8, 128))
-    payload = jnp.concatenate([flat, tags], axis=2)
-    pieces = lax.all_to_all(payload, axis, 0, 0, tiled=True)
-    chosen = pieces[:, ::8, width]
-    pieces = pieces[:, :, :width].reshape(count, per, -1)
+    cut = stacked.reshape(2, group_count, halves, rows, tiles, 128).transpose(0, 1, 4, 2, 3, 5)
+    cut = cut.reshape(count, rows, 128)
+    index = np.arange(count)
+    owner_group = (index // (tiles * halves)) % group_count
+    owner_tile = (index // halves) % tiles
+    owned = owner_tile[:, None] * per_tile + np.arange(per_tile)[None, :]
+    tags = jnp.pad(device_log[owner_group[:, None], owned], ((0, 0), (0, 128 - per_tile)))
+    tags = jnp.broadcast_to(tags[:, None, :], (count, 8, 128))
+    got = lax.all_to_all(jnp.concatenate([cut, tags], axis=1), axis, 0, 0, tiled=True)
+    chosen = got[:, rows, :per_tile]
+    pieces = got[:, :rows, :]
+    forward = place < count // 2
     position = jnp.arange(count)
     low = jnp.minimum(position[:, None], position[None, :])
     high = jnp.maximum(position[:, None], position[None, :])
@@ -60,11 +58,16 @@
     exponent = jnp.einsum("ijm,mc->cij", between.astype(jnp.float32), chosen, precision=precise)
     before = (position[None, :] < position[:, None])
     after = (position[None, :] > position[:, None])
-    mask = jnp.where((held < heads)[:, None, None], before[None], after[None])
-    weights = jnp.where(mask, jnp.exp(exponent), 0.0)
-    scanned = jnp.einsum("cij,jcx->icx", weights, pieces, precision=fast)
-    back = lax.all_to_all(scanned.reshape(count, per * 8, -1), axis, 0, 0, tiled=True)
-    back = back.reshape(shape).transpose(0, 1, 3, 2, 4)
+    mask = jnp.where(forward, before, after)
+    weights = jnp.where(mask[None], jnp.exp(exponent), 0.0)
+    lane_head = np.arange(128) // head_dim
+    scanned = jnp.zeros_like(pieces)
+    for head in range(per_tile):
+        part = jnp.einsum("ij,jrl->irl", weights[head], pieces, precision=fast)
+        scanned = jnp.where(lane_head == head, part, scanned)
+    back = lax.all_to_all(scanned, axis, 0, 0, tiled=True)
+    back = back.reshape(2, group_count, tiles, halves, rows, 128).transpose(0, 1, 3, 4, 2, 5)
+    back = back.reshape(shape)
     return back[0], back[1]
 
 def summarize(inputs, out_grad, input_proj, readout, step_size, decay_rate):

time: 168 us -> 174 us (1.036)
  matrix products: 13.3 us -> 18.2 us
  other arithmetic: 11.1 us -> 13.7 us
    reshape x3 -> x1, local copies, waits for them, and re-layouts: 9.41 us -> 2.34 us  [seq_scan(): back.reshape(2, group_count, tiles, halves, rows, 128)]
    another operation x0 -> x4, local copies, waits for them, and re-layouts: none -> 4.95 us
    unnamed x42 -> x50, local copies, waits for them, and re-layouts: 9.15 us -> 4.34 us
    dot_general x1 -> x2, matrix products: 0.99 us -> 4.41 us  [seq_scan(): part = jnp.einsum('ij,jrl->irl', weights[head], pieces, precision=fast)]
    transpose x1, other arithmetic: 0.22 us -> 3.64 us  [seq_scan(): stacked.reshape(2, group_count, halves, rows, tiles, 128)]
    select_n x0 -> x1, local copies, waits for them, and re-layouts: none -> 2.55 us  [seq_scan(): scanned = jnp.where(lane_head == head, part, scanned)]
    slice x2 -> x4, local copies, waits for them, and re-layouts: 0.57 us -> 3 us  [the longest x1 2.71 us: seq_scan(): return (back[0], back[1])]
  transfers between devices with their start and end apart: 3 -> 3, of which waited for: 3 -> 3; matrix products, arithmetic and copies ran while one was open for 11% -> 10% of each run, Pallas kernels for 0% -> 0%
where the time goes in v8:
time: 174 us; the launch traced here: 173 us
  waiting for transfers between devices  84.8 us (49%)
  local copies, waits for them, and re-layouts  28.6 us (16%)
  starting transfers between devices  26.9 us (15%)
  matrix products  18.2 us (10%)
  other arithmetic  13.7 us (8%)
    all_to_all x1, waiting for transfers between devices, seq_scan(): lax.all_to_all(jnp.concatenate([cut, tags], axis=1), axis, 0, 0, tiled=True)  51.1 us
    all_to_all x1, waiting for transfers between devices, seq_scan(): back = lax.all_to_all(scanned, axis, 0, 0, tiled=True)  31.6 us
    all_to_all x1, starting transfers between devices, seq_scan(): lax.all_to_all(jnp.concatenate([cut, tags], axis=1), axis, 0, 0, tiled=True)  11.9 us
    all_to_all x1, starting transfers between devices, body(): lax.all_to_all(grad_step, 'tp', split_axis=0, concat_axis=1, tiled=True)  7.81 us
    all_to_all x1, starting transfers between devices, seq_scan(): back = lax.all_to_all(scanned, axis, 0, 0, tiled=True)  7.2 us
    dot_general x2, matrix products, seq_scan(): part = jnp.einsum('ij,jrl->irl', weights[head], pieces, precision=fast)  4.41 us
    unnamed x50, local copies, waits for them, and re-layouts  4.34 us
    transpose x1, other arithmetic, seq_scan(): stacked.reshape(2, group_count, halves, rows, tiles, 128)  3.64 us
  transfers between devices with their start and end apart: 3, of which 3 were waited for; matrix products, arithmetic and copies ran while one was open for 10% of the time, Pallas kernels for 0%

profile of v8, /device:TPU:1, one launch (start us, length us, event | category | flops | bytes accessed | tf_op | source)
XLA Modules:
  0.0 173.3 jit_solution(9626166821562862800)
XLA Ops:
  7.2 1.5 stack.7
  8.7 3.6 %maximum_bitcast_fusion = f32[2,1,8,2,128,128]{4,3,5,2,1,0:T(2,128)} fusion(f32[1,1,2,128,8,128]{3,2,5,4,1,0:T(2,128)S(1)} %stack.8, f32[1,1,2,128,8,128]{3,2,5,4,1,0:T(2,128)} %stack.7), kind=kLoop, calls=%fused_computation.2 | loop fusion | flops 524288 | bytes 4194304 | tf_op jit(solution)/shard_map/transpose | solution.py:42
  12.3 2.7 %copy.65 = f32[2,1,8,2,128,128]{5,4,3,2,0,1:T(8,128)S(1)} copy(f32[2,1,8,2,128,128]{4,3,5,2,1,0:T(2,128)} %maximum_bitcast_fusion) | data formatting | bytes 4194304 | tf_op jit(solution)/shard_map/transpose | solution.py:42
  15.1 1.6 pad_maximum_fusion
  16.6 11.9 %all-to-all-start = ((f32[32,136,128]{2,1,0:T(8,128)}), f32[32,136,128]{2,1,0:T(8,128)S(1)}, u32[]{:S(2)}, u32[]{:S(2)}) async-start(f32[32,136,128]{2,1,0:T(8,128)} %pad_maximum_fusion), calls=%async_computation | async-start | bytes 4456448 | tf_op jit(solution)/shard_map/all_to_all | solution.py:50
  28.5 51.1 %all-to-all-done = f32[32,136,128]{2,1,0:T(8,128)S(1)} async-done(((f32[32,136,128]{2,1,0:T(8,128)}), f32[32,136,128]{2,1,0:T(8,128)S(1)}, u32[]{:S(2)}, u32[]{:S(2)}) %all-to-all-start) | async-done | bytes 2228256 | tf_op jit(solution)/shard_map/all_to_all | solution.py:50
  79.6 1.3 fusion.16
  81.2 2.1 %fusion = f32[32,128,128]{2,0,1:T(8,128)S(1)} fusion(f32[32,32,1]{1,0,2:T(8,128)S(1)} %bitcast.186, f32[32,128,128]{2,1,0:T(8,128)S(1)} %slice.36), kind=kOutput, calls=%fused_computation.4 | convolution fusion | flops 100663296 | bytes 4198400 | tf_op jit(solution)/shard_map/ij,jrl->irl/dot_general | solution.py:66
  83.4 2.3 %select_select_fusion = f32[32,128,128]{2,0,1:T(8,128)S(1)} fusion(f32[32,128,128]{2,0,1:T(8,128)S(1)} %fusion, f32[32,32,1]{1,0,2:T(8,128)S(1)} %bitcast.185, f32[32,128,128]{2,1,0:T(8,128)S(1)} %slice.36, pred[128]{0:T(512)(128)(4,1)S(1)} %copy-done.19, pred[128]{0:T(512)(128)(4,1)S(1)} %copy-done.20), kind=kOutput, calls=%fused_computation.3 | convolution fusion | flops 101711872 | bytes 6295808 | tf_op jit(solution)/shard_map/ij,jrl->irl/dot_general | solution.py:66
  85.7 2.6 %copy.68 = f32[32,128,128]{2,1,0:T(8,128)} copy(f32[32,128,128]{2,0,1:T(8,128)S(1)} %select_select_fusion) | data formatting | bytes 4194304 | tf_op jit(solution)/shard_map/jit(_where)/select_n | solution.py:67
  88.2 7.2 %all-to-all-start.1 = ((f32[32,128,128]{2,1,0:T(8,128)}), f32[32,128,128]{2,1,0:T(8,128)S(1)}, u32[]{:S(2)}, u32[]{:S(2)}) async-start(f32[32,128,128]{2,1,0:T(8,128)} %copy.68), calls=%async_computation.1 | async-start | bytes 4194304 | tf_op jit(solution)/shard_map/all_to_all | solution.py:68
  96.2 1.6 copy.61
  98.4 3.2 %broadcast_multiply_fusion = (f32[128,128,1,16]{1,0,3,2:T(8,128)}, f32[128,128]{1,0:T(8,128)}) fusion(f32[128,128]{1,0:T(8,128)} %copy.61, f32[128,16]{0,1:T(8,128)} %param.15, bf16[128,16,64]{0,2,1:T(8,128)(2,1)} %bitcast.178, bf16[128,16,64]{0,2,1:T(8,128)(2,1)S(1)} %bitcast.175, f32[128,128]{1,0:T(8,128)S(1)} %fusion.40, f32[128,16]{0,1:T(8,128)S(1)} %bitcast.183), kind=kOutput, calls=%fused_computation.50 | convolution fusion | flops 35373056 | bytes 1785856 | tf_op jit(solution)/shard_map/ughp,sghp->usgh/dot_general | solution.py:108
  101.6 2.6 %copy.74 = f32[128,128,1,16]{0,3,1,2:T(8,128)} copy(f32[128,128,1,16]{1,0,3,2:T(8,128)} %get-tuple-element.20) | data formatting | bytes 2097152 | tf_op jit(solution)/shard_map/mul | solution.py:117
  104.2 2.3 %fusion.49 = f32[128,128,1,16]{0,3,1,2:T(8,128)} fusion(f32[128,128,1,16]{0,3,1,2:T(8,128)} %copy.74), kind=kOutput, calls=%fused_computation.87 | output fusion | flops 33292288 | bytes 2097152 | tf_op jit(solution)/shard_map/jit(cumsum)/reduce_window_sum | solution.py:118
  106.5 2.6 %copy.75 = f32[128,128,1,16]{1,0,3,2:T(8,128)} copy(f32[128,128,1,16]{0,3,1,2:T(8,128)} %fusion.49) | data formatting | bytes 2097152 | tf_op jit(solution)/shard_map/jit(cumsum)/reduce_window_sum | solution.py:118
  109.1 2.3 %multiply_reduce_fusion.1 = f32[128,16]{0,1:T(8,128)} fusion(f32[128,128,1,16]{1,0,3,2:T(8,128)} %copy.75, f32[128,128,1,16]{1,0,3,2:T(8,128)} %get-tuple-element.20, f32[128,128]{1,0:T(8,128)} %copy-done.9), kind=kLoop, calls=%fused_computation.37 | loop fusion | flops 784384 | bytes 2170880 | tf_op jit(solution)/shard_map/reduce_sum | solution.py:119
  111.4 31.6 %all-to-all-done.1 = f32[32,128,128]{2,1,0:T(8,128)S(1)} async-done(((f32[32,128,128]{2,1,0:T(8,128)}), f32[32,128,128]{2,1,0:T(8,128)S(1)}, u32[]{:S(2)}, u32[]{:S(2)}) %all-to-all-start.1) | async-done | bytes 2097184 | tf_op jit(solution)/shard_map/all_to_all | solution.py:68
  143.0 2.3 %copy.69 = f32[2,1,8,2,128,128]{4,3,5,2,1,0:T(2,128)} copy(f32[2,1,8,2,128,128]{5,4,3,2,0,1:T(8,128)S(1)} %bitcast.168) | data formatting | bytes 4194304 | tf_op jit(solution)/shard_map/reshape | solution.py:69
  145.3 2.7 %fusion.46 = (f32[1,1,2,128,8,128]{3,2,5,4,1,0:T(2,128)}, f32[1,1,2,128,8,128]{3,2,5,4,1,0:T(2,128)S(1)}) fusion(f32[2,1,2,128,8,128]{3,2,5,4,1,0:T(2,128)} %bitcast.170), kind=kLoop, calls=%fused_computation.83 | loop fusion | bytes 4194304 | tf_op jit(solution)/shard_map/slice | solution.py:71
  148.9 2.8 %multiply_reduce_fusion.2 = (f32[128,16]{0,1:T(8,128)}, f32[128,16,64]{0,2,1:T(8,128)}) fusion(bf16[128,1024]{0,1:T(8,128)(2,1)} %copy-done.3, f32[256,16,64]{0,2,1:T(8,128)S(1)} %reshape.342, bf16[128,256]{1,0:T(8,128)(2,1)S(1)} %copy-done), kind=kOutput, calls=%fused_computation.51 | convolution fusion | flops 201717760 | bytes 1908736 | tf_op jit(solution)/shard_map/gnhp,sgn->sghp/dot_general | solution.py:139
  152.9 2.1 %reshape.344 = f32[256,16,64]{0,2,1:T(8,128)S(1)} reshape(f32[1,1,2,128,8,128]{3,2,5,4,1,0:T(2,128)} %get-tuple-element.18) | data formatting | bytes 2097152 | tf_op jit(solution)/shard_map/reshape.55
  158.9 7.8 %all-to-all-start.2 = ((f32[8,1,256]{2,1,0:T(1,128)}), f32[8,1,256]{2,1,0:T(1,128)S(1)}, u32[]{:S(2)}, u32[]{:S(2)}) async-start(f32[8,1,256]{2,1,0:T(1,128)} %reshape.363), calls=%async_computation.2 | async-start | bytes 16384 | tf_op jit(solution)/shard_map/all_to_all | solution.py:216
  169.2 2.1 %all-to-all-done.2 = f32[8,1,256]{2,1,0:T(1,128)S(1)} async-done(((f32[8,1,256]{2,1,0:T(1,128)}), f32[8,1,256]{2,1,0:T(1,128)S(1)}, u32[]{:S(2)}, u32[]{:S(2)}) %all-to-all-start.2) | async-done | bytes 8224 | tf_op jit(solution)/shard_map/all_to_all | solution.py:216
  (87 shorter events, 18.4 us)
Async XLA Ops:
  0.6 6.1 %copy-start = (bf16[128,256]{1,0:T(8,128)(2,1)S(1)}, bf16[128,256]{1,0:T(8,128)(2,1)}, u32[]{:S(2)}) copy-start(bf16[128,256]{1,0:T(8,128)(2,1)} %param.13) | copy-start | bytes 196612
  2.3 1.2 copy-start.12
  3.6 2.1 %copy-start.3 = (bf16[128,1024]{0,1:T(8,128)(2,1)}, bf16[128,1024]{0,1:T(8,128)(2,1)S(1)}, u32[]{:S(2)}) copy-start(bf16[128,1024]{0,1:T(8,128)(2,1)S(1)} %copy.63) | copy-start | bytes 786436
  3.6 1.2 copy-start.11
  3.6 1.3 copy-start.15
  4.6 1.1 copy-start.5
  4.9 0.8 copy-start.1
  16.6 63.0 %all-to-all-start = ((f32[32,136,128]{2,1,0:T(8,128)}), f32[32,136,128]{2,1,0:T(8,128)S(1)}, u32[]{:S(2)}, u32[]{:S(2)}) async-start(f32[32,136,128]{2,1,0:T(8,128)} %pad_maximum_fusion), calls=%async_computation | async-start | bytes 4456448 | tf_op jit(solution)/shard_map/all_to_all | solution.py:50
  81.2 2.2 %copy-start.19 = (pred[128]{0:T(512)(128)(4,1)S(1)}, pred[128]{0:T(512)(128)(4,1)}, u32[]{:S(2)}) copy-start(pred[128]{0:T(512)(128)(4,1)} %constant.40.clone) | copy-start | bytes 388
  81.2 2.2 %copy-start.20 = (pred[128]{0:T(512)(128)(4,1)S(1)}, pred[128]{0:T(512)(128)(4,1)}, u32[]{:S(2)}) copy-start(pred[128]{0:T(512)(128)(4,1)} %constant.41.clone) | copy-start | bytes 388
  88.2 10.2 %copy-start.2 = (bf16[128,1024]{0,1:T(8,128)(2,1)S(1)}, bf16[128,1024]{0,1:T(8,128)(2,1)}, u32[]{:S(2)}) copy-start(bf16[128,1024]{0,1:T(8,128)(2,1)} %copy-done.1) | copy-start | bytes 786436
  88.2 54.8 %all-to-all-start.1 = ((f32[32,128,128]{2,1,0:T(8,128)}), f32[32,128,128]{2,1,0:T(8,128)S(1)}, u32[]{:S(2)}, u32[]{:S(2)}) async-start(f32[32,128,128]{2,1,0:T(8,128)} %copy.68), calls=%async_computation.1 | async-start | bytes 4194304 | tf_op jit(solution)/shard_map/all_to_all | solution.py:68
  155.6 1.4 copy-start.14
  155.6 1.5 copy-start.4
  155.6 1.5 copy-start.6
  155.6 1.5 copy-start.10
  155.6 1.5 copy-start.13
  155.6 1.5 copy-start.16
  155.7 1.5 copy-start.18
  155.9 2.0 %copy-start.17 = (f32[128,16]{0,1:T(8,128)S(1)}, f32[128,16]{0,1:T(8,128)}, u32[]{:S(2)}) copy-start(f32[128,16]{0,1:T(8,128)} %get-tuple-element.30) | copy-start | bytes 24580
  155.9 2.1 %copy-start.21 = (f32[16]{0:T(128)S(1)}, f32[16]{0:T(128)}, u32[]{:S(2)}) copy-start(f32[16]{0:T(128)} %param.16) | copy-start | bytes 196
  155.9 10.8 %copy-start.7 = (f32[256,128]{0,1:T(8,128)S(1)}, f32[256,128]{0,1:T(8,128)}, u32[]{:S(2)}) copy-start(f32[256,128]{0,1:T(8,128)} %convolution_bitcast_fusion.9) | copy-start | bytes 393220
  155.9 10.8 %copy-start.8 = (f32[128,128]{1,0:T(8,128)S(1)}, f32[128,128]{1,0:T(8,128)}, u32[]{:S(2)}) copy-start(f32[128,128]{1,0:T(8,128)} %get-tuple-element.21) | copy-start | bytes 196612
  158.9 12.4 %all-to-all-start.2 = ((f32[8,1,256]{2,1,0:T(1,128)}), f32[8,1,256]{2,1,0:T(1,128)S(1)}, u32[]{:S(2)}, u32[]{:S(2)}) async-start(f32[8,1,256]{2,1,0:T(1,128)} %reshape.363), calls=%async_computation.2 | async-start | bytes 16384 | tf_op jit(solution)/shard_map/all_to_all | solution.py:216
  (1 other events, 0.6 us)

commit v9 on v7

--- a/solution.py
+++ b/solution.py
@@ -34,8 +34,9 @@
     place = lax.axis_index(axis)
     logs = device_log.reshape(-1)
     heads = logs.shape[0]
-    stacked = jnp.stack([device_fwd, device_bwd]).transpose(0, 1, 3, 2, 4)
+    stacked = jnp.stack([device_fwd, device_bwd]).transpose(0, 1, 3, 4, 2)
     shape = stacked.shape
+    head_dim, state_dim = shape[3], shape[4]
     combos = 2 * heads
     if combos % count == 0:
         per = combos // count
@@ -45,14 +46,15 @@
         per = 1
         targets = (np.arange(count) // (count // combos))[:, None]
         held = (place // (count // combos))[None]
-    flat = stacked.reshape(count, per * 8, -1)
-    width = flat.shape[2]
+    tiled = (count, per, head_dim // 8, 8, state_dim // 128, 128)
+    flat = stacked.reshape(tiled).transpose(0, 1, 2, 4, 3, 5).reshape(count, -1, 128)
+    body_rows = flat.shape[1]
     tags = jnp.repeat(logs[targets % heads], 8, axis=1)
     tags = jnp.broadcast_to(tags[..., None], (count, per * 8, 128))
-    payload = jnp.concatenate([flat, tags], axis=2)
+    payload = jnp.concatenate([flat, tags], axis=1)
     pieces = lax.all_to_all(payload, axis, 0, 0, tiled=True)
-    chosen = pieces[:, ::8, width]
-    pieces = pieces[:, :, :width].reshape(count, per, -1)
+    chosen = pieces[:, body_rows::8, 0]
+    pieces = pieces[:, :body_rows, :].reshape(count, per, -1)
     position = jnp.arange(count)
     low = jnp.minimum(position[:, None], position[None, :])
     high = jnp.maximum(position[:, None], position[None, :])
@@ -63,8 +65,9 @@
     mask = jnp.where((held < heads)[:, None, None], before[None], after[None])
     weights = jnp.where(mask, jnp.exp(exponent), 0.0)
     scanned = jnp.einsum("cij,jcx->icx", weights, pieces, precision=fast)
-    back = lax.all_to_all(scanned.reshape(count, per * 8, -1), axis, 0, 0, tiled=True)
-    back = back.reshape(shape).transpose(0, 1, 3, 2, 4)
+    back = lax.all_to_all(scanned.reshape(count, body_rows, 128), axis, 0, 0, tiled=True)
+    back = back.reshape(count, per, head_dim // 8, state_dim // 128, 8, 128).transpose(0, 1, 2, 4, 3, 5)
+    back = back.reshape(shape).transpose(0, 1, 4, 2, 3)
     return back[0], back[1]
 
 def summarize(inputs, out_grad, input_proj, readout, step_size, decay_rate):

time: 168 us -> 156 us (0.929)
  local copies, waits for them, and re-layouts: 30.2 us -> 15.9 us
    reshape x3 -> x0, local copies, waits for them, and re-layouts: 9.41 us -> none  [the longest x2 5.8 us: seq_scan(): back = back.reshape(shape).transpose(0, 1, 3, 2, 4)]
    transpose x1 -> x0, local copies, waits for them, and re-layouts: 2.7 us -> none  [seq_scan(): stacked = jnp.stack([device_fwd, device_bwd]).transpose(0, 1, 3, 2, 4)]
    unnamed x42 -> x39, local copies, waits for them, and re-layouts: 9.15 us -> 6.97 us
  transfers between devices with their start and end apart: 3 -> 3, of which waited for: 3 -> 3; matrix products, arithmetic and copies ran while one was open for 11% -> 12% of each run, Pallas kernels for 0% -> 0%
where the time goes in v9:
time: 156 us; the launch traced here: 155 us
  waiting for transfers between devices  84.9 us (54%)
  starting transfers between devices  26.8 us (17%)
  local copies, waits for them, and re-layouts  15.9 us (10%)
  matrix products  14.5 us (9%)
  other arithmetic  11.7 us (8%)
    all_to_all x1, waiting for transfers between devices, seq_scan(): pieces = lax.all_to_all(payload, axis, 0, 0, tiled=True)  51.1 us
    all_to_all x1, waiting for transfers between devices, seq_scan(): lax.all_to_all(scanned.reshape(count, body_rows, 128), axis, 0, 0, tiled=...  31.7 us
    all_to_all x1, starting transfers between devices, seq_scan(): pieces = lax.all_to_all(payload, axis, 0, 0, tiled=True)  11.9 us
    all_to_all x1, starting transfers between devices, body(): lax.all_to_all(grad_step, 'tp', split_axis=0, concat_axis=1, tiled=True)  7.92 us
    all_to_all x1, starting transfers between devices, seq_scan(): lax.all_to_all(scanned.reshape(count, body_rows, 128), axis, 0, 0, tiled=...  7.02 us
    unnamed x39, local copies, waits for them, and re-layouts  6.97 us
    dot_general x1, matrix products, span_local(): jnp.einsum('ughp,sghp->usgh', out_raw, inputs_raw, preferred_element_type...  3.14 us
  transfers between devices with their start and end apart: 3, of which 3 were waited for; matrix products, arithmetic and copies ran while one was open for 12% of the time, Pallas kernels for 0%

profile of v9, /device:TPU:1, one launch (start us, length us, event | category | flops | bytes accessed | tf_op | source)
XLA Modules:
  0.0 154.8 jit_solution(2801726104737137819)
XLA Ops:
  2.4 1.1 copy.68
  5.0 1.4 fusion.61
  6.4 1.1 copy.67
  8.8 1.6 %pad_maximum_fusion = f32[32,136,128]{2,1,0:T(8,128)} fusion(f32[32,8,128]{2,1,0:T(8,128)S(1)} %broadcast_in_dim.19, f32[32,128,128]{2,1,0:T(8,128)S(1)} %bitcast.198), kind=kLoop, calls=%fused_computation.1 | loop fusion | flops 557056 | bytes 4456448 | tf_op jit(solution)/shard_map/concatenate | solution.py:54
  10.4 11.9 %all-to-all-start = ((f32[32,136,128]{2,1,0:T(8,128)}), f32[32,136,128]{2,1,0:T(8,128)S(1)}, u32[]{:S(2)}, u32[]{:S(2)}) async-start(f32[32,136,128]{2,1,0:T(8,128)} %pad_maximum_fusion), calls=%async_computation | async-start | bytes 4456448 | tf_op jit(solution)/shard_map/all_to_all | solution.py:55
  22.2 51.1 %all-to-all-done = f32[32,136,128]{2,1,0:T(8,128)S(1)} async-done(((f32[32,136,128]{2,1,0:T(8,128)}), f32[32,136,128]{2,1,0:T(8,128)S(1)}, u32[]{:S(2)}, u32[]{:S(2)}) %all-to-all-start) | async-done | bytes 2228256 | tf_op jit(solution)/shard_map/all_to_all | solution.py:55
  73.7 1.2 fusion.41
  75.1 2.2 %fusion.3 = f32[4,8,128,128]{3,1,2,0:T(8,128)S(1)} fusion(f32[4,8,128,128]{3,2,1,0:T(8,128)S(1)} %bitcast.199, f32[32,32]{1,0:T(8,128)S(1)} %bitcast.214, pred[]{:T(512)S(6)} %lt.49), kind=kOutput, calls=%fused_computation.6 | convolution fusion | flops 100667392 | bytes 4198401 | tf_op jit(solution)/shard_map/cij,jcx->icx/dot_general | solution.py:67
  77.3 1.7 %copy.91 = f32[4,8,128,128]{3,2,1,0:T(8,128)} copy(f32[4,8,128,128]{3,1,2,0:T(8,128)S(1)} %fusion.3) | data formatting | bytes 4194304
  79.0 7.0 %all-to-all-start.1 = ((f32[32,128,128]{2,1,0:T(8,128)}), f32[32,128,128]{2,1,0:T(8,128)S(1)}, u32[]{:S(2)}, u32[]{:S(2)}) async-start(f32[32,128,128]{2,1,0:T(8,128)} %bitcast.197), calls=%async_computation.1 | async-start | bytes 4194304 | tf_op jit(solution)/shard_map/all_to_all | solution.py:68
  86.9 1.6 %copy.66 = f32[128,128]{1,0:T(8,128)} copy(f32[128,128]{0,1:T(8,128)} %convolution_bitcast_fusion.10) | data formatting | bytes 131072 | tf_op jit(solution)/shard_map/mul | solution.py:111
  89.1 3.1 %broadcast_multiply_fusion = (f32[128,128,1,16]{1,0,3,2:T(8,128)}, f32[128,128]{1,0:T(8,128)}) fusion(f32[128,128]{1,0:T(8,128)} %copy.66, f32[128,16]{0,1:T(8,128)} %param.11, bf16[128,16,64]{0,2,1:T(8,128)(2,1)} %bitcast.207, bf16[128,16,64]{0,2,1:T(8,128)(2,1)S(1)} %bitcast.204, f32[128,128]{1,0:T(8,128)S(1)} %fusion.49, f32[128,16]{0,1:T(8,128)S(1)} %bitcast.212), kind=kOutput, calls=%fused_computation.56 | convolution fusion | flops 35373056 | bytes 1785856 | tf_op jit(solution)/shard_map/ughp,sghp->usgh/dot_general | solution.py:108
  92.2 2.6 %copy.74 = f32[128,128,1,16]{0,3,1,2:T(8,128)} copy(f32[128,128,1,16]{1,0,3,2:T(8,128)} %get-tuple-element.22) | data formatting | bytes 2097152 | tf_op jit(solution)/shard_map/mul | solution.py:117
  94.8 2.3 %fusion.63 = f32[128,128,1,16]{0,3,1,2:T(8,128)} fusion(f32[128,128,1,16]{0,3,1,2:T(8,128)} %copy.74), kind=kOutput, calls=%fused_computation.99 | output fusion | flops 33292288 | bytes 2097152 | tf_op jit(solution)/shard_map/jit(cumsum)/reduce_window_sum | solution.py:118
  97.2 2.6 %copy.75 = f32[128,128,1,16]{1,0,3,2:T(8,128)} copy(f32[128,128,1,16]{0,3,1,2:T(8,128)} %fusion.63) | data formatting | bytes 2097152 | tf_op jit(solution)/shard_map/jit(cumsum)/reduce_window_sum | solution.py:118
  99.7 2.3 %multiply_reduce_fusion = f32[128,16]{0,1:T(8,128)} fusion(f32[128,128,1,16]{1,0,3,2:T(8,128)} %copy.75, f32[128,128,1,16]{1,0,3,2:T(8,128)} %get-tuple-element.22, f32[128,128]{1,0:T(8,128)} %copy-done.8), kind=kLoop, calls=%fused_computation.39 | loop fusion | flops 784384 | bytes 2170880 | tf_op jit(solution)/shard_map/reduce_sum | solution.py:119
  102.0 31.7 %all-to-all-done.1 = f32[32,128,128]{2,1,0:T(8,128)S(1)} async-done(((f32[32,128,128]{2,1,0:T(8,128)}), f32[32,128,128]{2,1,0:T(8,128)S(1)}, u32[]{:S(2)}, u32[]{:S(2)}) %all-to-all-start.1) | async-done | bytes 2097184 | tf_op jit(solution)/shard_map/all_to_all | solution.py:68
  133.7 1.4 multiply_reduce_fusion.1
  135.1 1.2 convolution_bitcast_fusion.9
  140.3 7.9 %all-to-all-start.2 = ((f32[8,1,256]{2,1,0:T(1,128)}), f32[8,1,256]{2,1,0:T(1,128)S(1)}, u32[]{:S(2)}, u32[]{:S(2)}) async-start(f32[8,1,256]{2,1,0:T(1,128)} %reshape.365), calls=%async_computation.2 | async-start | bytes 16384 | tf_op jit(solution)/shard_map/all_to_all | solution.py:216
  148.2 0.9 fusion.15
  149.1 0.8 fusion.14
  149.9 0.8 copy.77
  150.7 2.1 %all-to-all-done.2 = f32[8,1,256]{2,1,0:T(1,128)S(1)} async-done(((f32[8,1,256]{2,1,0:T(1,128)}), f32[8,1,256]{2,1,0:T(1,128)S(1)}, u32[]{:S(2)}, u32[]{:S(2)}) %all-to-all-start.2) | async-done | bytes 8224 | tf_op jit(solution)/shard_map/all_to_all | solution.py:216
  (64 shorter events, 12.1 us)
Async XLA Ops:
  0.6 7.4 %copy-start = (bf16[128,256]{1,0:T(8,128)(2,1)S(1)}, bf16[128,256]{1,0:T(8,128)(2,1)}, u32[]{:S(2)}) copy-start(bf16[128,256]{1,0:T(8,128)(2,1)} %param.9) | copy-start | bytes 196612
  0.6 6.9 %copy-start.5 = (bf16[128,256]{1,0:T(8,128)(2,1)S(1)}, bf16[128,256]{1,0:T(8,128)(2,1)}, u32[]{:S(2)}) copy-start(bf16[128,256]{1,0:T(8,128)(2,1)} %param.10) | copy-start | bytes 196612
  2.4 5.1 %copy-start.10 = (f32[128,1,16]{2,1,0:T(1,128)}, f32[128,1,16]{2,1,0:T(1,128)S(1)}, u32[]{:S(2)}) copy-start(f32[128,1,16]{2,1,0:T(1,128)S(1)} %fusion.62) | copy-start | bytes 24580
  3.6 4.4 %copy-start.3 = (bf16[128,1024]{0,1:T(8,128)(2,1)}, bf16[128,1024]{0,1:T(8,128)(2,1)S(1)}, u32[]{:S(2)}) copy-start(bf16[128,1024]{0,1:T(8,128)(2,1)S(1)} %copy.68) | copy-start | bytes 786436
  7.5 1.0 copy-start.1
  10.4 63.0 %all-to-all-start = ((f32[32,136,128]{2,1,0:T(8,128)}), f32[32,136,128]{2,1,0:T(8,128)S(1)}, u32[]{:S(2)}, u32[]{:S(2)}) async-start(f32[32,136,128]{2,1,0:T(8,128)} %pad_maximum_fusion), calls=%async_computation | async-start | bytes 4456448 | tf_op jit(solution)/shard_map/all_to_all | solution.py:55
  79.0 10.0 %copy-start.2 = (bf16[128,1024]{0,1:T(8,128)(2,1)S(1)}, bf16[128,1024]{0,1:T(8,128)(2,1)}, u32[]{:S(2)}) copy-start(bf16[128,1024]{0,1:T(8,128)(2,1)} %copy-done.1) | copy-start | bytes 786436
  79.0 54.7 %all-to-all-start.1 = ((f32[32,128,128]{2,1,0:T(8,128)}), f32[32,128,128]{2,1,0:T(8,128)S(1)}, u32[]{:S(2)}, u32[]{:S(2)}) async-start(f32[32,128,128]{2,1,0:T(8,128)} %bitcast.197), calls=%async_computation.1 | async-start | bytes 4194304 | tf_op jit(solution)/shard_map/all_to_all | solution.py:68
  88.5 0.6 copy-start.8
  137.0 1.4 copy-start.12
  137.0 1.6 %copy-start.4 = (bf16[128,1024]{0,1:T(8,128)(2,1)S(1)}, bf16[128,1024]{0,1:T(8,128)(2,1)}, u32[]{:S(2)}) copy-start(bf16[128,1024]{0,1:T(8,128)(2,1)} %copy-done.3) | copy-start | bytes 786436
  137.0 1.6 %copy-start.9 = (f32[128,128]{1,0:T(8,128)S(1)}, f32[128,128]{1,0:T(8,128)}, u32[]{:S(2)}) copy-start(f32[128,128]{1,0:T(8,128)} %copy-done.8) | copy-start | bytes 196612
  137.0 1.6 %copy-start.11 = (f32[128,128]{1,0:T(8,128)S(1)}, f32[128,128]{1,0:T(8,128)}, u32[]{:S(2)}) copy-start(f32[128,128]{1,0:T(8,128)} %copy.66) | copy-start | bytes 196612
  137.0 1.6 %copy-start.13 = (f32[128,16]{0,1:T(8,128)S(1)}, f32[128,16]{0,1:T(8,128)}, u32[]{:S(2)}) copy-start(f32[128,16]{0,1:T(8,128)} %param.11) | copy-start | bytes 24580
  137.0 1.6 %copy-start.14 = (f32[128,16]{0,1:T(8,128)S(1)}, f32[128,16]{0,1:T(8,128)}, u32[]{:S(2)}) copy-start(f32[128,16]{0,1:T(8,128)} %get-tuple-element.21) | copy-start | bytes 24580
  137.2 2.1 %copy-start.15 = (f32[16]{0:T(128)S(1)}, f32[16]{0:T(128)}, u32[]{:S(2)}) copy-start(f32[16]{0:T(128)} %param.12) | copy-start | bytes 196
  137.3 10.9 %copy-start.6 = (f32[256,128]{0,1:T(8,128)S(1)}, f32[256,128]{0,1:T(8,128)}, u32[]{:S(2)}) copy-start(f32[256,128]{0,1:T(8,128)} %convolution_bitcast_fusion.9) | copy-start | bytes 393220
  137.3 11.0 %copy-start.7 = (f32[128,128]{1,0:T(8,128)S(1)}, f32[128,128]{1,0:T(8,128)}, u32[]{:S(2)}) copy-start(f32[128,128]{1,0:T(8,128)} %get-tuple-element.23) | copy-start | bytes 196612
  140.3 12.5 %all-to-all-start.2 = ((f32[8,1,256]{2,1,0:T(1,128)}), f32[8,1,256]{2,1,0:T(1,128)S(1)}, u32[]{:S(2)}, u32[]{:S(2)}) async-start(f32[8,1,256]{2,1,0:T(1,128)} %reshape.365), calls=%async_computation.2 | async-start | bytes 16384 | tf_op jit(solution)/shard_map/all_to_all | solution.py:216

commit v10 on v9

--- a/solution.py
+++ b/solution.py
@@ -49,12 +49,9 @@
     tiled = (count, per, head_dim // 8, 8, state_dim // 128, 128)
     flat = stacked.reshape(tiled).transpose(0, 1, 2, 4, 3, 5).reshape(count, -1, 128)
     body_rows = flat.shape[1]
-    tags = jnp.repeat(logs[targets % heads], 8, axis=1)
-    tags = jnp.broadcast_to(tags[..., None], (count, per * 8, 128))
-    payload = jnp.concatenate([flat, tags], axis=1)
-    pieces = lax.all_to_all(payload, axis, 0, 0, tiled=True)
-    chosen = pieces[:, body_rows::8, 0]
-    pieces = pieces[:, :body_rows, :].reshape(count, per, -1)
+    tags = jnp.broadcast_to(logs[targets % heads][..., None], (count, per, 128))
+    chosen = lax.all_to_all(tags, axis, 0, 0, tiled=True)[:, :, 0]
+    pieces = lax.all_to_all(flat, axis, 0, 0, tiled=True).reshape(count, per, -1)
     position = jnp.arange(count)
     low = jnp.minimum(position[:, None], position[None, :])
     high = jnp.maximum(position[:, None], position[None, :])

time: 156 us -> 161 us (1.032)
  starting transfers between devices: 26.8 us -> 34.6 us
  waiting for transfers between devices: 84.9 us -> 80.1 us
  local copies, waits for them, and re-layouts: 15.9 us -> 17.8 us
    all_to_all x1 -> x2, starting transfers between devices: 11.9 us -> 18.8 us  [the longest x1 11.9 us: seq_scan(): chosen = lax.all_to_all(tags, axis, 0, 0, tiled=True)[:, :, 0]]
    all_to_all x1 -> x2, waiting for transfers between devices: 51.1 us -> 47.3 us  [the longest x1 45.1 us: seq_scan(): lax.all_to_all(flat, axis, 0, 0, tiled=True).reshape(count, per, -1)]
    unnamed x39 -> x37, local copies, waits for them, and re-layouts: 6.97 us -> 7.8 us
  transfers between devices with their start and end apart: 3 -> 4, of which waited for: 3 -> 4; matrix products, arithmetic and copies ran while one was open for 12% -> 17% of each run, Pallas kernels for 0% -> 0%
where the time goes in v10:
time: 161 us; the launch traced here: 160 us
  waiting for transfers between devices  80.1 us (50%)
  starting transfers between devices  34.6 us (21%)
  local copies, waits for them, and re-layouts  17.8 us (11%)
  matrix products  14.9 us (9%)
  other arithmetic  11.4 us (7%)
    all_to_all x1, waiting for transfers between devices, seq_scan(): lax.all_to_all(flat, axis, 0, 0, tiled=True).reshape(count, per, -1)  45.1 us
    all_to_all x1, waiting for transfers between devices, seq_scan(): lax.all_to_all(scanned.reshape(count, body_rows, 128), axis, 0, 0, tiled=...  30.7 us
    all_to_all x1, starting transfers between devices, seq_scan(): chosen = lax.all_to_all(tags, axis, 0, 0, tiled=True)[:, :, 0]  11.9 us
    all_to_all x1, starting transfers between devices, body(): lax.all_to_all(grad_step, 'tp', split_axis=0, concat_axis=1, tiled=True)  9.01 us
    unnamed x37, local copies, waits for them, and re-layouts  7.8 us
    all_to_all x1, starting transfers between devices, seq_scan(): lax.all_to_all(flat, axis, 0, 0, tiled=True).reshape(count, per, -1)  6.99 us
    all_to_all x1, starting transfers between devices, seq_scan(): lax.all_to_all(scanned.reshape(count, body_rows, 128), axis, 0, 0, tiled=...  6.71 us
  transfers between devices with their start and end apart: 4, of which 4 were waited for; matrix products, arithmetic and copies ran while one was open for 17% of the time, Pallas kernels for 0%

profile of v10, /device:TPU:1, one launch (start us, length us, event | category | flops | bytes accessed | tf_op | source)
XLA Modules:
  0.0 159.6 jit_solution(638808261927040983)
XLA Ops:
  4.4 11.9 %all-to-all-start.1 = ((f32[32,1,128]{2,1,0:T(1,128)}), f32[32,1,128]{2,1,0:T(1,128)S(1)}, u32[]{:S(2)}, u32[]{:S(2)}) async-start(f32[32,1,128]{2,1,0:T(1,128)} %broadcast_in_dim.23), calls=%async_computation.1 | async-start | bytes 32768 | tf_op jit(solution)/shard_map/all_to_all | solution.py:53
  16.3 1.4 fusion.61
  17.7 1.1 copy.66
  18.9 1.2 copy.65
  21.1 1.5 pad_maximum_fusion
  22.6 2.2 %all-to-all-done.1 = f32[32,1,128]{2,1,0:T(1,128)S(1)} async-done(((f32[32,1,128]{2,1,0:T(1,128)}), f32[32,1,128]{2,1,0:T(1,128)S(1)}, u32[]{:S(2)}, u32[]{:S(2)}) %all-to-all-start.1) | async-done | bytes 16416 | tf_op jit(solution)/shard_map/all_to_all | solution.py:53
  25.4 7.0 %all-to-all-start = ((f32[32,128,128]{2,1,0:T(8,128)}), f32[32,128,128]{2,1,0:T(8,128)S(1)}, u32[]{:S(2)}, u32[]{:S(2)}) async-start(f32[32,128,128]{2,1,0:T(8,128)} %bitcast.25), calls=%async_computation | async-start | bytes 4194304 | tf_op jit(solution)/shard_map/all_to_all | solution.py:54
  32.5 1.0 slice_reduce_fusion
  33.5 1.8 %fusion.41 = f32[1,32,32]{2,0,1:T(1,128)} fusion(s32[32,32]{1,0:T(8,128)S(1)} %get-tuple-element.32, s32[32,32]{1,0:T(8,128)S(1)} %get-tuple-element.33, f32[32]{0:T(128)S(1)} %slice_reduce_fusion), kind=kOutput, calls=%fused_computation.64 | convolution fusion | flops 491520 | bytes 12416 | tf_op jit(solution)/shard_map/ijm,mc->cij/dot_general | solution.py:59
  35.3 45.1 %all-to-all-done = f32[32,128,128]{2,1,0:T(8,128)S(1)} async-done(((f32[32,128,128]{2,1,0:T(8,128)}), f32[32,128,128]{2,1,0:T(8,128)S(1)}, u32[]{:S(2)}, u32[]{:S(2)}) %all-to-all-start) | async-done | bytes 2097184 | tf_op jit(solution)/shard_map/all_to_all | solution.py:54
  80.4 2.9 %fusion.3 = f32[4,8,128,128]{3,1,2,0:T(8,128)S(1)} fusion(f32[4,8,128,128]{3,2,1,0:T(8,128)S(1)} %bitcast.197, f32[32,32]{1,0:T(8,128)} %bitcast.213, pred[]{:T(512)S(6)} %lt.49), kind=kOutput, calls=%fused_computation.5 | convolution fusion | flops 100667392 | bytes 4198401 | tf_op jit(solution)/shard_map/cij,jcx->icx/dot_general | solution.py:64
  83.3 1.7 %copy.89 = f32[4,8,128,128]{3,2,1,0:T(8,128)} copy(f32[4,8,128,128]{3,1,2,0:T(8,128)S(1)} %fusion.3) | data formatting | bytes 4194304
  85.0 6.7 %all-to-all-start.2 = ((f32[32,128,128]{2,1,0:T(8,128)}), f32[32,128,128]{2,1,0:T(8,128)S(1)}, u32[]{:S(2)}, u32[]{:S(2)}) async-start(f32[32,128,128]{2,1,0:T(8,128)} %bitcast.198), calls=%async_computation.2 | async-start | bytes 4194304 | tf_op jit(solution)/shard_map/all_to_all | solution.py:65
  92.5 1.6 copy.64
  94.8 3.1 %broadcast_multiply_fusion = (f32[128,128,1,16]{1,0,3,2:T(8,128)}, f32[128,128]{1,0:T(8,128)}) fusion(f32[128,128]{1,0:T(8,128)} %copy.64, f32[128,16]{0,1:T(8,128)} %param.11, bf16[128,16,64]{0,2,1:T(8,128)(2,1)} %bitcast.206, bf16[128,16,64]{0,2,1:T(8,128)(2,1)S(1)} %bitcast.203, f32[128,128]{1,0:T(8,128)S(1)} %fusion.49, f32[128,16]{0,1:T(8,128)S(1)} %bitcast.211), kind=kOutput, calls=%fused_computation.55 | convolution fusion | flops 35373056 | bytes 1785856 | tf_op jit(solution)/shard_map/ughp,sghp->usgh/dot_general | solution.py:105
  97.9 2.6 %copy.72 = f32[128,128,1,16]{0,3,1,2:T(8,128)} copy(f32[128,128,1,16]{1,0,3,2:T(8,128)} %get-tuple-element.22) | data formatting | bytes 2097152 | tf_op jit(solution)/shard_map/mul | solution.py:114
  100.5 2.3 %fusion.63 = f32[128,128,1,16]{0,3,1,2:T(8,128)} fusion(f32[128,128,1,16]{0,3,1,2:T(8,128)} %copy.72), kind=kOutput, calls=%fused_computation.98 | output fusion | flops 33292288 | bytes 2097152 | tf_op jit(solution)/shard_map/jit(cumsum)/reduce_window_sum | solution.py:115
  102.8 2.6 %copy.73 = f32[128,128,1,16]{1,0,3,2:T(8,128)} copy(f32[128,128,1,16]{0,3,1,2:T(8,128)} %fusion.63) | data formatting | bytes 2097152 | tf_op jit(solution)/shard_map/jit(cumsum)/reduce_window_sum | solution.py:115
  105.4 2.3 %multiply_reduce_fusion = f32[128,16]{0,1:T(8,128)} fusion(f32[128,128,1,16]{1,0,3,2:T(8,128)} %copy.73, f32[128,128,1,16]{1,0,3,2:T(8,128)} %get-tuple-element.22, f32[128,128]{1,0:T(8,128)} %copy-done.6), kind=kLoop, calls=%fused_computation.38 | loop fusion | flops 784384 | bytes 2170880 | tf_op jit(solution)/shard_map/reduce_sum | solution.py:116
  107.7 30.7 %all-to-all-done.2 = f32[32,128,128]{2,1,0:T(8,128)S(1)} async-done(((f32[32,128,128]{2,1,0:T(8,128)}), f32[32,128,128]{2,1,0:T(8,128)S(1)}, u32[]{:S(2)}, u32[]{:S(2)}) %all-to-all-start.2) | async-done | bytes 2097184 | tf_op jit(solution)/shard_map/all_to_all | solution.py:65
  138.3 1.2 convolution_bitcast_fusion.9
  144.0 9.0 %all-to-all-start.3 = ((f32[8,1,256]{2,1,0:T(1,128)}), f32[8,1,256]{2,1,0:T(1,128)S(1)}, u32[]{:S(2)}, u32[]{:S(2)}) async-start(f32[8,1,256]{2,1,0:T(1,128)} %reshape.367), calls=%async_computation.3 | async-start | bytes 16384 | tf_op jit(solution)/shard_map/all_to_all | solution.py:213
  153.9 0.9 fusion.15
  155.6 2.1 %all-to-all-done.3 = f32[8,1,256]{2,1,0:T(1,128)S(1)} async-done(((f32[8,1,256]{2,1,0:T(1,128)}), f32[8,1,256]{2,1,0:T(1,128)S(1)}, u32[]{:S(2)}, u32[]{:S(2)}) %all-to-all-start.3) | async-done | bytes 8224 | tf_op jit(solution)/shard_map/all_to_all | solution.py:213
  (62 shorter events, 14.8 us)
Async XLA Ops:
  0.6 19.6 %copy-start = (bf16[128,256]{1,0:T(8,128)(2,1)S(1)}, bf16[128,256]{1,0:T(8,128)(2,1)}, u32[]{:S(2)}) copy-start(bf16[128,256]{1,0:T(8,128)(2,1)} %param.9) | copy-start | bytes 196612
  3.0 17.1 %copy-start.8 = (f32[128,1,16]{2,1,0:T(1,128)}, f32[128,1,16]{2,1,0:T(1,128)S(1)}, u32[]{:S(2)}) copy-start(f32[128,1,16]{2,1,0:T(1,128)S(1)} %fusion.62) | copy-start | bytes 24580
  4.4 20.4 %all-to-all-start.1 = ((f32[32,1,128]{2,1,0:T(1,128)}), f32[32,1,128]{2,1,0:T(1,128)S(1)}, u32[]{:S(2)}, u32[]{:S(2)}) async-start(f32[32,1,128]{2,1,0:T(1,128)} %broadcast_in_dim.23), calls=%async_computation.1 | async-start | bytes 32768 | tf_op jit(solution)/shard_map/all_to_all | solution.py:53
  17.7 2.9 %copy-start.3 = (bf16[128,256]{1,0:T(8,128)(2,1)S(1)}, bf16[128,256]{1,0:T(8,128)(2,1)}, u32[]{:S(2)}) copy-start(bf16[128,256]{1,0:T(8,128)(2,1)} %param.10) | copy-start | bytes 196612
  18.9 2.2 %copy-start.1 = (bf16[128,1024]{0,1:T(8,128)(2,1)}, bf16[128,1024]{0,1:T(8,128)(2,1)S(1)}, u32[]{:S(2)}) copy-start(bf16[128,1024]{0,1:T(8,128)(2,1)S(1)} %copy.66) | copy-start | bytes 786436
  24.8 0.6 copy-start.10
  25.4 55.0 %all-to-all-start = ((f32[32,128,128]{2,1,0:T(8,128)}), f32[32,128,128]{2,1,0:T(8,128)S(1)}, u32[]{:S(2)}, u32[]{:S(2)}) async-start(f32[32,128,128]{2,1,0:T(8,128)} %bitcast.25), calls=%async_computation | async-start | bytes 4194304 | tf_op jit(solution)/shard_map/all_to_all | solution.py:54
  85.0 53.3 %all-to-all-start.2 = ((f32[32,128,128]{2,1,0:T(8,128)}), f32[32,128,128]{2,1,0:T(8,128)S(1)}, u32[]{:S(2)}, u32[]{:S(2)}) async-start(f32[32,128,128]{2,1,0:T(8,128)} %bitcast.198), calls=%async_computation.2 | async-start | bytes 4194304 | tf_op jit(solution)/shard_map/all_to_all | solution.py:65
  94.1 0.6 copy-start.6
  139.6 0.9 copy-start.2
  140.5 1.6 %copy-start.11 = (f32[128,16]{0,1:T(8,128)S(1)}, f32[128,16]{0,1:T(8,128)}, u32[]{:S(2)}) copy-start(f32[128,16]{0,1:T(8,128)} %multiply_reduce_fusion) | copy-start | bytes 24580
  140.5 1.8 %copy-start.7 = (f32[128,128]{1,0:T(8,128)S(1)}, f32[128,128]{1,0:T(8,128)}, u32[]{:S(2)}) copy-start(f32[128,128]{1,0:T(8,128)} %copy-done.6) | copy-start | bytes 196612
  140.5 1.8 %copy-start.9 = (f32[128,128]{1,0:T(8,128)S(1)}, f32[128,128]{1,0:T(8,128)}, u32[]{:S(2)}) copy-start(f32[128,128]{1,0:T(8,128)} %copy.64) | copy-start | bytes 196612
  140.5 1.8 %copy-start.12 = (f32[128,16]{0,1:T(8,128)S(1)}, f32[128,16]{0,1:T(8,128)}, u32[]{:S(2)}) copy-start(f32[128,16]{0,1:T(8,128)} %param.11) | copy-start | bytes 24580
  140.5 1.8 %copy-start.13 = (f32[128,16]{0,1:T(8,128)S(1)}, f32[128,16]{0,1:T(8,128)}, u32[]{:S(2)}) copy-start(f32[128,16]{0,1:T(8,128)} %get-tuple-element.21) | copy-start | bytes 24580
  141.0 2.1 %copy-start.14 = (f32[16]{0:T(128)S(1)}, f32[16]{0:T(128)}, u32[]{:S(2)}) copy-start(f32[16]{0:T(128)} %param.12) | copy-start | bytes 196
  141.7 11.4 %copy-start.5 = (f32[128,128]{1,0:T(8,128)S(1)}, f32[128,128]{1,0:T(8,128)}, u32[]{:S(2)}) copy-start(f32[128,128]{1,0:T(8,128)} %get-tuple-element.23) | copy-start | bytes 196612
  141.7 12.2 %copy-start.4 = (f32[256,128]{0,1:T(8,128)S(1)}, f32[256,128]{0,1:T(8,128)}, u32[]{:S(2)}) copy-start(f32[256,128]{0,1:T(8,128)} %convolution_bitcast_fusion.9) | copy-start | bytes 393220
  144.0 13.6 %all-to-all-start.3 = ((f32[8,1,256]{2,1,0:T(1,128)}), f32[8,1,256]{2,1,0:T(1,128)S(1)}, u32[]{:S(2)}, u32[]{:S(2)}) async-start(f32[8,1,256]{2,1,0:T(1,128)} %reshape.367), calls=%async_computation.3 | async-start | bytes 16384 | tf_op jit(solution)/shard_map/all_to_all | solution.py:213

commit v11 on v9

--- a/solution.py
+++ b/solution.py
@@ -74,20 +74,16 @@
     cumulative = jnp.cumsum(-decay_rate[None] * step_size, axis=0)
     totals = cumulative[-1]
     to_end = jnp.exp(totals[None] - cumulative) * step_size
-    forward = jnp.einsum(
-        "qghp,qgn->gnhp",
-        inputs.astype(jnp.float32) * to_end[..., None],
-        input_proj.astype(jnp.float32),
-        precision=fast,
-    )
     from_start = jnp.exp(cumulative)
-    backward = jnp.einsum(
-        "qghp,qgn->gnhp",
-        out_grad.astype(jnp.float32) * from_start[..., None],
-        readout.astype(jnp.float32),
-        precision=fast,
-    )
-    return (totals, forward, backward)
+    scaled = jnp.stack(
+        [
+            inputs.astype(jnp.float32) * to_end[..., None],
+            out_grad.astype(jnp.float32) * from_start[..., None],
+        ]
+    )
+    vectors = jnp.stack([input_proj.astype(jnp.float32), readout.astype(jnp.float32)])
+    both = jnp.einsum("fqghp,fqgn->fgnhp", scaled, vectors, precision=fast)
+    return (totals, both[0], both[1])
 
 
 def span_local(inputs_raw, out_raw, proj_raw, read_raw, step_size, decay_rate):

time: 156 us -> 154 us (0.987)
  matrix products: 14.5 us -> 11.2 us
  waiting for transfers between devices: 84.9 us -> 87.5 us
    all_to_all x1, waiting for transfers between devices: 31.7 us -> 34.3 us  [seq_scan(): lax.all_to_all(scanned.reshape(count, body_rows, 128), axis, 0, 0, tiled=...]
    unnamed x39 -> x35, local copies, waits for them, and re-layouts: 6.97 us -> 7.35 us
  transfers between devices with their start and end apart: 3 -> 3, of which waited for: 3 -> 3; matrix products, arithmetic and copies ran while one was open for 12% -> 10% of each run, Pallas kernels for 0% -> 0%
where the time goes in v11:
time: 154 us
  waiting for transfers between devices  87.5 us (57%)
  starting transfers between devices  26.7 us (17%)
  local copies, waits for them, and re-layouts  15 us (10%)
  other arithmetic  12.2 us (8%)
  matrix products  11.2 us (7%)
    all_to_all x1, waiting for transfers between devices, seq_scan(): pieces = lax.all_to_all(payload, axis, 0, 0, tiled=True)  51.1 us
    all_to_all x1, waiting for transfers between devices, seq_scan(): lax.all_to_all(scanned.reshape(count, body_rows, 128), axis, 0, 0, tiled=...  34.3 us
    all_to_all x1, starting transfers between devices, seq_scan(): pieces = lax.all_to_all(payload, axis, 0, 0, tiled=True)  11.9 us
    all_to_all x1, starting transfers between devices, body(): lax.all_to_all(grad_step, 'tp', split_axis=0, concat_axis=1, tiled=True)  7.91 us
    unnamed x35, local copies, waits for them, and re-layouts  7.35 us
    all_to_all x1, starting transfers between devices, seq_scan(): lax.all_to_all(scanned.reshape(count, body_rows, 128), axis, 0, 0, tiled=...  6.9 us
  transfers between devices with their start and end apart: 3, of which 3 were waited for; matrix products, arithmetic and copies ran while one was open for 10% of the time, Pallas kernels for 0%

profile of v11, /device:TPU:1, one launch (start us, length us, event | category | flops | bytes accessed | tf_op | source)
XLA Modules:
  0.0 153.6 jit_solution(2090742570242875852)
XLA Ops:
  1.3 0.8 multiply_bitcast_fusion
  2.4 1.1 copy.68
  4.3 1.1 copy.67
  7.7 0.7 fusion.45
  9.0 1.6 %pad_maximum_fusion = f32[32,136,128]{2,1,0:T(8,128)} fusion(f32[32,8,128]{2,1,0:T(8,128)S(1)} %broadcast_in_dim.13, f32[32,128,128]{2,1,0:T(8,128)S(1)} %bitcast.198), kind=kLoop, calls=%fused_computation.1 | loop fusion | flops 557056 | bytes 4456448 | tf_op jit(solution)/shard_map/concatenate | solution.py:54
  10.5 11.9 %all-to-all-start = ((f32[32,136,128]{2,1,0:T(8,128)}), f32[32,136,128]{2,1,0:T(8,128)S(1)}, u32[]{:S(2)}, u32[]{:S(2)}) async-start(f32[32,136,128]{2,1,0:T(8,128)} %pad_maximum_fusion), calls=%async_computation | async-start | bytes 4456448 | tf_op jit(solution)/shard_map/all_to_all | solution.py:55
  22.4 51.1 %all-to-all-done = f32[32,136,128]{2,1,0:T(8,128)S(1)} async-done(((f32[32,136,128]{2,1,0:T(8,128)}), f32[32,136,128]{2,1,0:T(8,128)S(1)}, u32[]{:S(2)}, u32[]{:S(2)}) %all-to-all-start) | async-done | bytes 2228256 | tf_op jit(solution)/shard_map/all_to_all | solution.py:55
  73.8 1.2 fusion.41
  75.3 2.2 %fusion.3 = f32[4,8,128,128]{3,1,2,0:T(8,128)S(1)} fusion(f32[4,8,128,128]{3,2,1,0:T(8,128)S(1)} %bitcast.200, f32[32,32]{1,0:T(8,128)S(1)} %bitcast.218, pred[]{:T(512)S(6)} %lt.49), kind=kOutput, calls=%fused_computation.6 | convolution fusion | flops 100667392 | bytes 4198401 | tf_op jit(solution)/shard_map/cij,jcx->icx/dot_general | solution.py:67
  77.5 1.7 %copy.91 = f32[4,8,128,128]{3,2,1,0:T(8,128)} copy(f32[4,8,128,128]{3,1,2,0:T(8,128)S(1)} %fusion.3) | data formatting | bytes 4194304
  79.2 6.9 %all-to-all-start.1 = ((f32[32,128,128]{2,1,0:T(8,128)}), f32[32,128,128]{2,1,0:T(8,128)S(1)}, u32[]{:S(2)}, u32[]{:S(2)}) async-start(f32[32,128,128]{2,1,0:T(8,128)} %bitcast.197), calls=%async_computation.1 | async-start | bytes 4194304 | tf_op jit(solution)/shard_map/all_to_all | solution.py:68
  86.1 1.1 bitcast_multiply_fusion.1
  87.5 2.3 %broadcast_multiply_fusion = (f32[128,128,1,16]{1,0,3,2:T(8,128)}, f32[128,128]{1,0:T(8,128)S(1)}) fusion(f32[128,128]{1,0:T(8,128)S(1)} %copy.66, f32[128,16]{0,1:T(8,128)} %param.11, bf16[128,16,64]{0,2,1:T(8,128)(2,1)S(1)} %bitcast.204, bf16[128,16,64]{0,2,1:T(8,128)(2,1)S(1)} %bitcast.205, f32[128,128]{1,0:T(8,128)S(1)} %fusion.50, ...), kind=kOutput, calls=%fused_computation.57 | convolution fusion | flops 35373056 | bytes 1785856 | tf_op jit(solution)/shard_map/ughp,sghp->usgh/dot_general | solution.py:104
  89.7 2.6 %copy.74 = f32[128,128,1,16]{0,3,1,2:T(8,128)} copy(f32[128,128,1,16]{1,0,3,2:T(8,128)} %get-tuple-element.24) | data formatting | bytes 2097152 | tf_op jit(solution)/shard_map/mul | solution.py:113
  92.3 2.3 %fusion.65 = f32[128,128,1,16]{0,3,1,2:T(8,128)} fusion(f32[128,128,1,16]{0,3,1,2:T(8,128)} %copy.74), kind=kOutput, calls=%fused_computation.105 | output fusion | flops 33292288 | bytes 2097152 | tf_op jit(solution)/shard_map/jit(cumsum)/reduce_window_sum | solution.py:114
  94.7 2.6 %copy.75 = f32[128,128,1,16]{1,0,3,2:T(8,128)} copy(f32[128,128,1,16]{0,3,1,2:T(8,128)} %fusion.65) | data formatting | bytes 2097152 | tf_op jit(solution)/shard_map/jit(cumsum)/reduce_window_sum | solution.py:114
  97.2 2.3 %multiply_reduce_fusion = f32[128,16]{0,1:T(8,128)} fusion(f32[128,128,1,16]{1,0,3,2:T(8,128)} %copy.75, f32[128,128,1,16]{1,0,3,2:T(8,128)} %get-tuple-element.24, f32[128,128]{1,0:T(8,128)S(1)} %fusion.50), kind=kLoop, calls=%fused_computation.40 | loop fusion | flops 784384 | bytes 2170880 | tf_op jit(solution)/shard_map/reduce_sum | solution.py:115
  99.5 34.3 %all-to-all-done.1 = f32[32,128,128]{2,1,0:T(8,128)S(1)} async-done(((f32[32,128,128]{2,1,0:T(8,128)}), f32[32,128,128]{2,1,0:T(8,128)S(1)}, u32[]{:S(2)}, u32[]{:S(2)}) %all-to-all-start.1) | async-done | bytes 2097184 | tf_op jit(solution)/shard_map/all_to_all | solution.py:68
  137.4 0.7 multiply_reduce_fusion.2
  139.1 7.9 %all-to-all-start.2 = ((f32[8,1,256]{2,1,0:T(1,128)}), f32[8,1,256]{2,1,0:T(1,128)S(1)}, u32[]{:S(2)}, u32[]{:S(2)}) async-start(f32[8,1,256]{2,1,0:T(1,128)} %reshape.399), calls=%async_computation.2 | async-start | bytes 16384 | tf_op jit(solution)/shard_map/all_to_all | solution.py:212
  147.0 0.9 fusion.15
  147.9 0.8 fusion.14
  148.7 0.8 copy.77
  149.5 2.1 %all-to-all-done.2 = f32[8,1,256]{2,1,0:T(1,128)S(1)} async-done(((f32[8,1,256]{2,1,0:T(1,128)}), f32[8,1,256]{2,1,0:T(1,128)S(1)}, u32[]{:S(2)}, u32[]{:S(2)}) %all-to-all-start.2) | async-done | bytes 8224 | tf_op jit(solution)/shard_map/all_to_all | solution.py:212
  (64 shorter events, 11.7 us)
Async XLA Ops:
  0.6 5.5 %copy-start.10 = (f32[128,16]{0,1:T(8,128)S(1)}, f32[128,16]{0,1:T(8,128)}, u32[]{:S(2)}) copy-start(f32[128,16]{0,1:T(8,128)} %param.11) | copy-start | bytes 24580
  2.3 2.0 %copy-start.6 = (f32[128,1,16]{2,1,0:T(1,128)}, f32[128,1,16]{2,1,0:T(1,128)S(1)}, u32[]{:S(2)}) copy-start(f32[128,1,16]{2,1,0:T(1,128)S(1)} %fusion.64) | copy-start | bytes 24580
  3.6 3.5 %copy-start.2 = (f32[128,1024]{0,1:T(8,128)}, f32[128,1024]{0,1:T(8,128)S(1)}, u32[]{:S(2)}) copy-start(f32[128,1024]{0,1:T(8,128)S(1)} %convert_element_type.142) | copy-start | bytes 1572868
  6.8 0.8 copy-start.4
  6.8 0.9 copy-start.5
  10.5 63.0 %all-to-all-start = ((f32[32,136,128]{2,1,0:T(8,128)}), f32[32,136,128]{2,1,0:T(8,128)S(1)}, u32[]{:S(2)}, u32[]{:S(2)}) async-start(f32[32,136,128]{2,1,0:T(8,128)} %pad_maximum_fusion), calls=%async_computation | async-start | bytes 4456448 | tf_op jit(solution)/shard_map/all_to_all | solution.py:55
  79.2 54.6 %all-to-all-start.1 = ((f32[32,128,128]{2,1,0:T(8,128)}), f32[32,128,128]{2,1,0:T(8,128)S(1)}, u32[]{:S(2)}, u32[]{:S(2)}) async-start(f32[32,128,128]{2,1,0:T(8,128)} %bitcast.197), calls=%async_computation.1 | async-start | bytes 4194304 | tf_op jit(solution)/shard_map/all_to_all | solution.py:68
  87.4 4.9 %copy-start.7 = (f32[128,128]{1,0:T(8,128)}, f32[128,128]{1,0:T(8,128)S(1)}, u32[]{:S(2)}) copy-start(f32[128,128]{1,0:T(8,128)S(1)} %copy.66) | copy-start | bytes 196612
  133.8 1.0 copy-start.1
  134.2 1.2 copy-start
  135.4 1.8 %copy-start.9 = (f32[128,16]{0,1:T(8,128)S(1)}, f32[128,16]{0,1:T(8,128)}, u32[]{:S(2)}) copy-start(f32[128,16]{0,1:T(8,128)} %multiply_reduce_fusion) | copy-start | bytes 24580
  135.4 1.9 %copy-start.3 = (f32[128,1024]{0,1:T(8,128)S(1)}, f32[128,1024]{0,1:T(8,128)}, u32[]{:S(2)}) copy-start(f32[128,1024]{0,1:T(8,128)} %copy-done.2) | copy-start | bytes 1572868
  135.4 1.9 %copy-start.8 = (f32[128,128]{1,0:T(8,128)S(1)}, f32[128,128]{1,0:T(8,128)}, u32[]{:S(2)}) copy-start(f32[128,128]{1,0:T(8,128)} %copy-done.7) | copy-start | bytes 196612
  135.5 1.9 %copy-start.11 = (f32[128,16]{0,1:T(8,128)S(1)}, f32[128,16]{0,1:T(8,128)}, u32[]{:S(2)}) copy-start(f32[128,16]{0,1:T(8,128)} %param.11) | copy-start | bytes 24580
  135.5 1.9 %copy-start.12 = (f32[128,16]{0,1:T(8,128)S(1)}, f32[128,16]{0,1:T(8,128)}, u32[]{:S(2)}) copy-start(f32[128,16]{0,1:T(8,128)} %get-tuple-element.21) | copy-start | bytes 24580
  136.1 2.0 %copy-start.13 = (f32[16]{0:T(128)S(1)}, f32[16]{0:T(128)}, u32[]{:S(2)}) copy-start(f32[16]{0:T(128)} %param.12) | copy-start | bytes 196
  139.1 12.5 %all-to-all-start.2 = ((f32[8,1,256]{2,1,0:T(1,128)}), f32[8,1,256]{2,1,0:T(1,128)S(1)}, u32[]{:S(2)}, u32[]{:S(2)}) async-start(f32[8,1,256]{2,1,0:T(1,128)} %reshape.399), calls=%async_computation.2 | async-start | bytes 16384 | tf_op jit(solution)/shard_map/all_to_all | solution.py:212

commit v12 on v11

--- a/solution.py
+++ b/solution.py
@@ -49,7 +49,7 @@
     tiled = (count, per, head_dim // 8, 8, state_dim // 128, 128)
     flat = stacked.reshape(tiled).transpose(0, 1, 2, 4, 3, 5).reshape(count, -1, 128)
     body_rows = flat.shape[1]
-    tags = jnp.repeat(logs[targets % heads], 8, axis=1)
+    tags = jnp.repeat(jnp.stack([logs[i % heads] for i in targets.reshape(-1)]).reshape(targets.shape), 8, axis=1)
     tags = jnp.broadcast_to(tags[..., None], (count, per * 8, 128))
     payload = jnp.concatenate([flat, tags], axis=1)
     pieces = lax.all_to_all(payload, axis, 0, 0, tiled=True)

time: 154 us -> 174 us (1.13)
  local copies, waits for them, and re-layouts: 15 us -> 35.9 us
    another operation x0 -> x1, local copies, waits for them, and re-layouts: none -> 20.7 us  [seq_scan(): jnp.stack([logs[i % heads] for i in targets.reshape(-1)])]
    unnamed x35 -> x37, local copies, waits for them, and re-layouts: 7.35 us -> 7.55 us
  transfers between devices with their start and end apart: 3 -> 3, of which waited for: 3 -> 3; matrix products, arithmetic and copies ran while one was open for 10% -> 9% of each run, Pallas kernels for 0% -> 0%
where the time goes in v12:
time: 174 us; the launch traced here: 173 us
  waiting for transfers between devices  87.4 us (50%)
  local copies, waits for them, and re-layouts  35.9 us (21%)
  starting transfers between devices  26.6 us (15%)
  matrix products  11.2 us (6%)
  other arithmetic  10.8 us (6%)
    all_to_all x1, waiting for transfers between devices, seq_scan(): pieces = lax.all_to_all(payload, axis, 0, 0, tiled=True)  51.1 us
    all_to_all x1, waiting for transfers between devices, seq_scan(): lax.all_to_all(scanned.reshape(count, body_rows, 128), axis, 0, 0, tiled=...  34.3 us
    another operation x1, local copies, waits for them, and re-layouts, seq_scan(): jnp.stack([logs[i % heads] for i in targets.reshape(-1)])  20.7 us
    all_to_all x1, starting transfers between devices, seq_scan(): pieces = lax.all_to_all(payload, axis, 0, 0, tiled=True)  11.9 us
    all_to_all x1, starting transfers between devices, body(): lax.all_to_all(grad_step, 'tp', split_axis=0, concat_axis=1, tiled=True)  7.9 us
    unnamed x37, local copies, waits for them, and re-layouts  7.55 us
    all_to_all x1, starting transfers between devices, seq_scan(): lax.all_to_all(scanned.reshape(count, body_rows, 128), axis, 0, 0, tiled=...  6.9 us
  transfers between devices with their start and end apart: 3, of which 3 were waited for; matrix products, arithmetic and copies ran while one was open for 9% of the time, Pallas kernels for 0%

profile of v12, /device:TPU:1, one launch (start us, length us, event | category | flops | bytes accessed | tf_op | source)
XLA Modules:
  0.0 173.0 jit_solution(4269076398205824880)
XLA Ops:
  1.3 0.8 multiply_bitcast_fusion
  3.1 1.1 copy.66
  4.3 1.3 copy.65
  7.2 0.7 fusion.45
  8.3 20.7 %stack.28 = f32[32]{0:T(128)S(1)} concatenate(f32[1]{0:T(128)} %bitcast.26, f32[1]{0:T(128)} %bitcast.27, f32[1]{0:T(128)} %bitcast.28, f32[1]{0:T(128)} %bitcast.29, f32[1]{0:T(128)} %bitcast.30, f32[1]{0:T(128)} %bitcast.31, f32[1]{0:T(128)} %bitcast.32, f32[1]{0:T(128)} %bitcast.33, f32[1]{0:T(128)} %bitcast.34, f32[1]{0:T(128)} %bitcast.35, f32[1]{0:T(128)} %bitcast.36, ...), dimensions={0} | concatenate | bytes 256 | tf_op jit(solution)/shard_map/stack | solution.py:52
  29.1 1.6 pad_maximum_fusion
  30.6 11.9 %all-to-all-start = ((f32[32,136,128]{2,1,0:T(8,128)}), f32[32,136,128]{2,1,0:T(8,128)S(1)}, u32[]{:S(2)}, u32[]{:S(2)}) async-start(f32[32,136,128]{2,1,0:T(8,128)} %pad_maximum_fusion), calls=%async_computation | async-start | bytes 4456448 | tf_op jit(solution)/shard_map/all_to_all | solution.py:55
  42.5 51.1 %all-to-all-done = f32[32,136,128]{2,1,0:T(8,128)S(1)} async-done(((f32[32,136,128]{2,1,0:T(8,128)}), f32[32,136,128]{2,1,0:T(8,128)S(1)}, u32[]{:S(2)}, u32[]{:S(2)}) %all-to-all-start) | async-done | bytes 2228256 | tf_op jit(solution)/shard_map/all_to_all | solution.py:55
  93.9 1.2 fusion.41
  95.4 2.2 %fusion.3 = f32[4,8,128,128]{3,1,2,0:T(8,128)S(1)} fusion(f32[4,8,128,128]{3,2,1,0:T(8,128)S(1)} %bitcast.216, f32[32,32]{1,0:T(8,128)S(1)} %bitcast.234, pred[]{:T(512)S(6)} %lt.49), kind=kOutput, calls=%fused_computation.5 | convolution fusion | flops 100667392 | bytes 4198401 | tf_op jit(solution)/shard_map/cij,jcx->icx/dot_general | solution.py:67
  97.6 1.7 copy.89
  99.3 6.9 %all-to-all-start.1 = ((f32[32,128,128]{2,1,0:T(8,128)}), f32[32,128,128]{2,1,0:T(8,128)S(1)}, u32[]{:S(2)}, u32[]{:S(2)}) async-start(f32[32,128,128]{2,1,0:T(8,128)} %bitcast.213), calls=%async_computation.1 | async-start | bytes 4194304 | tf_op jit(solution)/shard_map/all_to_all | solution.py:68
  106.2 1.1 bitcast_multiply_fusion.1
  107.6 2.3 %broadcast_multiply_fusion = (f32[128,128,1,16]{1,0,3,2:T(8,128)}, f32[128,128]{1,0:T(8,128)S(1)}) fusion(f32[128,128]{1,0:T(8,128)S(1)} %copy.64, f32[128,16]{0,1:T(8,128)} %param.9, bf16[128,16,64]{0,2,1:T(8,128)(2,1)S(1)} %bitcast.220, bf16[128,16,64]{0,2,1:T(8,128)(2,1)S(1)} %bitcast.221, f32[128,128]{1,0:T(8,128)S(1)} %fusion.50, ...), kind=kOutput, calls=%fused_computation.56 | convolution fusion | flops 35373056 | bytes 1785856 | tf_op jit(solution)/shard_map/ughp,sghp->usgh/dot_general | solution.py:104
  109.9 2.6 %copy.72 = f32[128,128,1,16]{0,3,1,2:T(8,128)} copy(f32[128,128,1,16]{1,0,3,2:T(8,128)} %get-tuple-element.24) | data formatting | bytes 2097152 | tf_op jit(solution)/shard_map/mul | solution.py:113
  112.5 2.3 %fusion.66 = f32[128,128,1,16]{0,3,1,2:T(8,128)} fusion(f32[128,128,1,16]{0,3,1,2:T(8,128)} %copy.72), kind=kOutput, calls=%fused_computation.104 | output fusion | flops 33292288 | bytes 2097152 | tf_op jit(solution)/shard_map/jit(cumsum)/reduce_window_sum | solution.py:114
  114.8 2.5 %copy.73 = f32[128,128,1,16]{1,0,3,2:T(8,128)} copy(f32[128,128,1,16]{0,3,1,2:T(8,128)} %fusion.66) | data formatting | bytes 2097152 | tf_op jit(solution)/shard_map/jit(cumsum)/reduce_window_sum | solution.py:114
  117.4 2.3 %multiply_reduce_fusion = f32[128,16]{0,1:T(8,128)} fusion(f32[128,128,1,16]{1,0,3,2:T(8,128)} %copy.73, f32[128,128,1,16]{1,0,3,2:T(8,128)} %get-tuple-element.24, f32[128,128]{1,0:T(8,128)S(1)} %fusion.50), kind=kLoop, calls=%fused_computation.39 | loop fusion | flops 784384 | bytes 2170880 | tf_op jit(solution)/shard_map/reduce_sum | solution.py:115
  119.6 34.3 %all-to-all-done.1 = f32[32,128,128]{2,1,0:T(8,128)S(1)} async-done(((f32[32,128,128]{2,1,0:T(8,128)}), f32[32,128,128]{2,1,0:T(8,128)S(1)}, u32[]{:S(2)}, u32[]{:S(2)}) %all-to-all-start.1) | async-done | bytes 2097184 | tf_op jit(solution)/shard_map/all_to_all | solution.py:68
  158.6 7.9 %all-to-all-start.2 = ((f32[8,1,256]{2,1,0:T(1,128)}), f32[8,1,256]{2,1,0:T(1,128)S(1)}, u32[]{:S(2)}, u32[]{:S(2)}) async-start(f32[8,1,256]{2,1,0:T(1,128)} %reshape.406), calls=%async_computation.2 | async-start | bytes 16384 | tf_op jit(solution)/shard_map/all_to_all | solution.py:212
  166.5 0.9 fusion.15
  167.3 0.8 fusion.14
  168.1 0.8 copy.75
  169.0 2.1 %all-to-all-done.2 = f32[8,1,256]{2,1,0:T(1,128)S(1)} async-done(((f32[8,1,256]{2,1,0:T(1,128)}), f32[8,1,256]{2,1,0:T(1,128)S(1)}, u32[]{:S(2)}, u32[]{:S(2)}) %all-to-all-start.2) | async-done | bytes 8224 | tf_op jit(solution)/shard_map/all_to_all | solution.py:212
  (66 shorter events, 11.0 us)
Async XLA Ops:
  0.6 5.0 %copy-start.11 = (f32[128,16]{0,1:T(8,128)S(1)}, f32[128,16]{0,1:T(8,128)}, u32[]{:S(2)}) copy-start(f32[128,16]{0,1:T(8,128)} %param.9) | copy-start | bytes 24580
  4.3 2.3 %copy-start.2 = (f32[128,1024]{0,1:T(8,128)}, f32[128,1024]{0,1:T(8,128)S(1)}, u32[]{:S(2)}) copy-start(f32[128,1024]{0,1:T(8,128)S(1)} %convert_element_type.142) | copy-start | bytes 1572868
  6.3 0.8 copy-start.4
  6.3 0.9 copy-start.5
  30.6 63.0 %all-to-all-start = ((f32[32,136,128]{2,1,0:T(8,128)}), f32[32,136,128]{2,1,0:T(8,128)S(1)}, u32[]{:S(2)}, u32[]{:S(2)}) async-start(f32[32,136,128]{2,1,0:T(8,128)} %pad_maximum_fusion), calls=%async_computation | async-start | bytes 4456448 | tf_op jit(solution)/shard_map/all_to_all | solution.py:55
  99.3 54.6 %all-to-all-start.1 = ((f32[32,128,128]{2,1,0:T(8,128)}), f32[32,128,128]{2,1,0:T(8,128)S(1)}, u32[]{:S(2)}, u32[]{:S(2)}) async-start(f32[32,128,128]{2,1,0:T(8,128)} %bitcast.213), calls=%async_computation.1 | async-start | bytes 4194304 | tf_op jit(solution)/shard_map/all_to_all | solution.py:68
  107.5 4.9 %copy-start.8 = (f32[128,128]{1,0:T(8,128)}, f32[128,128]{1,0:T(8,128)S(1)}, u32[]{:S(2)}) copy-start(f32[128,128]{1,0:T(8,128)S(1)} %copy.64) | copy-start | bytes 196612
  107.6 9.8 %copy-start.6 = (f32[128,128]{1,0:T(8,128)}, f32[128,128]{1,0:T(8,128)S(1)}, u32[]{:S(2)}) copy-start(f32[128,128]{1,0:T(8,128)S(1)} %fusion.50) | copy-start | bytes 196612
  153.9 1.0 copy-start.1
  154.3 1.3 copy-start
  155.5 1.2 copy-start.10
  155.5 1.3 copy-start.3
  155.6 1.3 copy-start.7
  155.6 1.3 copy-start.9
  155.6 1.3 copy-start.12
  155.6 1.3 copy-start.13
  156.2 1.4 copy-start.14
  158.6 12.5 %all-to-all-start.2 = ((f32[8,1,256]{2,1,0:T(1,128)}), f32[8,1,256]{2,1,0:T(1,128)S(1)}, u32[]{:S(2)}, u32[]{:S(2)}) async-start(f32[8,1,256]{2,1,0:T(1,128)} %reshape.406), calls=%async_computation.2 | async-start | bytes 16384 | tf_op jit(solution)/shard_map/all_to_all | solution.py:212

commit v13 on v11

--- a/solution.py
+++ b/solution.py
@@ -54,7 +54,7 @@
     payload = jnp.concatenate([flat, tags], axis=1)
     pieces = lax.all_to_all(payload, axis, 0, 0, tiled=True)
     chosen = pieces[:, body_rows::8, 0]
-    pieces = pieces[:, :body_rows, :].reshape(count, per, -1)
+    pieces = pieces[:, :body_rows, :].reshape(count, per, body_rows // per, 128)
     position = jnp.arange(count)
     low = jnp.minimum(position[:, None], position[None, :])
     high = jnp.maximum(position[:, None], position[None, :])
@@ -64,7 +64,7 @@
     after = (position[None, :] > position[:, None])
     mask = jnp.where((held < heads)[:, None, None], before[None], after[None])
     weights = jnp.where(mask, jnp.exp(exponent), 0.0)
-    scanned = jnp.einsum("cij,jcx->icx", weights, pieces, precision=fast)
+    scanned = jnp.sum(weights.transpose(1, 2, 0)[:, :, :, None, None] * pieces[None], axis=1)
     back = lax.all_to_all(scanned.reshape(count, body_rows, 128), axis, 0, 0, tiled=True)
     back = back.reshape(count, per, head_dim // 8, state_dim // 128, 8, 128).transpose(0, 1, 2, 4, 3, 5)
     back = back.reshape(shape).transpose(0, 1, 4, 2, 3)

time: 154 us -> 161 us (1.045)
  other arithmetic: 12.2 us -> 22.9 us
  matrix products: 11.2 us -> 9.01 us
  local copies, waits for them, and re-layouts: 15 us -> 13.3 us
    reduce_sum x0 -> x1, other arithmetic: none -> 10.7 us  [seq_scan(): jnp.sum(weights.transpose(1, 2, 0)[:, :, :, None, None] * pieces[None], a...]
    dot_general x1 -> x0, matrix products: 2.18 us -> none  [seq_scan(): scanned = jnp.einsum('cij,jcx->icx', weights, pieces, precision=fast)]
    unnamed x35 -> x34, local copies, waits for them, and re-layouts: 7.35 us -> 5.62 us
where the time goes in v13:
time: 161 us; the launch traced here: 160 us
  waiting for transfers between devices  87.5 us (54%)
  starting transfers between devices  26.7 us (17%)
  other arithmetic  22.9 us (14%)
  local copies, waits for them, and re-layouts  13.3 us (8%)
  matrix products  9.01 us (6%)
    all_to_all x1, waiting for transfers between devices, seq_scan(): pieces = lax.all_to_all(payload, axis, 0, 0, tiled=True)  51.1 us
    all_to_all x1, waiting for transfers between devices, seq_scan(): lax.all_to_all(scanned.reshape(count, body_rows, 128), axis, 0, 0, tiled=...  34.3 us
    all_to_all x1, starting transfers between devices, seq_scan(): pieces = lax.all_to_all(payload, axis, 0, 0, tiled=True)  11.9 us
    reduce_sum x1, other arithmetic, seq_scan(): jnp.sum(weights.transpose(1, 2, 0)[:, :, :, None, None] * pieces[None], a...  10.7 us
    all_to_all x1, starting transfers between devices, body(): lax.all_to_all(grad_step, 'tp', split_axis=0, concat_axis=1, tiled=True)  7.91 us
    all_to_all x1, starting transfers between devices, seq_scan(): lax.all_to_all(scanned.reshape(count, body_rows, 128), axis, 0, 0, tiled=...  6.89 us
    unnamed x34, local copies, waits for them, and re-layouts  5.62 us
  transfers between devices with their start and end apart: 3, of which 3 were waited for; matrix products, arithmetic and copies ran while one was open for 10% of the time, Pallas kernels for 0%

profile of v13, /device:TPU:1, one launch (start us, length us, event | category | flops | bytes accessed | tf_op | source)
XLA Modules:
  0.0 160.3 jit_solution(8766198285650503264)
XLA Ops:
  1.3 0.8 multiply_bitcast_fusion
  2.4 1.1 copy.85
  4.3 1.1 copy.84
  5.4 0.7 gather_fusion
  7.7 0.7 fusion.39
  9.0 1.6 pad_maximum_fusion
  10.5 11.9 %all-to-all-start = ((f32[32,136,128]{2,1,0:T(8,128)}), f32[32,136,128]{2,1,0:T(8,128)S(1)}, u32[]{:S(2)}, u32[]{:S(2)}) async-start(f32[32,136,128]{2,1,0:T(8,128)} %pad_maximum_fusion), calls=%async_computation | async-start | bytes 4456448 | tf_op jit(solution)/shard_map/all_to_all | solution.py:55
  22.4 51.1 %all-to-all-done = f32[32,136,128]{2,1,0:T(8,128)S(1)} async-done(((f32[32,136,128]{2,1,0:T(8,128)}), f32[32,136,128]{2,1,0:T(8,128)S(1)}, u32[]{:S(2)}, u32[]{:S(2)}) %all-to-all-start) | async-done | bytes 2228256 | tf_op jit(solution)/shard_map/all_to_all | solution.py:55
  73.8 1.2 fusion.35
  75.3 10.7 %multiply_reduce_fusion = f32[32,128,128]{2,1,0:T(8,128)} fusion(f32[32,128,128]{2,1,0:T(8,128)S(1)} %slice.44, f32[32,32]{1,0:T(8,128)S(1)} %exponential_select_fusion), kind=kLoop, calls=%fused_computation.1 | loop fusion | flops 33030144 | bytes 4198400 | tf_op jit(solution)/shard_map/reduce_sum | solution.py:67
  86.0 6.9 %all-to-all-start.1 = ((f32[32,128,128]{2,1,0:T(8,128)}), f32[32,128,128]{2,1,0:T(8,128)S(1)}, u32[]{:S(2)}, u32[]{:S(2)}) async-start(f32[32,128,128]{2,1,0:T(8,128)} %multiply_reduce_fusion), calls=%async_computation.1 | async-start | bytes 4194304 | tf_op jit(solution)/shard_map/all_to_all | solution.py:68
  92.9 1.1 bitcast_multiply_fusion.1
  94.3 2.3 %broadcast_multiply_fusion = (f32[128,128,1,16]{1,0,3,2:T(8,128)}, f32[128,128]{1,0:T(8,128)S(1)}) fusion(f32[128,128]{1,0:T(8,128)S(1)} %copy.83, f32[128,16]{0,1:T(8,128)} %param.11, bf16[128,16,64]{0,2,1:T(8,128)(2,1)S(1)} %bitcast.188, bf16[128,16,64]{0,2,1:T(8,128)(2,1)S(1)} %bitcast.189, f32[128,128]{1,0:T(8,128)S(1)} %fusion.44, ...), kind=kOutput, calls=%fused_computation.54 | convolution fusion | flops 35373056 | bytes 1785856 | tf_op jit(solution)/shard_map/ughp,sghp->usgh/dot_general | solution.py:104
  96.5 2.6 %copy.91 = f32[128,128,1,16]{0,3,1,2:T(8,128)} copy(f32[128,128,1,16]{1,0,3,2:T(8,128)} %get-tuple-element.28) | data formatting | bytes 2097152 | tf_op jit(solution)/shard_map/mul | solution.py:113
  99.1 2.3 %fusion.53 = f32[128,128,1,16]{0,3,1,2:T(8,128)} fusion(f32[128,128,1,16]{0,3,1,2:T(8,128)} %copy.91), kind=kOutput, calls=%fused_computation.98 | output fusion | flops 33292288 | bytes 2097152 | tf_op jit(solution)/shard_map/jit(cumsum)/reduce_window_sum | solution.py:114
  101.5 2.6 %copy.92 = f32[128,128,1,16]{1,0,3,2:T(8,128)} copy(f32[128,128,1,16]{0,3,1,2:T(8,128)} %fusion.53) | data formatting | bytes 2097152 | tf_op jit(solution)/shard_map/jit(cumsum)/reduce_window_sum | solution.py:114
  104.0 2.3 %multiply_reduce_fusion.1 = f32[128,16]{0,1:T(8,128)} fusion(f32[128,128,1,16]{1,0,3,2:T(8,128)} %copy.92, f32[128,128,1,16]{1,0,3,2:T(8,128)} %get-tuple-element.28, f32[128,128]{1,0:T(8,128)S(1)} %fusion.44), kind=kLoop, calls=%fused_computation.37 | loop fusion | flops 784384 | bytes 2170880 | tf_op jit(solution)/shard_map/reduce_sum | solution.py:115
  106.3 34.3 %all-to-all-done.1 = f32[32,128,128]{2,1,0:T(8,128)S(1)} async-done(((f32[32,128,128]{2,1,0:T(8,128)}), f32[32,128,128]{2,1,0:T(8,128)S(1)}, u32[]{:S(2)}, u32[]{:S(2)}) %all-to-all-start.1) | async-done | bytes 2097184 | tf_op jit(solution)/shard_map/all_to_all | solution.py:68
  144.2 0.7 multiply_reduce_fusion.3
  145.9 7.9 %all-to-all-start.2 = ((f32[8,1,256]{2,1,0:T(1,128)}), f32[8,1,256]{2,1,0:T(1,128)S(1)}, u32[]{:S(2)}, u32[]{:S(2)}) async-start(f32[8,1,256]{2,1,0:T(1,128)} %reshape.400), calls=%async_computation.2 | async-start | bytes 16384 | tf_op jit(solution)/shard_map/all_to_all | solution.py:212
  153.8 0.9 fusion.9
  154.6 0.8 fusion.8
  155.4 0.8 copy.94
  156.3 2.1 %all-to-all-done.2 = f32[8,1,256]{2,1,0:T(1,128)S(1)} async-done(((f32[8,1,256]{2,1,0:T(1,128)}), f32[8,1,256]{2,1,0:T(1,128)S(1)}, u32[]{:S(2)}, u32[]{:S(2)}) %all-to-all-start.2) | async-done | bytes 8224 | tf_op jit(solution)/shard_map/all_to_all | solution.py:212
  (64 shorter events, 11.0 us)
Async XLA Ops:
  0.6 5.5 %copy-start.10 = (f32[128,16]{0,1:T(8,128)S(1)}, f32[128,16]{0,1:T(8,128)}, u32[]{:S(2)}) copy-start(f32[128,16]{0,1:T(8,128)} %param.11) | copy-start | bytes 24580
  2.3 2.0 %copy-start.6 = (f32[128,1,16]{2,1,0:T(1,128)}, f32[128,1,16]{2,1,0:T(1,128)S(1)}, u32[]{:S(2)}) copy-start(f32[128,1,16]{2,1,0:T(1,128)S(1)} %fusion.52) | copy-start | bytes 24580
  3.6 3.5 %copy-start.2 = (f32[128,1024]{0,1:T(8,128)}, f32[128,1024]{0,1:T(8,128)S(1)}, u32[]{:S(2)}) copy-start(f32[128,1024]{0,1:T(8,128)S(1)} %convert_element_type.142) | copy-start | bytes 1572868
  6.8 0.8 copy-start.4
  6.8 0.9 copy-start.5
  10.5 63.0 %all-to-all-start = ((f32[32,136,128]{2,1,0:T(8,128)}), f32[32,136,128]{2,1,0:T(8,128)S(1)}, u32[]{:S(2)}, u32[]{:S(2)}) async-start(f32[32,136,128]{2,1,0:T(8,128)} %pad_maximum_fusion), calls=%async_computation | async-start | bytes 4456448 | tf_op jit(solution)/shard_map/all_to_all | solution.py:55
  86.0 54.6 %all-to-all-start.1 = ((f32[32,128,128]{2,1,0:T(8,128)}), f32[32,128,128]{2,1,0:T(8,128)S(1)}, u32[]{:S(2)}, u32[]{:S(2)}) async-start(f32[32,128,128]{2,1,0:T(8,128)} %multiply_reduce_fusion), calls=%async_computation.1 | async-start | bytes 4194304 | tf_op jit(solution)/shard_map/all_to_all | solution.py:68
  94.2 4.9 %copy-start.7 = (f32[128,128]{1,0:T(8,128)}, f32[128,128]{1,0:T(8,128)S(1)}, u32[]{:S(2)}) copy-start(f32[128,128]{1,0:T(8,128)S(1)} %copy.83) | copy-start | bytes 196612
  140.6 1.0 copy-start.1
  141.0 1.2 copy-start
  142.2 1.8 %copy-start.9 = (f32[128,16]{0,1:T(8,128)S(1)}, f32[128,16]{0,1:T(8,128)}, u32[]{:S(2)}) copy-start(f32[128,16]{0,1:T(8,128)} %multiply_reduce_fusion.1) | copy-start | bytes 24580
  142.2 1.9 %copy-start.3 = (f32[128,1024]{0,1:T(8,128)S(1)}, f32[128,1024]{0,1:T(8,128)}, u32[]{:S(2)}) copy-start(f32[128,1024]{0,1:T(8,128)} %copy-done.2) | copy-start | bytes 1572868
  142.2 1.9 %copy-start.8 = (f32[128,128]{1,0:T(8,128)S(1)}, f32[128,128]{1,0:T(8,128)}, u32[]{:S(2)}) copy-start(f32[128,128]{1,0:T(8,128)} %copy-done.7) | copy-start | bytes 196612
  142.2 1.9 %copy-start.11 = (f32[128,16]{0,1:T(8,128)S(1)}, f32[128,16]{0,1:T(8,128)}, u32[]{:S(2)}) copy-start(f32[128,16]{0,1:T(8,128)} %param.11) | copy-start | bytes 24580
  142.3 1.9 %copy-start.12 = (f32[128,16]{0,1:T(8,128)S(1)}, f32[128,16]{0,1:T(8,128)}, u32[]{:S(2)}) copy-start(f32[128,16]{0,1:T(8,128)} %get-tuple-element.25) | copy-start | bytes 24580
  142.9 2.0 %copy-start.13 = (f32[16]{0:T(128)S(1)}, f32[16]{0:T(128)}, u32[]{:S(2)}) copy-start(f32[16]{0:T(128)} %param.12) | copy-start | bytes 196
  145.9 12.5 %all-to-all-start.2 = ((f32[8,1,256]{2,1,0:T(1,128)}), f32[8,1,256]{2,1,0:T(1,128)S(1)}, u32[]{:S(2)}, u32[]{:S(2)}) async-start(f32[8,1,256]{2,1,0:T(1,128)} %reshape.400), calls=%async_computation.2 | async-start | bytes 16384 | tf_op jit(solution)/shard_map/all_to_all | solution.py:212

commit v14 on v12

--- a/solution.py
+++ b/solution.py
@@ -49,7 +49,12 @@
     tiled = (count, per, head_dim // 8, 8, state_dim // 128, 128)
     flat = stacked.reshape(tiled).transpose(0, 1, 2, 4, 3, 5).reshape(count, -1, 128)
     body_rows = flat.shape[1]
-    tags = jnp.repeat(jnp.stack([logs[i % heads] for i in targets.reshape(-1)]).reshape(targets.shape), 8, axis=1)
+    owned = targets % heads
+    if per == 1 and np.array_equal(owned[:, 0], np.arange(count) % heads):
+        chosen_logs = jnp.tile(logs, count // heads)[:, None]
+    else:
+        chosen_logs = logs[owned]
+    tags = jnp.repeat(chosen_logs, 8, axis=1)
     tags = jnp.broadcast_to(tags[..., None], (count, per * 8, 128))
     payload = jnp.concatenate([flat, tags], axis=1)
     pieces = lax.all_to_all(payload, axis, 0, 0, tiled=True)

time: 174 us -> 153 us (0.88)
  local copies, waits for them, and re-layouts: 35.9 us -> 14.5 us
    another operation x1 -> x2, local copies, waits for them, and re-layouts: 20.7 us -> 0.08 us  [seq_scan(): chosen_logs = jnp.tile(logs, count // heads)[:, None]]
    unnamed x37 -> x35, local copies, waits for them, and re-layouts: 7.55 us -> 7.45 us
  transfers between devices with their start and end apart: 3 -> 3, of which waited for: 3 -> 3; matrix products, arithmetic and copies ran while one was open for 9% -> 10% of each run, Pallas kernels for 0% -> 0%
where the time goes in v14:
time: 153 us; the launch traced here: 152 us
  waiting for transfers between devices  87.5 us (57%)
  starting transfers between devices  26.7 us (17%)
  local copies, waits for them, and re-layouts  14.5 us (9%)
  other arithmetic  11.5 us (8%)
  matrix products  11.2 us (7%)
    all_to_all x1, waiting for transfers between devices, seq_scan(): pieces = lax.all_to_all(payload, axis, 0, 0, tiled=True)  51.1 us
    all_to_all x1, waiting for transfers between devices, seq_scan(): lax.all_to_all(scanned.reshape(count, body_rows, 128), axis, 0, 0, tiled=...  34.3 us
    all_to_all x1, starting transfers between devices, seq_scan(): pieces = lax.all_to_all(payload, axis, 0, 0, tiled=True)  11.9 us
    all_to_all x1, starting transfers between devices, body(): lax.all_to_all(grad_step, 'tp', split_axis=0, concat_axis=1, tiled=True)  7.91 us
    unnamed x35, local copies, waits for them, and re-layouts  7.45 us
    all_to_all x1, starting transfers between devices, seq_scan(): lax.all_to_all(scanned.reshape(count, body_rows, 128), axis, 0, 0, tiled=...  6.9 us
  transfers between devices with their start and end apart: 3, of which 3 were waited for; matrix products, arithmetic and copies ran while one was open for 10% of the time, Pallas kernels for 0%

profile of v14, /device:TPU:1, one launch (start us, length us, event | category | flops | bytes accessed | tf_op | source)
XLA Modules:
  0.0 152.4 jit_solution(503601961577762727)
XLA Ops:
  1.3 0.8 multiply_bitcast_fusion
  2.4 1.1 copy.66
  3.7 1.2 copy.65
  6.5 0.7 fusion.45
  7.8 1.6 %pad_maximum_fusion = f32[32,136,128]{2,1,0:T(8,128)} fusion(f32[32,8,128]{2,1,0:T(8,128)S(1)} %broadcast_in_dim.10, f32[32,128,128]{2,1,0:T(8,128)S(1)} %bitcast.198), kind=kLoop, calls=%fused_computation | loop fusion | flops 557056 | bytes 4456448 | tf_op jit(solution)/shard_map/concatenate | solution.py:59
  9.3 11.9 %all-to-all-start = ((f32[32,136,128]{2,1,0:T(8,128)}), f32[32,136,128]{2,1,0:T(8,128)S(1)}, u32[]{:S(2)}, u32[]{:S(2)}) async-start(f32[32,136,128]{2,1,0:T(8,128)} %pad_maximum_fusion), calls=%async_computation | async-start | bytes 4456448 | tf_op jit(solution)/shard_map/all_to_all | solution.py:60
  21.2 51.1 %all-to-all-done = f32[32,136,128]{2,1,0:T(8,128)S(1)} async-done(((f32[32,136,128]{2,1,0:T(8,128)}), f32[32,136,128]{2,1,0:T(8,128)S(1)}, u32[]{:S(2)}, u32[]{:S(2)}) %all-to-all-start) | async-done | bytes 2228256 | tf_op jit(solution)/shard_map/all_to_all | solution.py:60
  72.6 1.2 fusion.41
  74.1 2.2 %fusion.3 = f32[4,8,128,128]{3,1,2,0:T(8,128)S(1)} fusion(f32[4,8,128,128]{3,2,1,0:T(8,128)S(1)} %bitcast.200, f32[32,32]{1,0:T(8,128)S(1)} %bitcast.218, pred[]{:T(512)S(6)} %lt.49), kind=kOutput, calls=%fused_computation.5 | convolution fusion | flops 100667392 | bytes 4198401 | tf_op jit(solution)/shard_map/cij,jcx->icx/dot_general | solution.py:72
  76.3 1.7 %copy.89 = f32[4,8,128,128]{3,2,1,0:T(8,128)} copy(f32[4,8,128,128]{3,1,2,0:T(8,128)S(1)} %fusion.3) | data formatting | bytes 4194304
  78.0 6.9 %all-to-all-start.1 = ((f32[32,128,128]{2,1,0:T(8,128)}), f32[32,128,128]{2,1,0:T(8,128)S(1)}, u32[]{:S(2)}, u32[]{:S(2)}) async-start(f32[32,128,128]{2,1,0:T(8,128)} %bitcast.197), calls=%async_computation.1 | async-start | bytes 4194304 | tf_op jit(solution)/shard_map/all_to_all | solution.py:73
  84.9 1.1 bitcast_multiply_fusion.1
  86.3 2.3 %broadcast_multiply_fusion = (f32[128,128,1,16]{1,0,3,2:T(8,128)}, f32[128,128]{1,0:T(8,128)S(1)}) fusion(f32[128,128]{1,0:T(8,128)S(1)} %copy.64, f32[128,16]{0,1:T(8,128)} %param.9, bf16[128,16,64]{0,2,1:T(8,128)(2,1)S(1)} %bitcast.204, bf16[128,16,64]{0,2,1:T(8,128)(2,1)S(1)} %bitcast.205, f32[128,128]{1,0:T(8,128)S(1)} %fusion.50, ...), kind=kOutput, calls=%fused_computation.56 | convolution fusion | flops 35373056 | bytes 1785856 | tf_op jit(solution)/shard_map/ughp,sghp->usgh/dot_general | solution.py:109
  88.5 2.6 %copy.72 = f32[128,128,1,16]{0,3,1,2:T(8,128)} copy(f32[128,128,1,16]{1,0,3,2:T(8,128)} %get-tuple-element.24) | data formatting | bytes 2097152 | tf_op jit(solution)/shard_map/mul | solution.py:118
  91.1 2.3 %fusion.65 = f32[128,128,1,16]{0,3,1,2:T(8,128)} fusion(f32[128,128,1,16]{0,3,1,2:T(8,128)} %copy.72), kind=kOutput, calls=%fused_computation.103 | output fusion | flops 33292288 | bytes 2097152 | tf_op jit(solution)/shard_map/jit(cumsum)/reduce_window_sum | solution.py:119
  93.5 2.6 %copy.73 = f32[128,128,1,16]{1,0,3,2:T(8,128)} copy(f32[128,128,1,16]{0,3,1,2:T(8,128)} %fusion.65) | data formatting | bytes 2097152 | tf_op jit(solution)/shard_map/jit(cumsum)/reduce_window_sum | solution.py:119
  96.0 2.3 %multiply_reduce_fusion = f32[128,16]{0,1:T(8,128)} fusion(f32[128,128,1,16]{1,0,3,2:T(8,128)} %copy.73, f32[128,128,1,16]{1,0,3,2:T(8,128)} %get-tuple-element.24, f32[128,128]{1,0:T(8,128)S(1)} %fusion.50), kind=kLoop, calls=%fused_computation.39 | loop fusion | flops 784384 | bytes 2170880 | tf_op jit(solution)/shard_map/reduce_sum | solution.py:120
  98.3 34.3 %all-to-all-done.1 = f32[32,128,128]{2,1,0:T(8,128)S(1)} async-done(((f32[32,128,128]{2,1,0:T(8,128)}), f32[32,128,128]{2,1,0:T(8,128)S(1)}, u32[]{:S(2)}, u32[]{:S(2)}) %all-to-all-start.1) | async-done | bytes 2097184 | tf_op jit(solution)/shard_map/all_to_all | solution.py:73
  136.2 0.7 multiply_reduce_fusion.2
  137.9 7.9 %all-to-all-start.2 = ((f32[8,1,256]{2,1,0:T(1,128)}), f32[8,1,256]{2,1,0:T(1,128)S(1)}, u32[]{:S(2)}, u32[]{:S(2)}) async-start(f32[8,1,256]{2,1,0:T(1,128)} %reshape.392), calls=%async_computation.2 | async-start | bytes 16384 | tf_op jit(solution)/shard_map/all_to_all | solution.py:217
  145.8 0.9 fusion.15
  146.7 0.8 fusion.14
  147.5 0.8 copy.75
  148.3 2.1 %all-to-all-done.2 = f32[8,1,256]{2,1,0:T(1,128)S(1)} async-done(((f32[8,1,256]{2,1,0:T(1,128)}), f32[8,1,256]{2,1,0:T(1,128)S(1)}, u32[]{:S(2)}, u32[]{:S(2)}) %all-to-all-start.2) | async-done | bytes 8224 | tf_op jit(solution)/shard_map/all_to_all | solution.py:217
  (64 shorter events, 10.4 us)
Async XLA Ops:
  0.6 4.3 %copy-start.10 = (f32[128,16]{0,1:T(8,128)S(1)}, f32[128,16]{0,1:T(8,128)}, u32[]{:S(2)}) copy-start(f32[128,16]{0,1:T(8,128)} %param.9) | copy-start | bytes 24580
  2.3 1.4 copy-start.6
  3.6 2.3 %copy-start.2 = (f32[128,1024]{0,1:T(8,128)}, f32[128,1024]{0,1:T(8,128)S(1)}, u32[]{:S(2)}) copy-start(f32[128,1024]{0,1:T(8,128)S(1)} %convert_element_type.142) | copy-start | bytes 1572868
  5.6 0.8 copy-start.4
  5.6 0.9 copy-start.5
  9.3 63.0 %all-to-all-start = ((f32[32,136,128]{2,1,0:T(8,128)}), f32[32,136,128]{2,1,0:T(8,128)S(1)}, u32[]{:S(2)}, u32[]{:S(2)}) async-start(f32[32,136,128]{2,1,0:T(8,128)} %pad_maximum_fusion), calls=%async_computation | async-start | bytes 4456448 | tf_op jit(solution)/shard_map/all_to_all | solution.py:60
  78.0 54.6 %all-to-all-start.1 = ((f32[32,128,128]{2,1,0:T(8,128)}), f32[32,128,128]{2,1,0:T(8,128)S(1)}, u32[]{:S(2)}, u32[]{:S(2)}) async-start(f32[32,128,128]{2,1,0:T(8,128)} %bitcast.197), calls=%async_computation.1 | async-start | bytes 4194304 | tf_op jit(solution)/shard_map/all_to_all | solution.py:73
  86.2 4.9 %copy-start.7 = (f32[128,128]{1,0:T(8,128)}, f32[128,128]{1,0:T(8,128)S(1)}, u32[]{:S(2)}) copy-start(f32[128,128]{1,0:T(8,128)S(1)} %copy.64) | copy-start | bytes 196612
  132.6 1.0 copy-start.1
  133.1 1.2 copy-start
  134.2 1.8 %copy-start.9 = (f32[128,16]{0,1:T(8,128)S(1)}, f32[128,16]{0,1:T(8,128)}, u32[]{:S(2)}) copy-start(f32[128,16]{0,1:T(8,128)} %multiply_reduce_fusion) | copy-start | bytes 24580
  134.3 1.9 %copy-start.3 = (f32[128,1024]{0,1:T(8,128)S(1)}, f32[128,1024]{0,1:T(8,128)}, u32[]{:S(2)}) copy-start(f32[128,1024]{0,1:T(8,128)} %copy-done.2) | copy-start | bytes 1572868
  134.3 1.9 %copy-start.8 = (f32[128,128]{1,0:T(8,128)S(1)}, f32[128,128]{1,0:T(8,128)}, u32[]{:S(2)}) copy-start(f32[128,128]{1,0:T(8,128)} %copy-done.7) | copy-start | bytes 196612
  134.3 1.9 %copy-start.11 = (f32[128,16]{0,1:T(8,128)S(1)}, f32[128,16]{0,1:T(8,128)}, u32[]{:S(2)}) copy-start(f32[128,16]{0,1:T(8,128)} %param.9) | copy-start | bytes 24580
  134.3 1.9 %copy-start.12 = (f32[128,16]{0,1:T(8,128)S(1)}, f32[128,16]{0,1:T(8,128)}, u32[]{:S(2)}) copy-start(f32[128,16]{0,1:T(8,128)} %get-tuple-element.21) | copy-start | bytes 24580
  134.9 2.0 %copy-start.13 = (f32[16]{0:T(128)S(1)}, f32[16]{0:T(128)}, u32[]{:S(2)}) copy-start(f32[16]{0:T(128)} %param.10) | copy-start | bytes 196
  137.9 12.5 %all-to-all-start.2 = ((f32[8,1,256]{2,1,0:T(1,128)}), f32[8,1,256]{2,1,0:T(1,128)S(1)}, u32[]{:S(2)}, u32[]{:S(2)}) async-start(f32[8,1,256]{2,1,0:T(1,128)} %reshape.392), calls=%async_computation.2 | async-start | bytes 16384 | tf_op jit(solution)/shard_map/all_to_all | solution.py:217
